TPU v7x, 128 devices: a whole 4x4x4 slice. The times are simulated.
128 devices in a mesh: region: 64 (over z, y, x), chan: 2 (over core).
Axes of the slice: x: 4, y: 4, z: 4, core: 2. Of those that a mesh axis runs over, the one named last changes fastest.
Arguments:
- features: bfloat16 [384, 196608], P('chan', 'region'), may hold values from -6 to 6
- gain: float32 [384], P('chan'), may hold values from 0.1 to 1.9
- bias: float32 [384], P('chan'), may hold values from -3 to 3
- live: int32 [64], P('region'), may hold values from 1024 to 3072, as said below
- neighbors: int32 [27, 196608], P(None, 'region'), may hold values from -1 to 196607, as said below
- weights: bfloat16 [27, 384, 384], P(None, 'chan'), may hold values from -0.0625 to 0.0625
- grad_out: bfloat16 [384, 196608], P('chan', 'region'), may hold values from -0.059814453 to 0.059814453
Outputs:
- conv_out: bfloat16 [384, 196608], P('chan', 'region')
- kernel_grad: float32 [27, 384, 384], P(None, 'chan')
Inputs may be any that keep to these rules, and one draw needn't show every extreme that they name: One region has all 3072 slots counted live. `neighbors`: an entry [k, i] is -1 or the index of a live site at most 256 away from i; every entry of a site that is not live is -1.
All inputs are finite; a program needn't handle non-finite values.
Results may differ from a plain program's by a relative error of at most 0.0049.
Values may be sent and summed in bfloat16 or wider, within the bound.
No kernel may reach another device: no remote copies, remote signals or barrier semaphores. Data moves between devices by JAX's collectives and lax.ppermute only.
A program may use at most 128 MiB of HBM per device.

v0:
```python
import jax
import jax.numpy as jnp
from jax import lax
from jax.sharding import PartitionSpec as P


def padded(x, sides, width):
    for axis, dim in sides:
        count, length = (lax.axis_size(axis), x.shape[dim])
        up = [(i, (i + 1) % count) for i in range(count - 1)]
        down = [(j, i) for i, j in up]
        last = lax.slice_in_dim(x, length - width, length, axis=dim)
        first = lax.slice_in_dim(x, 0, width, axis=dim)
        before = lax.ppermute(last, axis, up)
        after = lax.ppermute(first, axis, down)
        x = jnp.concatenate([before, x, after], axis=dim)
    return x


def per_device(features, gain, bias, live, neighbors, weights, grad_out):
    channels, columns = features.shape
    border = columns // 12
    region_idx = lax.axis_index("region")
    column = jnp.arange(columns, dtype=jnp.int32)
    live_limit = live[0] - border
    live_mask = ((column < live_limit) | (column >= columns - border)).astype(jnp.float32)
    values = features.astype(jnp.float32)
    masked = values * live_mask[None, :]
    live_rows = jnp.sum(live_mask)
    totals, live_total = lax.psum((jnp.sum(masked, axis=1), live_rows), "region")
    average = totals / live_total
    centered = (values - average[:, None]) * live_mask[None, :]
    variance = lax.psum(jnp.sum(centered * centered, axis=1), "region") / live_total
    factor = gain * lax.rsqrt(variance + 1e-05)
    normed = (
        jnp.maximum((values - average[:, None]) * factor[:, None] + bias[:, None], 0.0)
        * live_mask[None, :]
    )
    site_rows = jnp.transpose(normed).astype(jnp.bfloat16)
    own_chans = lax.all_gather(site_rows, "chan", axis=1, tiled=True)
    gathered = padded(own_chans, (("region", 0),), border)
    anchor = region_idx * columns - border
    extent = columns + 2 * border

    def offset_step(running, operand):
        kernel, targets = operand
        position = jnp.where(targets < 0, extent, targets - anchor)
        picked = jnp.take(gathered, position, axis=0, mode="fill", fill_value=0)
        running = running + lax.dot_general(
            kernel, picked, (((1,), (1,)), ((), ())), preferred_element_type=jnp.float32
        )
        grad_piece = jnp.dot(grad_out, picked, preferred_element_type=jnp.float32)
        return (running, grad_piece)

    start = jnp.zeros((weights.shape[1], columns), jnp.float32)
    conv_sum, grad_parts = lax.scan(offset_step, start, (weights, neighbors))
    kernel_grad = lax.psum(grad_parts, "region")
    return (conv_sum.astype(jnp.bfloat16), kernel_grad)


def solution(mesh):
    return jax.shard_map(
        per_device,
        mesh=mesh,
        in_specs=(
            P("chan", "region"),
            P("chan"),
            P("chan"),
            P("region"),
            P(None, "region"),
            P(None, "chan", None),
            P("chan", "region"),
        ),
        out_specs=(P("chan", "region"), P(None, "chan", None)),
        check_vma=False,
    )
```

profile of v0, /device:TPU:0, one launch (start us, length us, event | category | flops | bytes accessed | tf_op | source)
XLA Modules:
  0.0 1147.6 jit_solution(15399305372164420835)
XLA Ops:
  10.2 181.1 %all-reduce = (f32[192]{0:T(256)S(1)}, f32[]{:T(128)}) all-reduce(f32[192]{0:T(256)S(1)} %fusion.14, f32[]{:T(128)} %fusion.18), channel_id=1, replica_groups=mesh['region'=64,'chan'=2] {'region'}, use_global_device_ids=true, to_apply=%region_1.0 | all-reduce | flops 193 | bytes 1544 | tf_op jit(solution)/shard_map/psum | solution.py:30
  193.8 171.8 %psum.30 = f32[192]{0:T(256)S(1)} all-reduce(f32[192]{0:T(256)S(1)} %fusion.9), channel_id=1, replica_groups=mesh['region'=64,'chan'=2] {'region'}, use_global_device_ids=true, to_apply=%region_5.0 | all-reduce | flops 192 | bytes 1536 | tf_op jit(solution)/shard_map/psum | solution.py:33
  368.0 8.9 all-gather.2.cloned.1.call-done
  378.0 3.5 collective-permute-start
  386.1 4.1 collective-permute-done.1
  390.2 3.4 pad_maximum_fusion
  393.6 3.3 copy.11
  397.0 563.0 %while.13 = (s32[]{:T(128)}, f32[192,3072]{1,0:T(8,128)}, f32[27,192,384]{2,1,0:T(8,128)}, bf16[27,192,384]{2,1,0:T(8,128)(2,1)}, s32[27,3072]{1,0:T(8,128)}, /*...) while((s32[]{:T(128)}, f32[192,3072]{1,0:T(8,128)}, ...), condition=%wide.region_7.8_spmd.clone, body=%wide.region_6.7_spmd.clone.sunk | while | flops 909548544 | bytes 30030000 | solution.py:56
  397.9 13.1 %gather_fusion = bf16[3072,384]{1,0:T(8,128)(2,1)} fusion(bf16[3584,384]{1,0:T(8,128)(2,1)S(1)} %get-tuple-element.183, s32[3072]{0:T(1024)S(1)} %broadcast_clamp_fusion.2), kind=kCustom, calls=%fused_computation.clone.clone.1 | custom fusion | bytes 4730880 | tf_op jit(solution)/shard_map/while/body/eval_jaxpr/jit(_take)/gather | solution.py:48
  411.1 4.5 convolution_add_fusion.2
  418.1 13.1 %gather_fusion = bf16[3072,384]{1,0:T(8,128)(2,1)} fusion(bf16[3584,384]{1,0:T(8,128)(2,1)S(1)} %get-tuple-element.183, s32[3072]{0:T(1024)S(1)} %broadcast_clamp_fusion.2), kind=kCustom, calls=%fused_computation.clone.clone.1 | custom fusion | bytes 4730880 | tf_op jit(solution)/shard_map/while/body/eval_jaxpr/jit(_take)/gather | solution.py:48
  431.3 5.2 convolution_add_fusion.2
  439.0 13.1 %gather_fusion = bf16[3072,384]{1,0:T(8,128)(2,1)} fusion(bf16[3584,384]{1,0:T(8,128)(2,1)S(1)} %get-tuple-element.183, s32[3072]{0:T(1024)S(1)} %broadcast_clamp_fusion.2), kind=kCustom, calls=%fused_computation.clone.clone.1 | custom fusion | bytes 4730880 | tf_op jit(solution)/shard_map/while/body/eval_jaxpr/jit(_take)/gather | solution.py:48
  452.1 5.2 convolution_add_fusion.2
  459.9 13.1 %gather_fusion = bf16[3072,384]{1,0:T(8,128)(2,1)} fusion(bf16[3584,384]{1,0:T(8,128)(2,1)S(1)} %get-tuple-element.183, s32[3072]{0:T(1024)S(1)} %broadcast_clamp_fusion.2), kind=kCustom, calls=%fused_computation.clone.clone.1 | custom fusion | bytes 4730880 | tf_op jit(solution)/shard_map/while/body/eval_jaxpr/jit(_take)/gather | solution.py:48
  473.0 5.2 convolution_add_fusion.2
  480.7 13.1 %gather_fusion = bf16[3072,384]{1,0:T(8,128)(2,1)} fusion(bf16[3584,384]{1,0:T(8,128)(2,1)S(1)} %get-tuple-element.183, s32[3072]{0:T(1024)S(1)} %broadcast_clamp_fusion.2), kind=kCustom, calls=%fused_computation.clone.clone.1 | custom fusion | bytes 4730880 | tf_op jit(solution)/shard_map/while/body/eval_jaxpr/jit(_take)/gather | solution.py:48
  493.9 5.2 convolution_add_fusion.2
  501.6 13.1 %gather_fusion = bf16[3072,384]{1,0:T(8,128)(2,1)} fusion(bf16[3584,384]{1,0:T(8,128)(2,1)S(1)} %get-tuple-element.183, s32[3072]{0:T(1024)S(1)} %broadcast_clamp_fusion.2), kind=kCustom, calls=%fused_computation.clone.clone.1 | custom fusion | bytes 4730880 | tf_op jit(solution)/shard_map/while/body/eval_jaxpr/jit(_take)/gather | solution.py:48
  514.8 5.2 convolution_add_fusion.2
  522.5 13.1 %gather_fusion = bf16[3072,384]{1,0:T(8,128)(2,1)} fusion(bf16[3584,384]{1,0:T(8,128)(2,1)S(1)} %get-tuple-element.183, s32[3072]{0:T(1024)S(1)} %broadcast_clamp_fusion.2), kind=kCustom, calls=%fused_computation.clone.clone.1 | custom fusion | bytes 4730880 | tf_op jit(solution)/shard_map/while/body/eval_jaxpr/jit(_take)/gather | solution.py:48
  535.6 5.2 convolution_add_fusion.2
  543.4 13.1 %gather_fusion = bf16[3072,384]{1,0:T(8,128)(2,1)} fusion(bf16[3584,384]{1,0:T(8,128)(2,1)S(1)} %get-tuple-element.183, s32[3072]{0:T(1024)S(1)} %broadcast_clamp_fusion.2), kind=kCustom, calls=%fused_computation.clone.clone.1 | custom fusion | bytes 4730880 | tf_op jit(solution)/shard_map/while/body/eval_jaxpr/jit(_take)/gather | solution.py:48
  556.5 5.2 convolution_add_fusion.2
  564.2 13.1 %gather_fusion = bf16[3072,384]{1,0:T(8,128)(2,1)} fusion(bf16[3584,384]{1,0:T(8,128)(2,1)S(1)} %get-tuple-element.183, s32[3072]{0:T(1024)S(1)} %broadcast_clamp_fusion.2), kind=kCustom, calls=%fused_computation.clone.clone.1 | custom fusion | bytes 4730880 | tf_op jit(solution)/shard_map/while/body/eval_jaxpr/jit(_take)/gather | solution.py:48
  577.4 5.2 convolution_add_fusion.2
  585.1 13.1 %gather_fusion = bf16[3072,384]{1,0:T(8,128)(2,1)} fusion(bf16[3584,384]{1,0:T(8,128)(2,1)S(1)} %get-tuple-element.183, s32[3072]{0:T(1024)S(1)} %broadcast_clamp_fusion.2), kind=kCustom, calls=%fused_computation.clone.clone.1 | custom fusion | bytes 4730880 | tf_op jit(solution)/shard_map/while/body/eval_jaxpr/jit(_take)/gather | solution.py:48
  598.3 5.2 convolution_add_fusion.2
  606.0 13.1 %gather_fusion = bf16[3072,384]{1,0:T(8,128)(2,1)} fusion(bf16[3584,384]{1,0:T(8,128)(2,1)S(1)} %get-tuple-element.183, s32[3072]{0:T(1024)S(1)} %broadcast_clamp_fusion.2), kind=kCustom, calls=%fused_computation.clone.clone.1 | custom fusion | bytes 4730880 | tf_op jit(solution)/shard_map/while/body/eval_jaxpr/jit(_take)/gather | solution.py:48
  619.1 5.2 convolution_add_fusion.2
  626.9 13.1 %gather_fusion = bf16[3072,384]{1,0:T(8,128)(2,1)} fusion(bf16[3584,384]{1,0:T(8,128)(2,1)S(1)} %get-tuple-element.183, s32[3072]{0:T(1024)S(1)} %broadcast_clamp_fusion.2), kind=kCustom, calls=%fused_computation.clone.clone.1 | custom fusion | bytes 4730880 | tf_op jit(solution)/shard_map/while/body/eval_jaxpr/jit(_take)/gather | solution.py:48
  640.0 5.2 convolution_add_fusion.2
  647.7 13.1 %gather_fusion = bf16[3072,384]{1,0:T(8,128)(2,1)} fusion(bf16[3584,384]{1,0:T(8,128)(2,1)S(1)} %get-tuple-element.183, s32[3072]{0:T(1024)S(1)} %broadcast_clamp_fusion.2), kind=kCustom, calls=%fused_computation.clone.clone.1 | custom fusion | bytes 4730880 | tf_op jit(solution)/shard_map/while/body/eval_jaxpr/jit(_take)/gather | solution.py:48
  660.9 5.2 convolution_add_fusion.2
  668.6 13.1 %gather_fusion = bf16[3072,384]{1,0:T(8,128)(2,1)} fusion(bf16[3584,384]{1,0:T(8,128)(2,1)S(1)} %get-tuple-element.183, s32[3072]{0:T(1024)S(1)} %broadcast_clamp_fusion.2), kind=kCustom, calls=%fused_computation.clone.clone.1 | custom fusion | bytes 4730880 | tf_op jit(solution)/shard_map/while/body/eval_jaxpr/jit(_take)/gather | solution.py:48
  681.8 5.2 convolution_add_fusion.2
  689.5 13.1 %gather_fusion = bf16[3072,384]{1,0:T(8,128)(2,1)} fusion(bf16[3584,384]{1,0:T(8,128)(2,1)S(1)} %get-tuple-element.183, s32[3072]{0:T(1024)S(1)} %broadcast_clamp_fusion.2), kind=kCustom, calls=%fused_computation.clone.clone.1 | custom fusion | bytes 4730880 | tf_op jit(solution)/shard_map/while/body/eval_jaxpr/jit(_take)/gather | solution.py:48
  702.6 5.2 convolution_add_fusion.2
  710.4 13.1 %gather_fusion = bf16[3072,384]{1,0:T(8,128)(2,1)} fusion(bf16[3584,384]{1,0:T(8,128)(2,1)S(1)} %get-tuple-element.183, s32[3072]{0:T(1024)S(1)} %broadcast_clamp_fusion.2), kind=kCustom, calls=%fused_computation.clone.clone.1 | custom fusion | bytes 4730880 | tf_op jit(solution)/shard_map/while/body/eval_jaxpr/jit(_take)/gather | solution.py:48
  723.5 5.2 convolution_add_fusion.2
  731.2 13.1 %gather_fusion = bf16[3072,384]{1,0:T(8,128)(2,1)} fusion(bf16[3584,384]{1,0:T(8,128)(2,1)S(1)} %get-tuple-element.183, s32[3072]{0:T(1024)S(1)} %broadcast_clamp_fusion.2), kind=kCustom, calls=%fused_computation.clone.clone.1 | custom fusion | bytes 4730880 | tf_op jit(solution)/shard_map/while/body/eval_jaxpr/jit(_take)/gather | solution.py:48
  744.4 5.2 convolution_add_fusion.2
  752.1 13.1 %gather_fusion = bf16[3072,384]{1,0:T(8,128)(2,1)} fusion(bf16[3584,384]{1,0:T(8,128)(2,1)S(1)} %get-tuple-element.183, s32[3072]{0:T(1024)S(1)} %broadcast_clamp_fusion.2), kind=kCustom, calls=%fused_computation.clone.clone.1 | custom fusion | bytes 4730880 | tf_op jit(solution)/shard_map/while/body/eval_jaxpr/jit(_take)/gather | solution.py:48
  765.3 5.2 convolution_add_fusion.2
  773.0 13.1 %gather_fusion = bf16[3072,384]{1,0:T(8,128)(2,1)} fusion(bf16[3584,384]{1,0:T(8,128)(2,1)S(1)} %get-tuple-element.183, s32[3072]{0:T(1024)S(1)} %broadcast_clamp_fusion.2), kind=kCustom, calls=%fused_computation.clone.clone.1 | custom fusion | bytes 4730880 | tf_op jit(solution)/shard_map/while/body/eval_jaxpr/jit(_take)/gather | solution.py:48
  786.2 5.2 convolution_add_fusion.2
  793.9 13.1 %gather_fusion = bf16[3072,384]{1,0:T(8,128)(2,1)} fusion(bf16[3584,384]{1,0:T(8,128)(2,1)S(1)} %get-tuple-element.183, s32[3072]{0:T(1024)S(1)} %broadcast_clamp_fusion.2), kind=kCustom, calls=%fused_computation.clone.clone.1 | custom fusion | bytes 4730880 | tf_op jit(solution)/shard_map/while/body/eval_jaxpr/jit(_take)/gather | solution.py:48
  807.0 5.2 convolution_add_fusion.2
  814.8 13.1 %gather_fusion = bf16[3072,384]{1,0:T(8,128)(2,1)} fusion(bf16[3584,384]{1,0:T(8,128)(2,1)S(1)} %get-tuple-element.183, s32[3072]{0:T(1024)S(1)} %broadcast_clamp_fusion.2), kind=kCustom, calls=%fused_computation.clone.clone.1 | custom fusion | bytes 4730880 | tf_op jit(solution)/shard_map/while/body/eval_jaxpr/jit(_take)/gather | solution.py:48
  827.9 5.2 convolution_add_fusion.2
  835.6 13.1 %gather_fusion = bf16[3072,384]{1,0:T(8,128)(2,1)} fusion(bf16[3584,384]{1,0:T(8,128)(2,1)S(1)} %get-tuple-element.183, s32[3072]{0:T(1024)S(1)} %broadcast_clamp_fusion.2), kind=kCustom, calls=%fused_computation.clone.clone.1 | custom fusion | bytes 4730880 | tf_op jit(solution)/shard_map/while/body/eval_jaxpr/jit(_take)/gather | solution.py:48
  848.8 5.2 convolution_add_fusion.2
  856.5 13.1 %gather_fusion = bf16[3072,384]{1,0:T(8,128)(2,1)} fusion(bf16[3584,384]{1,0:T(8,128)(2,1)S(1)} %get-tuple-element.183, s32[3072]{0:T(1024)S(1)} %broadcast_clamp_fusion.2), kind=kCustom, calls=%fused_computation.clone.clone.1 | custom fusion | bytes 4730880 | tf_op jit(solution)/shard_map/while/body/eval_jaxpr/jit(_take)/gather | solution.py:48
  869.7 5.2 convolution_add_fusion.2
  877.4 13.1 %gather_fusion = bf16[3072,384]{1,0:T(8,128)(2,1)} fusion(bf16[3584,384]{1,0:T(8,128)(2,1)S(1)} %get-tuple-element.183, s32[3072]{0:T(1024)S(1)} %broadcast_clamp_fusion.2), kind=kCustom, calls=%fused_computation.clone.clone.1 | custom fusion | bytes 4730880 | tf_op jit(solution)/shard_map/while/body/eval_jaxpr/jit(_take)/gather | solution.py:48
  890.5 5.2 convolution_add_fusion.2
  898.3 13.1 %gather_fusion = bf16[3072,384]{1,0:T(8,128)(2,1)} fusion(bf16[3584,384]{1,0:T(8,128)(2,1)S(1)} %get-tuple-element.183, s32[3072]{0:T(1024)S(1)} %broadcast_clamp_fusion.2), kind=kCustom, calls=%fused_computation.clone.clone.1 | custom fusion | bytes 4730880 | tf_op jit(solution)/shard_map/while/body/eval_jaxpr/jit(_take)/gather | solution.py:48
  911.4 5.2 convolution_add_fusion.2
  919.1 13.1 %gather_fusion = bf16[3072,384]{1,0:T(8,128)(2,1)} fusion(bf16[3584,384]{1,0:T(8,128)(2,1)S(1)} %get-tuple-element.183, s32[3072]{0:T(1024)S(1)} %broadcast_clamp_fusion.2), kind=kCustom, calls=%fused_computation.clone.clone.1 | custom fusion | bytes 4730880 | tf_op jit(solution)/shard_map/while/body/eval_jaxpr/jit(_take)/gather | solution.py:48
  932.3 5.2 convolution_add_fusion.2
  940.0 13.1 %gather_fusion = bf16[3072,384]{1,0:T(8,128)(2,1)} fusion(bf16[3584,384]{1,0:T(8,128)(2,1)S(1)} %get-tuple-element.183, s32[3072]{0:T(1024)S(1)} %broadcast_clamp_fusion.2), kind=kCustom, calls=%fused_computation.clone.clone.1 | custom fusion | bytes 4730880 | tf_op jit(solution)/shard_map/while/body/eval_jaxpr/jit(_take)/gather | solution.py:48
  953.2 5.2 convolution_add_fusion.2
  962.8 170.6 %all-reduce.3.cloned.1.call-done = f32[27,192,384]{2,1,0:T(8,128)} async-done(((f32[27,192,384]{2,1,0:T(8,128)}), f32[27,192,384]{2,1,0:T(8,128)}) %all-reduce.3.cloned.1.call-update) | async-done | bytes 7962640 | tf_op jit(solution)/shard_map/psum | solution.py:57
  1133.4 7.4 copy.24
  (241 shorter events, 84.6 us)
Async XLA Ops:
  7.2 359.0 %copy-start.2 = (bf16[192,3072]{1,0:T(8,128)(2,1)S(1)}, bf16[192,3072]{1,0:T(8,128)(2,1)}, u32[]{:S(2)}) copy-start(bf16[192,3072]{1,0:T(8,128)(2,1)} %param.9) | copy-start | bytes 3538948
  7.2 358.4 %copy-start.4 = (f32[192]{0:T(256)S(1)}, f32[192]{0:T(256)}, u32[]{:S(2)}) copy-start(f32[192]{0:T(256)} %param.10) | copy-start | bytes 2308
  7.2 359.0 %copy-start.3 = (f32[192]{0:T(256)S(1)}, f32[192]{0:T(256)}, u32[]{:S(2)}) copy-start(f32[192]{0:T(256)} %param.11) | copy-start | bytes 2308
  7.2 369.8 %all-gather.2.cloned.1.call-start = ((), (), s32[]{:S(2)}) async-start(), calls=%async_computation | async-start | bytes 3538944 | tf_op jit(solution)/shard_map/all_gather | solution.py:40
  368.0 765.5 %all-reduce.3.cloned.1.call-start = ((), (), s32[]{:S(2)}) async-start(), calls=%async_computation.1 | async-start | bytes 15925248 | tf_op jit(solution)/shard_map/psum | solution.py:57
  378.0 8.1 collective-permute-start
  381.5 8.7 collective-permute-start.1
  411.1 4.5 copy-start
  411.1 4.5 copy-start.5
  431.2 5.2 copy-start
  431.3 5.2 copy-start.5
  452.1 5.2 copy-start
  452.1 5.2 copy-start.5
  473.0 5.2 copy-start
  473.0 5.2 copy-start.5
  493.9 5.2 copy-start
  493.9 5.2 copy-start.5
  514.7 5.2 copy-start
  514.8 5.2 copy-start.5
  535.6 5.2 copy-start
  535.6 5.2 copy-start.5
  556.5 5.2 copy-start
  556.5 5.2 copy-start.5
  577.4 5.2 copy-start
  577.4 5.2 copy-start.5
  598.3 5.2 copy-start
  598.3 5.2 copy-start.5
  619.1 5.2 copy-start
  619.1 5.2 copy-start.5
  640.0 5.2 copy-start
  640.0 5.2 copy-start.5
  660.9 5.2 copy-start
  660.9 5.2 copy-start.5
  681.8 5.2 copy-start
  681.8 5.2 copy-start.5
  702.6 5.2 copy-start
  702.6 5.2 copy-start.5
  723.5 5.2 copy-start
  723.5 5.2 copy-start.5
  744.4 5.2 copy-start
  744.4 5.2 copy-start.5
  765.3 5.2 copy-start
  765.3 5.2 copy-start.5
  786.1 5.2 copy-start
  786.1 5.2 copy-start.5
  807.0 5.2 copy-start
  807.0 5.2 copy-start.5
  827.9 5.2 copy-start
  827.9 5.2 copy-start.5
  848.8 5.2 copy-start
  848.8 5.2 copy-start.5
  869.6 5.2 copy-start
  869.6 5.2 copy-start.5
  890.5 5.2 copy-start
  890.5 5.2 copy-start.5
  911.4 5.2 copy-start
  911.4 5.2 copy-start.5
  932.3 5.2 copy-start
  932.3 5.2 copy-start.5
  953.1 5.2 copy-start
  953.1 5.2 copy-start.5
  959.9 1.7 copy-start.1
Sparse Core Ops, SparseCore 0:
  368.1 8.8 all-gather.1
  960.1 173.2 all-reduce.2
where the time goes:
time: 1150 us
  local copies, waits for them, and re-layouts  368 us (32%)
  blocking collectives  353 us (31%)
  waiting for transfers between devices  187 us (16%)
  matrix products  182 us (16%)
  other arithmetic  36.9 us (3%)
  between operations  14.9 us (1%)
    gather x27, local copies, waits for them, and re-layouts, offset_step(): picked = jnp.take(gathered, position, axis=0, mode='fill', fill_value=0)  354 us
    psum x1, blocking collectives, per_device(): lax.psum((jnp.sum(masked, axis=1), live_rows), 'region')  181 us
    psum x1, blocking collectives, per_device(): lax.psum(jnp.sum(centered * centered, axis=1), 'region') / live_total  172 us
    psum x1, waiting for transfers between devices, per_device(): kernel_grad = lax.psum(grad_parts, 'region')  171 us
    dot_general x27, matrix products, offset_step(): lax.dot_general(kernel, picked, (((1,), (1,)), ((), ())), preferred_eleme...  139 us
    dot_general x27, matrix products, offset_step(): grad_piece = jnp.dot(grad_out, picked, preferred_element_type=jnp.float32)  43.4 us
    select_n x27, other arithmetic, offset_step(): picked = jnp.take(gathered, position, axis=0, mode='fill', fill_value=0)  24.9 us
  transfers between devices with their start and end apart: 4, of which 4 were waited for; matrix products, arithmetic and copies ran while one was open for 0% of the time, Pallas kernels for 0%

commit v1 on v0

v1 whole, which is shorter than its diff:
```python
import jax
import jax.numpy as jnp
import numpy as np
from jax import lax
from jax.sharding import Mesh
from jax.sharding import PartitionSpec as P

SUB = ("z", "y", "x")


def region_sum(x):
    for axis in reversed(SUB):
        x = lax.psum(x, axis)
    return x


def padded(x, width):
    count = lax.axis_size(SUB)
    length = x.shape[0]
    up = [(i, (i + 1) % count) for i in range(count - 1)]
    down = [(j, i) for i, j in up]
    last = lax.slice_in_dim(x, length - width, length, axis=0)
    first = lax.slice_in_dim(x, 0, width, axis=0)
    before = lax.ppermute(last, SUB, up)
    after = lax.ppermute(first, SUB, down)
    return jnp.concatenate([before, x, after], axis=0)


def per_device(features, gain, bias, live, neighbors, weights, grad_out):
    channels, columns = features.shape
    border = columns // 12
    region_idx = lax.axis_index(SUB)
    column = jnp.arange(columns, dtype=jnp.int32)
    live_limit = live[0] - border
    live_mask = ((column < live_limit) | (column >= columns - border)).astype(jnp.float32)
    values = features.astype(jnp.float32)
    masked = values * live_mask[None, :]
    live_rows = jnp.sum(live_mask)
    totals, live_total = region_sum((jnp.sum(masked, axis=1), live_rows))
    average = totals / live_total
    centered = (values - average[:, None]) * live_mask[None, :]
    variance = region_sum(jnp.sum(centered * centered, axis=1)) / live_total
    factor = gain * lax.rsqrt(variance + 1e-05)
    normed = (
        jnp.maximum((values - average[:, None]) * factor[:, None] + bias[:, None], 0.0)
        * live_mask[None, :]
    )
    site_rows = jnp.transpose(normed).astype(jnp.bfloat16)
    own_chans = lax.all_gather(site_rows, "chan", axis=1, tiled=True)
    gathered = padded(own_chans, border)
    anchor = region_idx * columns - border
    extent = columns + 2 * border

    def offset_step(running, operand):
        kernel, targets = operand
        position = jnp.where(targets < 0, extent, targets - anchor)
        picked = jnp.take(gathered, position, axis=0, mode="fill", fill_value=0)
        running = running + lax.dot_general(
            kernel, picked, (((1,), (1,)), ((), ())), preferred_element_type=jnp.float32
        )
        grad_piece = jnp.dot(grad_out, picked, preferred_element_type=jnp.float32)
        return (running, grad_piece)

    start = jnp.zeros((weights.shape[1], columns), jnp.float32)
    conv_sum, grad_parts = lax.scan(offset_step, start, (weights, neighbors))
    kernel_grad = region_sum(grad_parts)
    return (conv_sum.astype(jnp.bfloat16), kernel_grad)


def sub_mesh(mesh):
    devices = np.asarray(mesh.devices)
    count = devices.shape[0]
    first = devices[:, 0]
    try:
        sizes = [len({d.coords[a] for d in first}) for a in (2, 1, 0)]
    except (AttributeError, IndexError, TypeError):
        sizes = [count, 1, 1]
    if int(np.prod(sizes)) != count:
        sizes = [count, 1, 1]
    return Mesh(devices.reshape(*sizes, devices.shape[1]), SUB + ("chan",))


def solution(mesh):
    sites = ("chan", SUB)
    return jax.shard_map(
        per_device,
        mesh=sub_mesh(mesh),
        in_specs=(
            P(*sites),
            P("chan"),
            P("chan"),
            P(SUB),
            P(None, SUB),
            P(None, "chan", None),
            P(*sites),
        ),
        out_specs=(P(*sites), P(None, "chan", None)),
        check_vma=False,
    )
```

time: 1150 us -> 1150 us (level)
  waiting for transfers between devices: 187 us -> 486 us
  blocking collectives: 353 us -> 58.2 us
    psum x1 -> x3, waiting for transfers between devices: 171 us -> 467 us  [region_sum(): x = lax.psum(x, axis)]
    psum x2 -> x6, blocking collectives: 353 us -> 58.2 us  [region_sum(): x = lax.psum(x, axis)]
  transfers between devices with their start and end apart: 4 -> 6, of which waited for: 4 -> 6; matrix products, arithmetic and copies ran while one was open for 0% -> 0% of each run, Pallas kernels for 0% -> 0%
where the time goes in v1:
time: 1150 us
  waiting for transfers between devices  486 us (42%)
  local copies, waits for them, and re-layouts  366 us (32%)
  matrix products  181 us (16%)
  blocking collectives  58.2 us (5%)
  other arithmetic  36.9 us (3%)
  between operations  14.6 us (1%)
    psum x3, waiting for transfers between devices, region_sum(): x = lax.psum(x, axis)  467 us
    gather x27, local copies, waits for them, and re-layouts, offset_step(): picked = jnp.take(gathered, position, axis=0, mode='fill', fill_value=0)  352 us
    dot_general x27, matrix products, offset_step(): lax.dot_general(kernel, picked, (((1,), (1,)), ((), ())), preferred_eleme...  137 us
    psum x6, blocking collectives, region_sum(): x = lax.psum(x, axis)  58.2 us
    dot_general x27, matrix products, offset_step(): grad_piece = jnp.dot(grad_out, picked, preferred_element_type=jnp.float32)  43.4 us
    select_n x27, other arithmetic, offset_step(): picked = jnp.take(gathered, position, axis=0, mode='fill', fill_value=0)  24.9 us
  transfers between devices with their start and end apart: 6, of which 6 were waited for; matrix products, arithmetic and copies ran while one was open for 0% of the time, Pallas kernels for 0%

profile of v1, /device:TPU:0, one launch (start us, length us, event | category | flops | bytes accessed | tf_op | source)
XLA Modules:
  0.0 1148.6 jit_solution(16765144622355839185)
XLA Ops:
  10.2 11.2 all-reduce
  21.4 11.3 all-reduce.1
  32.8 12.4 %all-reduce.2 = (f32[192]{0:T(256)S(1)}, f32[]{:T(128)}) all-reduce(f32[192]{0:T(256)S(1)} %get-tuple-element.100, f32[]{:T(128)} %get-tuple-element.101), channel_id=1, replica_groups=mesh['z'=4,'y'=4,'x'=4,'chan'=2] {'z'}, use_global_device_ids=true, to_apply=%region_3.0 | all-reduce | flops 193 | bytes 1544 | tf_op jit(solution)/shard_map/psum | solution.py:13
  47.6 7.7 psum.90
  55.3 7.7 psum.91
  63.1 7.7 psum.92
  73.3 11.9 %all-gather.2.cloned.1.call-done = bf16[3072,384]{0,1:T(8,128)(2,1)} async-done(((bf16[3072,192]{0,1:T(8,128)(2,1)}), bf16[3072,384]{0,1:T(8,128)(2,1)}) %all-gather.2.cloned.1.call-update) | async-done | bytes 2359312 | tf_op jit(solution)/shard_map/all_gather | solution.py:49
  105.2 559.6 %while.13 = (s32[]{:T(128)}, f32[192,3072]{1,0:T(8,128)}, f32[27,192,384]{2,1,0:T(8,128)}, bf16[27,192,384]{2,1,0:T(8,128)(2,1)}, s32[27,3072]{1,0:T(8,128)}, /*...) while((s32[]{:T(128)}, f32[192,3072]{1,0:T(8,128)}, ...), condition=%wide.region_13.14_spmd.clone, body=%wide.region_12.13_spmd.clone.sunk | while | flops 909548544 | bytes 30030000 | solution.py:65
  106.2 13.0 %gather_fusion = bf16[3072,384]{1,0:T(8,128)(2,1)} fusion(bf16[3584,384]{1,0:T(8,128)(2,1)S(1)} %get-tuple-element.187, s32[3072]{0:T(1024)S(1)} %broadcast_clamp_fusion.2), kind=kCustom, calls=%fused_computation.clone.clone.1 | custom fusion | bytes 4730880 | tf_op jit(solution)/shard_map/while/body/eval_jaxpr/jit(_take)/gather | solution.py:57
  126.2 13.0 %gather_fusion = bf16[3072,384]{1,0:T(8,128)(2,1)} fusion(bf16[3584,384]{1,0:T(8,128)(2,1)S(1)} %get-tuple-element.187, s32[3072]{0:T(1024)S(1)} %broadcast_clamp_fusion.2), kind=kCustom, calls=%fused_computation.clone.clone.1 | custom fusion | bytes 4730880 | tf_op jit(solution)/shard_map/while/body/eval_jaxpr/jit(_take)/gather | solution.py:57
  139.3 5.1 convolution_add_fusion.2
  147.0 13.0 %gather_fusion = bf16[3072,384]{1,0:T(8,128)(2,1)} fusion(bf16[3584,384]{1,0:T(8,128)(2,1)S(1)} %get-tuple-element.187, s32[3072]{0:T(1024)S(1)} %broadcast_clamp_fusion.2), kind=kCustom, calls=%fused_computation.clone.clone.1 | custom fusion | bytes 4730880 | tf_op jit(solution)/shard_map/while/body/eval_jaxpr/jit(_take)/gather | solution.py:57
  160.0 5.1 convolution_add_fusion.2
  167.7 13.0 %gather_fusion = bf16[3072,384]{1,0:T(8,128)(2,1)} fusion(bf16[3584,384]{1,0:T(8,128)(2,1)S(1)} %get-tuple-element.187, s32[3072]{0:T(1024)S(1)} %broadcast_clamp_fusion.2), kind=kCustom, calls=%fused_computation.clone.clone.1 | custom fusion | bytes 4730880 | tf_op jit(solution)/shard_map/while/body/eval_jaxpr/jit(_take)/gather | solution.py:57
  180.8 5.1 convolution_add_fusion.2
  188.5 13.0 %gather_fusion = bf16[3072,384]{1,0:T(8,128)(2,1)} fusion(bf16[3584,384]{1,0:T(8,128)(2,1)S(1)} %get-tuple-element.187, s32[3072]{0:T(1024)S(1)} %broadcast_clamp_fusion.2), kind=kCustom, calls=%fused_computation.clone.clone.1 | custom fusion | bytes 4730880 | tf_op jit(solution)/shard_map/while/body/eval_jaxpr/jit(_take)/gather | solution.py:57
  201.5 5.1 convolution_add_fusion.2
  209.2 13.0 %gather_fusion = bf16[3072,384]{1,0:T(8,128)(2,1)} fusion(bf16[3584,384]{1,0:T(8,128)(2,1)S(1)} %get-tuple-element.187, s32[3072]{0:T(1024)S(1)} %broadcast_clamp_fusion.2), kind=kCustom, calls=%fused_computation.clone.clone.1 | custom fusion | bytes 4730880 | tf_op jit(solution)/shard_map/while/body/eval_jaxpr/jit(_take)/gather | solution.py:57
  222.3 5.1 convolution_add_fusion.2
  230.0 13.0 %gather_fusion = bf16[3072,384]{1,0:T(8,128)(2,1)} fusion(bf16[3584,384]{1,0:T(8,128)(2,1)S(1)} %get-tuple-element.187, s32[3072]{0:T(1024)S(1)} %broadcast_clamp_fusion.2), kind=kCustom, calls=%fused_computation.clone.clone.1 | custom fusion | bytes 4730880 | tf_op jit(solution)/shard_map/while/body/eval_jaxpr/jit(_take)/gather | solution.py:57
  243.0 5.1 convolution_add_fusion.2
  250.7 13.0 %gather_fusion = bf16[3072,384]{1,0:T(8,128)(2,1)} fusion(bf16[3584,384]{1,0:T(8,128)(2,1)S(1)} %get-tuple-element.187, s32[3072]{0:T(1024)S(1)} %broadcast_clamp_fusion.2), kind=kCustom, calls=%fused_computation.clone.clone.1 | custom fusion | bytes 4730880 | tf_op jit(solution)/shard_map/while/body/eval_jaxpr/jit(_take)/gather | solution.py:57
  263.8 5.1 convolution_add_fusion.2
  271.5 13.0 %gather_fusion = bf16[3072,384]{1,0:T(8,128)(2,1)} fusion(bf16[3584,384]{1,0:T(8,128)(2,1)S(1)} %get-tuple-element.187, s32[3072]{0:T(1024)S(1)} %broadcast_clamp_fusion.2), kind=kCustom, calls=%fused_computation.clone.clone.1 | custom fusion | bytes 4730880 | tf_op jit(solution)/shard_map/while/body/eval_jaxpr/jit(_take)/gather | solution.py:57
  284.5 5.1 convolution_add_fusion.2
  292.2 13.0 %gather_fusion = bf16[3072,384]{1,0:T(8,128)(2,1)} fusion(bf16[3584,384]{1,0:T(8,128)(2,1)S(1)} %get-tuple-element.187, s32[3072]{0:T(1024)S(1)} %broadcast_clamp_fusion.2), kind=kCustom, calls=%fused_computation.clone.clone.1 | custom fusion | bytes 4730880 | tf_op jit(solution)/shard_map/while/body/eval_jaxpr/jit(_take)/gather | solution.py:57
  305.3 5.1 convolution_add_fusion.2
  312.9 13.0 %gather_fusion = bf16[3072,384]{1,0:T(8,128)(2,1)} fusion(bf16[3584,384]{1,0:T(8,128)(2,1)S(1)} %get-tuple-element.187, s32[3072]{0:T(1024)S(1)} %broadcast_clamp_fusion.2), kind=kCustom, calls=%fused_computation.clone.clone.1 | custom fusion | bytes 4730880 | tf_op jit(solution)/shard_map/while/body/eval_jaxpr/jit(_take)/gather | solution.py:57
  326.0 5.1 convolution_add_fusion.2
  333.7 13.0 %gather_fusion = bf16[3072,384]{1,0:T(8,128)(2,1)} fusion(bf16[3584,384]{1,0:T(8,128)(2,1)S(1)} %get-tuple-element.187, s32[3072]{0:T(1024)S(1)} %broadcast_clamp_fusion.2), kind=kCustom, calls=%fused_computation.clone.clone.1 | custom fusion | bytes 4730880 | tf_op jit(solution)/shard_map/while/body/eval_jaxpr/jit(_take)/gather | solution.py:57
  346.8 5.1 convolution_add_fusion.2
  354.4 13.0 %gather_fusion = bf16[3072,384]{1,0:T(8,128)(2,1)} fusion(bf16[3584,384]{1,0:T(8,128)(2,1)S(1)} %get-tuple-element.187, s32[3072]{0:T(1024)S(1)} %broadcast_clamp_fusion.2), kind=kCustom, calls=%fused_computation.clone.clone.1 | custom fusion | bytes 4730880 | tf_op jit(solution)/shard_map/while/body/eval_jaxpr/jit(_take)/gather | solution.py:57
  367.5 5.1 convolution_add_fusion.2
  375.2 13.0 %gather_fusion = bf16[3072,384]{1,0:T(8,128)(2,1)} fusion(bf16[3584,384]{1,0:T(8,128)(2,1)S(1)} %get-tuple-element.187, s32[3072]{0:T(1024)S(1)} %broadcast_clamp_fusion.2), kind=kCustom, calls=%fused_computation.clone.clone.1 | custom fusion | bytes 4730880 | tf_op jit(solution)/shard_map/while/body/eval_jaxpr/jit(_take)/gather | solution.py:57
  388.3 5.1 convolution_add_fusion.2
  395.9 13.0 %gather_fusion = bf16[3072,384]{1,0:T(8,128)(2,1)} fusion(bf16[3584,384]{1,0:T(8,128)(2,1)S(1)} %get-tuple-element.187, s32[3072]{0:T(1024)S(1)} %broadcast_clamp_fusion.2), kind=kCustom, calls=%fused_computation.clone.clone.1 | custom fusion | bytes 4730880 | tf_op jit(solution)/shard_map/while/body/eval_jaxpr/jit(_take)/gather | solution.py:57
  409.0 5.1 convolution_add_fusion.2
  416.7 13.0 %gather_fusion = bf16[3072,384]{1,0:T(8,128)(2,1)} fusion(bf16[3584,384]{1,0:T(8,128)(2,1)S(1)} %get-tuple-element.187, s32[3072]{0:T(1024)S(1)} %broadcast_clamp_fusion.2), kind=kCustom, calls=%fused_computation.clone.clone.1 | custom fusion | bytes 4730880 | tf_op jit(solution)/shard_map/while/body/eval_jaxpr/jit(_take)/gather | solution.py:57
  429.8 5.1 convolution_add_fusion.2
  437.4 13.0 %gather_fusion = bf16[3072,384]{1,0:T(8,128)(2,1)} fusion(bf16[3584,384]{1,0:T(8,128)(2,1)S(1)} %get-tuple-element.187, s32[3072]{0:T(1024)S(1)} %broadcast_clamp_fusion.2), kind=kCustom, calls=%fused_computation.clone.clone.1 | custom fusion | bytes 4730880 | tf_op jit(solution)/shard_map/while/body/eval_jaxpr/jit(_take)/gather | solution.py:57
  450.5 5.1 convolution_add_fusion.2
  458.2 13.0 %gather_fusion = bf16[3072,384]{1,0:T(8,128)(2,1)} fusion(bf16[3584,384]{1,0:T(8,128)(2,1)S(1)} %get-tuple-element.187, s32[3072]{0:T(1024)S(1)} %broadcast_clamp_fusion.2), kind=kCustom, calls=%fused_computation.clone.clone.1 | custom fusion | bytes 4730880 | tf_op jit(solution)/shard_map/while/body/eval_jaxpr/jit(_take)/gather | solution.py:57
  471.3 5.1 convolution_add_fusion.2
  478.9 13.0 %gather_fusion = bf16[3072,384]{1,0:T(8,128)(2,1)} fusion(bf16[3584,384]{1,0:T(8,128)(2,1)S(1)} %get-tuple-element.187, s32[3072]{0:T(1024)S(1)} %broadcast_clamp_fusion.2), kind=kCustom, calls=%fused_computation.clone.clone.1 | custom fusion | bytes 4730880 | tf_op jit(solution)/shard_map/while/body/eval_jaxpr/jit(_take)/gather | solution.py:57
  492.0 5.1 convolution_add_fusion.2
  499.7 13.0 %gather_fusion = bf16[3072,384]{1,0:T(8,128)(2,1)} fusion(bf16[3584,384]{1,0:T(8,128)(2,1)S(1)} %get-tuple-element.187, s32[3072]{0:T(1024)S(1)} %broadcast_clamp_fusion.2), kind=kCustom, calls=%fused_computation.clone.clone.1 | custom fusion | bytes 4730880 | tf_op jit(solution)/shard_map/while/body/eval_jaxpr/jit(_take)/gather | solution.py:57
  512.8 5.1 convolution_add_fusion.2
  520.4 13.0 %gather_fusion = bf16[3072,384]{1,0:T(8,128)(2,1)} fusion(bf16[3584,384]{1,0:T(8,128)(2,1)S(1)} %get-tuple-element.187, s32[3072]{0:T(1024)S(1)} %broadcast_clamp_fusion.2), kind=kCustom, calls=%fused_computation.clone.clone.1 | custom fusion | bytes 4730880 | tf_op jit(solution)/shard_map/while/body/eval_jaxpr/jit(_take)/gather | solution.py:57
  533.5 5.1 convolution_add_fusion.2
  541.2 13.0 %gather_fusion = bf16[3072,384]{1,0:T(8,128)(2,1)} fusion(bf16[3584,384]{1,0:T(8,128)(2,1)S(1)} %get-tuple-element.187, s32[3072]{0:T(1024)S(1)} %broadcast_clamp_fusion.2), kind=kCustom, calls=%fused_computation.clone.clone.1 | custom fusion | bytes 4730880 | tf_op jit(solution)/shard_map/while/body/eval_jaxpr/jit(_take)/gather | solution.py:57
  554.3 5.1 convolution_add_fusion.2
  561.9 13.0 %gather_fusion = bf16[3072,384]{1,0:T(8,128)(2,1)} fusion(bf16[3584,384]{1,0:T(8,128)(2,1)S(1)} %get-tuple-element.187, s32[3072]{0:T(1024)S(1)} %broadcast_clamp_fusion.2), kind=kCustom, calls=%fused_computation.clone.clone.1 | custom fusion | bytes 4730880 | tf_op jit(solution)/shard_map/while/body/eval_jaxpr/jit(_take)/gather | solution.py:57
  575.0 5.1 convolution_add_fusion.2
  582.7 13.0 %gather_fusion = bf16[3072,384]{1,0:T(8,128)(2,1)} fusion(bf16[3584,384]{1,0:T(8,128)(2,1)S(1)} %get-tuple-element.187, s32[3072]{0:T(1024)S(1)} %broadcast_clamp_fusion.2), kind=kCustom, calls=%fused_computation.clone.clone.1 | custom fusion | bytes 4730880 | tf_op jit(solution)/shard_map/while/body/eval_jaxpr/jit(_take)/gather | solution.py:57
  595.8 5.1 convolution_add_fusion.2
  603.4 13.0 %gather_fusion = bf16[3072,384]{1,0:T(8,128)(2,1)} fusion(bf16[3584,384]{1,0:T(8,128)(2,1)S(1)} %get-tuple-element.187, s32[3072]{0:T(1024)S(1)} %broadcast_clamp_fusion.2), kind=kCustom, calls=%fused_computation.clone.clone.1 | custom fusion | bytes 4730880 | tf_op jit(solution)/shard_map/while/body/eval_jaxpr/jit(_take)/gather | solution.py:57
  616.5 5.1 convolution_add_fusion.2
  624.2 13.0 %gather_fusion = bf16[3072,384]{1,0:T(8,128)(2,1)} fusion(bf16[3584,384]{1,0:T(8,128)(2,1)S(1)} %get-tuple-element.187, s32[3072]{0:T(1024)S(1)} %broadcast_clamp_fusion.2), kind=kCustom, calls=%fused_computation.clone.clone.1 | custom fusion | bytes 4730880 | tf_op jit(solution)/shard_map/while/body/eval_jaxpr/jit(_take)/gather | solution.py:57
  644.9 13.0 %gather_fusion = bf16[3072,384]{1,0:T(8,128)(2,1)} fusion(bf16[3584,384]{1,0:T(8,128)(2,1)S(1)} %get-tuple-element.187, s32[3072]{0:T(1024)S(1)} %broadcast_clamp_fusion.2), kind=kCustom, calls=%fused_computation.clone.clone.1 | custom fusion | bytes 4730880 | tf_op jit(solution)/shard_map/while/body/eval_jaxpr/jit(_take)/gather | solution.py:57
  658.0 5.1 convolution_add_fusion.2
  664.8 158.1 %all-reduce.7.cloned.1.call-done = f32[27,192,384]{2,1,0:T(8,128)} async-done(((f32[27,192,384]{2,1,0:T(8,128)}), f32[27,192,384]{2,1,0:T(8,128)}) %all-reduce.7.cloned.1.call-update) | async-done | bytes 7962640 | tf_op jit(solution)/shard_map/psum | solution.py:13
  823.0 155.8 %all-reduce.9.cloned.1.call-done = f32[27,192,384]{2,1,0:T(8,128)} async-done(((f32[27,192,384]{2,1,0:T(8,128)}), f32[27,192,384]{2,1,0:T(8,128)}) %all-reduce.9.cloned.1.call-update) | async-done | bytes 7962640 | tf_op jit(solution)/shard_map/psum | solution.py:13
  981.6 153.1 %all-reduce.11.cloned.1.call-done = f32[27,192,384]{2,1,0:T(8,128)} async-done(((f32[27,192,384]{2,1,0:T(8,128)}), f32[27,192,384]{2,1,0:T(8,128)}) %all-reduce.11.cloned.1.call-update) | async-done | bytes 7962640 | tf_op jit(solution)/shard_map/psum | solution.py:13
  1134.7 7.4 copy.26
  (251 shorter events, 108.5 us)
Async XLA Ops:
  7.2 64.3 %copy-start.2 = (bf16[192,3072]{1,0:T(8,128)(2,1)S(1)}, bf16[192,3072]{1,0:T(8,128)(2,1)}, u32[]{:S(2)}) copy-start(bf16[192,3072]{1,0:T(8,128)(2,1)} %param.9) | copy-start | bytes 3538948
  7.2 63.6 %copy-start.4 = (f32[192]{0:T(256)S(1)}, f32[192]{0:T(256)}, u32[]{:S(2)}) copy-start(f32[192]{0:T(256)} %param.10) | copy-start | bytes 2308
  7.2 64.3 %copy-start.3 = (f32[192]{0:T(256)S(1)}, f32[192]{0:T(256)}, u32[]{:S(2)}) copy-start(f32[192]{0:T(256)} %param.11) | copy-start | bytes 2308
  7.2 78.0 %all-gather.2.cloned.1.call-start = ((), (), s32[]{:S(2)}) async-start(), calls=%async_computation | async-start | bytes 3538944 | tf_op jit(solution)/shard_map/all_gather | solution.py:49
  73.2 749.7 %all-reduce.7.cloned.1.call-start = ((), (), s32[]{:S(2)}) async-start(), calls=%async_computation.1 | async-start | bytes 15925248 | tf_op jit(solution)/shard_map/psum | solution.py:13
  86.2 8.1 collective-permute-start
  89.7 8.7 collective-permute-start.1
  119.2 4.4 copy-start
  119.2 4.4 copy-start.5
  139.3 5.1 copy-start
  139.3 5.1 copy-start.5
  160.0 5.1 copy-start
  160.0 5.1 copy-start.5
  180.8 5.1 copy-start
  180.8 5.1 copy-start.5
  201.5 5.1 copy-start
  201.5 5.1 copy-start.5
  222.3 5.1 copy-start
  222.3 5.1 copy-start.5
  243.0 5.1 copy-start
  243.0 5.1 copy-start.5
  263.8 5.1 copy-start
  263.8 5.1 copy-start.5
  284.5 5.1 copy-start
  284.5 5.1 copy-start.5
  305.3 5.1 copy-start
  305.3 5.1 copy-start.5
  326.0 5.1 copy-start
  326.0 5.1 copy-start.5
  346.8 5.1 copy-start
  346.8 5.1 copy-start.5
  367.5 5.1 copy-start
  367.5 5.1 copy-start.5
  388.3 5.1 copy-start
  388.3 5.1 copy-start.5
  409.0 5.1 copy-start
  409.0 5.1 copy-start.5
  429.8 5.1 copy-start
  429.8 5.1 copy-start.5
  450.5 5.1 copy-start
  450.5 5.1 copy-start.5
  471.3 5.1 copy-start
  471.3 5.1 copy-start.5
  492.0 5.1 copy-start
  492.0 5.1 copy-start.5
  512.8 5.1 copy-start
  512.8 5.1 copy-start.5
  533.5 5.1 copy-start
  533.5 5.1 copy-start.5
  554.3 5.1 copy-start
  554.3 5.1 copy-start.5
  575.0 5.1 copy-start
  575.0 5.1 copy-start.5
  595.8 5.1 copy-start
  595.8 5.1 copy-start.5
  616.5 5.1 copy-start
  616.5 5.1 copy-start.5
  637.3 5.1 copy-start
  637.3 5.1 copy-start.5
  658.0 5.1 copy-start
  658.0 5.1 copy-start.5
  664.8 314.0 %all-reduce.9.cloned.1.call-start = ((), (), s32[]{:S(2)}) async-start(), calls=%async_computation.2 | async-start | bytes 15925248 | tf_op jit(solution)/shard_map/psum | solution.py:13
  823.0 311.8 %all-reduce.11.cloned.1.call-start = ((), (), s32[]{:S(2)}) async-start(), calls=%async_computation.3 | async-start | bytes 15925248 | tf_op jit(solution)/shard_map/psum | solution.py:13
  978.8 1.7 copy-start.1
Sparse Core Ops, SparseCore 0:
  73.3 11.7 all-gather.1
  664.9 157.9 all-reduce.6
  825.4 153.3 all-reduce.8
  981.1 153.5 all-reduce.10

commit v2 on v1

--- a/solution.py
+++ b/solution.py
@@ -1,11 +1,16 @@
+import functools
+
 import jax
 import jax.numpy as jnp
 import numpy as np
 from jax import lax
+from jax.experimental import pallas as pl
+from jax.experimental.pallas import tpu as pltpu
 from jax.sharding import Mesh
 from jax.sharding import PartitionSpec as P
 
 SUB = ("z", "y", "x")
+BLOCK = 256
 
 
 def region_sum(x):
@@ -16,14 +21,69 @@
 
 def padded(x, width):
     count = lax.axis_size(SUB)
-    length = x.shape[0]
+    length = x.shape[1]
     up = [(i, (i + 1) % count) for i in range(count - 1)]
     down = [(j, i) for i, j in up]
-    last = lax.slice_in_dim(x, length - width, length, axis=0)
-    first = lax.slice_in_dim(x, 0, width, axis=0)
+    last = lax.slice_in_dim(x, length - width, length, axis=1)
+    first = lax.slice_in_dim(x, 0, width, axis=1)
     before = lax.ppermute(last, SUB, up)
     after = lax.ppermute(first, SUB, down)
-    return jnp.concatenate([before, x, after], axis=0)
+    return jnp.concatenate([before, x, after], axis=1)
+
+
+def conv_kernel(rel_ref, act_ref, w_ref, g_ref, out_ref, kg_ref, *, halo, offsets):
+    b = pl.program_id(0)
+    window = BLOCK + 2 * halo
+
+    @pl.when(b == 0)
+    def _():
+        kg_ref[...] = jnp.zeros_like(kg_ref)
+
+    start = pl.multiple_of(b * BLOCK, BLOCK)
+    win = act_ref[:, pl.ds(start, window)]
+    g_blk = g_ref[...]
+    rows = lax.broadcasted_iota(jnp.int32, (window, BLOCK), 0)
+
+    def step(k, acc):
+        idx = rel_ref[pl.ds(k, 1), :]
+        onehot = jnp.where(rows == idx, 1.0, 0.0).astype(jnp.bfloat16)
+        picked = jnp.dot(win, onehot, preferred_element_type=jnp.float32).astype(jnp.bfloat16)
+        acc = acc + jnp.dot(w_ref[k], picked, preferred_element_type=jnp.float32)
+        kg_ref[k] += lax.dot_general(
+            g_blk, picked, (((1,), (1,)), ((), ())), preferred_element_type=jnp.float32
+        )
+        return acc
+
+    acc = lax.fori_loop(0, offsets, step, jnp.zeros(out_ref.shape, jnp.float32))
+    out_ref[...] = acc.astype(out_ref.dtype)
+
+
+def conv_call(rel, act, weights, grad_out, halo):
+    offsets, o_ch, c_all = weights.shape
+    columns = grad_out.shape[1]
+    extent = act.shape[1]
+    kern = functools.partial(conv_kernel, halo=halo, offsets=offsets)
+    return pl.pallas_call(
+        kern,
+        grid=(columns // BLOCK,),
+        in_specs=[
+            pl.BlockSpec((offsets, BLOCK), lambda b: (0, b)),
+            pl.BlockSpec((c_all, extent), lambda b: (0, 0)),
+            pl.BlockSpec((offsets, o_ch, c_all), lambda b: (0, 0, 0)),
+            pl.BlockSpec((o_ch, BLOCK), lambda b: (0, b)),
+        ],
+        out_specs=[
+            pl.BlockSpec((o_ch, BLOCK), lambda b: (0, b)),
+            pl.BlockSpec((offsets, o_ch, c_all), lambda b: (0, 0, 0)),
+        ],
+        out_shape=[
+            jax.ShapeDtypeStruct((o_ch, columns), jnp.bfloat16),
+            jax.ShapeDtypeStruct((offsets, o_ch, c_all), jnp.float32),
+        ],
+        compiler_params=pltpu.CompilerParams(
+            dimension_semantics=("arbitrary",), vmem_limit_bytes=56 * 1024 * 1024
+        ),
+    )(rel, act, weights, grad_out)
 
 
 def per_device(features, gain, bias, live, neighbors, weights, grad_out):
@@ -44,27 +104,15 @@
     normed = (
         jnp.maximum((values - average[:, None]) * factor[:, None] + bias[:, None], 0.0)
         * live_mask[None, :]
-    )
-    site_rows = jnp.transpose(normed).astype(jnp.bfloat16)
-    own_chans = lax.all_gather(site_rows, "chan", axis=1, tiled=True)
+    ).astype(jnp.bfloat16)
+    own_chans = lax.all_gather(normed, "chan", axis=0, tiled=True)
     gathered = padded(own_chans, border)
     anchor = region_idx * columns - border
-    extent = columns + 2 * border
-
-    def offset_step(running, operand):
-        kernel, targets = operand
-        position = jnp.where(targets < 0, extent, targets - anchor)
-        picked = jnp.take(gathered, position, axis=0, mode="fill", fill_value=0)
-        running = running + lax.dot_general(
-            kernel, picked, (((1,), (1,)), ((), ())), preferred_element_type=jnp.float32
-        )
-        grad_piece = jnp.dot(grad_out, picked, preferred_element_type=jnp.float32)
-        return (running, grad_piece)
-
-    start = jnp.zeros((weights.shape[1], columns), jnp.float32)
-    conv_sum, grad_parts = lax.scan(offset_step, start, (weights, neighbors))
-    kernel_grad = region_sum(grad_parts)
-    return (conv_sum.astype(jnp.bfloat16), kernel_grad)
+    block_base = (column // BLOCK) * BLOCK
+    rel = jnp.where(neighbors < 0, -1, neighbors - anchor - block_base[None, :])
+    conv_out, grad_parts = conv_call(rel, gathered, weights, grad_out, border)
+    kernel_grad = lax.psum(grad_parts, SUB)
+    return (conv_out, kernel_grad)
 
 
 def sub_mesh(mesh):

time: 1150 us -> 535 us (0.47)
  local copies, waits for them, and re-layouts: 366 us -> 8.43 us
  waiting for transfers between devices: 486 us -> 192 us
  Pallas kernels: 0 us -> 244 us
  matrix products: 181 us -> 0 us
  other arithmetic: 36.9 us -> 11.3 us
    gather x27 -> x0, local copies, waits for them, and re-layouts: 352 us -> none  [offset_step(): picked = jnp.take(gathered, position, axis=0, mode='fill', fill_value=0)]
    psum x3 -> x1, waiting for transfers between devices: 467 us -> 173 us  [per_device(): kernel_grad = lax.psum(grad_parts, SUB)]
    pallas_call x0 -> x1, Pallas kernels: none -> 244 us  [conv_call(): pl.pallas_call(kern, grid=(columns // BLOCK,), in_specs=[pl.BlockSpec((of...]
    dot_general x54 -> x0, matrix products: 181 us -> none  [the longest x27 137 us: offset_step(): lax.dot_general(kernel, picked, (((1,), (1,)), ((), ())), preferred_eleme...]
    select_n x27 -> x1, other arithmetic: 24.9 us -> 0.81 us  [per_device(): rel = jnp.where(neighbors < 0, -1, neighbors - anchor - block_base[None, :])]
  transfers between devices with their start and end apart: 6 -> 4, of which waited for: 6 -> 4; matrix products, arithmetic and copies ran while one was open for 0% -> 0% of each run, Pallas kernels for 0% -> 0%
where the time goes in v2:
time: 535 us; the launch traced here: 534 us
  Pallas kernels  244 us (46%)
  waiting for transfers between devices  192 us (36%)
  blocking collectives  58.3 us (11%)
  between operations  14.9 us (3%)
  other arithmetic  11.3 us (2%)
  local copies, waits for them, and re-layouts  8.43 us (2%)
    pallas_call x1, Pallas kernels, conv_call(): pl.pallas_call(kern, grid=(columns // BLOCK,), in_specs=[pl.BlockSpec((of...  244 us
    psum x1, waiting for transfers between devices, per_device(): kernel_grad = lax.psum(grad_parts, SUB)  173 us
    psum x6, blocking collectives, region_sum(): x = lax.psum(x, axis)  58.3 us
    all_gather x1, waiting for transfers between devices, per_device(): own_chans = lax.all_gather(normed, 'chan', axis=0, tiled=True)  11.9 us
  transfers between devices with their start and end apart: 4, of which 4 were waited for; matrix products, arithmetic and copies ran while one was open for 0% of the time, Pallas kernels for 0%

profile of v2, /device:TPU:0, one launch (start us, length us, event | category | flops | bytes accessed | tf_op | source)
XLA Modules:
  0.0 534.0 jit_solution(2776440845565446522)
XLA Ops:
  7.2 0.0 copy-start
  7.2 0.0 copy-start.3
  7.2 0.0 copy-start.2
  7.2 0.0 all-gather.2.cloned.1.call-start
  8.0 0.6 fusion.15
  8.6 1.6 fusion.8
  10.2 11.2 %all-reduce = (f32[192]{0:T(256)S(1)}, f32[]{:T(128)}) all-reduce(f32[192]{0:T(256)S(1)} %fusion.8, f32[]{:T(128)} %fusion.15), channel_id=1, replica_groups=mesh['z'=4,'y'=4,'x'=4,'chan'=2] {'x'}, use_global_device_ids=true, to_apply=%region_1.0 | all-reduce | flops 193 | bytes 1544 | tf_op jit(solution)/shard_map/psum | solution.py:18
  21.4 11.3 %all-reduce.1 = (f32[192]{0:T(256)S(1)}, f32[]{:T(128)}) all-reduce(f32[192]{0:T(256)S(1)} %get-tuple-element.6, f32[]{:T(128)} %get-tuple-element.7), channel_id=1, replica_groups=mesh['z'=4,'y'=4,'x'=4,'chan'=2] {'y'}, use_global_device_ids=true, to_apply=%region_2.0 | all-reduce | flops 193 | bytes 1544 | tf_op jit(solution)/shard_map/psum | solution.py:18
  32.8 12.4 %all-reduce.2 = (f32[192]{0:T(256)S(1)}, f32[]{:T(128)}) all-reduce(f32[192]{0:T(256)S(1)} %get-tuple-element.8, f32[]{:T(128)} %get-tuple-element.9), channel_id=1, replica_groups=mesh['z'=4,'y'=4,'x'=4,'chan'=2] {'z'}, use_global_device_ids=true, to_apply=%region_3.0 | all-reduce | flops 193 | bytes 1544 | tf_op jit(solution)/shard_map/psum | solution.py:18
  45.1 0.6 broadcast_divide_fusion
  45.8 1.8 fusion.3
  47.6 0.0 copy-start.1
  47.6 7.9 %psum.76 = f32[192]{0:T(256)S(1)} all-reduce(f32[192]{0:T(256)S(1)} %fusion.3), channel_id=1, replica_groups=mesh['z'=4,'y'=4,'x'=4,'chan'=2] {'x'}, use_global_device_ids=true, to_apply=%region_9.0 | all-reduce | flops 192 | bytes 1536 | tf_op jit(solution)/shard_map/psum | solution.py:18
  55.5 7.7 %psum.77 = f32[192]{0:T(256)S(1)} all-reduce(f32[192]{0:T(256)S(1)} %psum.76), channel_id=1, replica_groups=mesh['z'=4,'y'=4,'x'=4,'chan'=2] {'y'}, use_global_device_ids=true, to_apply=%region_10.0 | all-reduce | flops 192 | bytes 1536 | tf_op jit(solution)/shard_map/psum | solution.py:18
  63.2 7.7 %psum.78 = f32[192]{0:T(256)S(1)} all-reduce(f32[192]{0:T(256)S(1)} %psum.77), channel_id=1, replica_groups=mesh['z'=4,'y'=4,'x'=4,'chan'=2] {'z'}, use_global_device_ids=true, to_apply=%region_11.0 | all-reduce | flops 192 | bytes 1536 | tf_op jit(solution)/shard_map/psum | solution.py:18
  70.9 0.0 copy-done.3
  70.9 0.7 rsqrt_multiply_fusion
  71.6 0.0 copy-done
  71.6 0.0 copy-done.2
  71.6 1.7 fusion.7
  73.3 0.0 all-gather.2.cloned.1.call-update
  73.4 0.0 all-reduce.5.cloned.1.call-start
  73.4 11.9 %all-gather.2.cloned.1.call-done = bf16[384,3072]{1,0:T(8,128)(2,1)} async-done(((bf16[192,3072]{1,0:T(8,128)(2,1)}), bf16[384,3072]{1,0:T(8,128)(2,1)}) %all-gather.2.cloned.1.call-update) | async-done | bytes 2359312 | tf_op jit(solution)/shard_map/all_gather | solution.py:108
  85.3 1.1 fusion.16
  86.4 3.5 collective-permute-start
  89.9 1.3 collective-permute-start.1
  91.2 0.0 copy-done.1
  91.2 0.8 subtract_select_fusion.rel_ref
  92.0 2.5 collective-permute-done
  94.4 4.1 collective-permute-done.1
  98.6 3.4 pad_maximum_fusion.act_ref
  102.0 244.4 %shard_map.86 = (bf16[192,3072]{1,0:T(8,128)(2,1)}, f32[27,192,384]{2,1,0:T(8,128)}) custom-call(s32[27,3072]{1,0:T(8,128)} %subtract_select_fusion.rel_ref, bf16[384,3584]{1,0:T(8,128)(2,1)} %pad_maximum_fusion.act_ref, bf16[27,192,384]{2,1,0:T(8,128)(2,1)} %w_ref.1, bf16[192,3072]{1,0:T(8,128)(2,1)} %g_ref.1), custom_call_target="tpu_custom_call" | custom-call | tf_op jit(solution)/shard_map/pallas_call | solution.py:66
  346.4 0.0 all-reduce.5.cloned.1.call-update
  346.4 173.4 %all-reduce.5.cloned.1.call-done = f32[27,192,384]{2,1,0:T(8,128)} async-done(((f32[27,192,384]{2,1,0:T(8,128)}), f32[27,192,384]{2,1,0:T(8,128)}) %all-reduce.5.cloned.1.call-update) | async-done | bytes 7962640 | tf_op jit(solution)/shard_map/psum | solution.py:114
  519.8 7.4 %copy.11 = f32[27,192,384]{2,1,0:T(8,128)} copy(f32[27,192,384]{2,1,0:T(8,128)} %all-reduce.5.cloned.1.call-done) | data formatting | bytes 15925248
  (2 shorter events, 0.0 us)
Async XLA Ops:
  7.2 64.4 %copy-start = (bf16[192,3072]{1,0:T(8,128)(2,1)S(1)}, bf16[192,3072]{1,0:T(8,128)(2,1)}, u32[]{:S(2)}) copy-start(bf16[192,3072]{1,0:T(8,128)(2,1)} %param.7) | copy-start | bytes 3538948
  7.2 63.7 %copy-start.3 = (f32[192]{0:T(256)S(1)}, f32[192]{0:T(256)}, u32[]{:S(2)}) copy-start(f32[192]{0:T(256)} %param.8) | copy-start | bytes 2308
  7.2 64.4 %copy-start.2 = (f32[192]{0:T(256)S(1)}, f32[192]{0:T(256)}, u32[]{:S(2)}) copy-start(f32[192]{0:T(256)} %param.9) | copy-start | bytes 2308
  7.2 78.1 %all-gather.2.cloned.1.call-start = ((), (), s32[]{:S(2)}) async-start(), calls=%async_computation | async-start | bytes 3538944 | tf_op jit(solution)/shard_map/all_gather | solution.py:108
  47.6 43.6 %copy-start.1 = (s32[27,3072]{1,0:T(8,128)S(1)}, s32[27,3072]{1,0:T(8,128)}, u32[]{:S(2)}) copy-start(s32[27,3072]{1,0:T(8,128)} %param.11) | copy-start | bytes 995332
  73.4 446.5 %all-reduce.5.cloned.1.call-start = ((), (), s32[]{:S(2)}) async-start(), calls=%async_computation.1 | async-start | bytes 15925248 | tf_op jit(solution)/shard_map/psum | solution.py:114
  86.4 8.1 %collective-permute-start = (bf16[384,256]{1,0:T(8,128)(2,1)S(1)}, bf16[384,256]{1,0:T(8,128)(2,1)S(1)}, u32[]{:S(2)}, u32[]{:S(2)}) collective-permute-start(bf16[384,256]{1,0:T(8,128)(2,1)S(1)} %get-tuple-element.12), channel_id=1, source_target_pairs={{0,2},{2,4},{4,6},{6,8},{8,10},{10,12},{12,14},{14,16},{16,18},{18... | collective-permute-start | bytes 589832 | tf_op jit(solution)/shard_map/ppermute | solution.py:29
  89.9 8.7 %collective-permute-start.1 = (bf16[384,256]{1,0:T(8,128)(2,1)S(1)}, bf16[384,256]{1,0:T(8,128)(2,1)S(1)}, u32[]{:S(2)}, u32[]{:S(2)}) collective-permute-start(bf16[384,256]{1,0:T(8,128)(2,1)S(1)} %get-tuple-element.13), channel_id=1, source_target_pairs={{2,0},{4,2},{6,4},{8,6},{10,8},{12,10},{14,12},{16,14},{18,16},{20... | collective-permute-start | bytes 589832 | tf_op jit(solution)/shard_map/ppermute | solution.py:30
Sparse Core Ops, SparseCore 0:
  73.5 11.7 all-gather.1
  346.5 173.2 all-reduce.4

commit v3 on v2

--- a/solution.py
+++ b/solution.py
@@ -11,6 +11,7 @@
 
 SUB = ("z", "y", "x")
 BLOCK = 256
+CHUNKS = (9, 7, 5, 4, 2)
 
 
 def region_sum(x):
@@ -31,7 +32,11 @@
     return jnp.concatenate([before, x, after], axis=1)
 
 
-def conv_kernel(rel_ref, act_ref, w_ref, g_ref, out_ref, kg_ref, *, halo, offsets):
+def conv_kernel(*refs, halo, k0, count, first):
+    if first:
+        rel_ref, act_ref, w_ref, g_ref, out_ref, kg_ref = refs
+    else:
+        rel_ref, act_ref, w_ref, g_ref, acc_ref, out_ref, kg_ref = refs
     b = pl.program_id(0)
     window = BLOCK + 2 * halo
 
@@ -45,45 +50,55 @@
     rows = lax.broadcasted_iota(jnp.int32, (window, BLOCK), 0)
 
     def step(k, acc):
-        idx = rel_ref[pl.ds(k, 1), :]
+        idx = rel_ref[pl.ds(k0 + k, 1), :]
         onehot = jnp.where(rows == idx, 1.0, 0.0).astype(jnp.bfloat16)
         picked = jnp.dot(win, onehot, preferred_element_type=jnp.float32).astype(jnp.bfloat16)
-        acc = acc + jnp.dot(w_ref[k], picked, preferred_element_type=jnp.float32)
+        acc = acc + jnp.dot(w_ref[k0 + k], picked, preferred_element_type=jnp.float32)
         kg_ref[k] += lax.dot_general(
             g_blk, picked, (((1,), (1,)), ((), ())), preferred_element_type=jnp.float32
         )
         return acc
 
-    acc = lax.fori_loop(0, offsets, step, jnp.zeros(out_ref.shape, jnp.float32))
+    init = jnp.zeros(out_ref.shape, jnp.float32) if first else acc_ref[...]
+    acc = lax.fori_loop(0, count, step, init)
     out_ref[...] = acc.astype(out_ref.dtype)
 
 
-def conv_call(rel, act, weights, grad_out, halo):
+def conv_call(rel, act, weights, grad_out, acc, halo, k0, count, last):
     offsets, o_ch, c_all = weights.shape
     columns = grad_out.shape[1]
     extent = act.shape[1]
-    kern = functools.partial(conv_kernel, halo=halo, offsets=offsets)
+    first = acc is None
+    kern = functools.partial(conv_kernel, halo=halo, k0=k0, count=count, first=first)
+    site_block = pl.BlockSpec((o_ch, BLOCK), lambda b: (0, b))
+    in_specs = [
+        pl.BlockSpec((offsets, BLOCK), lambda b: (0, b)),
+        pl.BlockSpec((c_all, extent), lambda b: (0, 0)),
+        pl.BlockSpec((offsets, o_ch, c_all), lambda b: (0, 0, 0)),
+        site_block,
+    ]
+    args = [rel, act, weights, grad_out]
+    aliases = {}
+    if not first:
+        in_specs.append(site_block)
+        args.append(acc)
+        if not last:
+            aliases = {4: 0}
+    out_type = jnp.bfloat16 if last else jnp.float32
     return pl.pallas_call(
         kern,
         grid=(columns // BLOCK,),
-        in_specs=[
-            pl.BlockSpec((offsets, BLOCK), lambda b: (0, b)),
-            pl.BlockSpec((c_all, extent), lambda b: (0, 0)),
-            pl.BlockSpec((offsets, o_ch, c_all), lambda b: (0, 0, 0)),
-            pl.BlockSpec((o_ch, BLOCK), lambda b: (0, b)),
+        in_specs=in_specs,
+        out_specs=[site_block, pl.BlockSpec((count, o_ch, c_all), lambda b: (0, 0, 0))],
+        out_shape=[
+            jax.ShapeDtypeStruct((o_ch, columns), out_type),
+            jax.ShapeDtypeStruct((count, o_ch, c_all), jnp.float32),
         ],
-        out_specs=[
-            pl.BlockSpec((o_ch, BLOCK), lambda b: (0, b)),
-            pl.BlockSpec((offsets, o_ch, c_all), lambda b: (0, 0, 0)),
-        ],
-        out_shape=[
-            jax.ShapeDtypeStruct((o_ch, columns), jnp.bfloat16),
-            jax.ShapeDtypeStruct((offsets, o_ch, c_all), jnp.float32),
-        ],
+        input_output_aliases=aliases,
         compiler_params=pltpu.CompilerParams(
             dimension_semantics=("arbitrary",), vmem_limit_bytes=56 * 1024 * 1024
         ),
-    )(rel, act, weights, grad_out)
+    )(*args)
 
 
 def per_device(features, gain, bias, live, neighbors, weights, grad_out):
@@ -110,9 +125,18 @@
     anchor = region_idx * columns - border
     block_base = (column // BLOCK) * BLOCK
     rel = jnp.where(neighbors < 0, -1, neighbors - anchor - block_base[None, :])
-    conv_out, grad_parts = conv_call(rel, gathered, weights, grad_out, border)
-    kernel_grad = lax.psum(grad_parts, SUB)
-    return (conv_out, kernel_grad)
+    acc = None
+    pieces = []
+    k0 = 0
+    for count in CHUNKS:
+        acc, part = conv_call(
+            rel, gathered, weights, grad_out, acc, border, k0, count, k0 + count == len(weights)
+        )
+        if pieces:
+            part, _ = lax.optimization_barrier((part, pieces[-1]))
+        pieces.append(lax.psum(part, SUB))
+        k0 += count
+    return (acc, jnp.concatenate(pieces, axis=0))
 
 
 def sub_mesh(mesh):

time: 535 us -> 868 us (1.62)
  waiting for transfers between devices: 192 us -> 503 us
  Pallas kernels: 244 us -> 265 us
    psum x1 -> x5, waiting for transfers between devices: 173 us -> 486 us  [per_device(): pieces.append(lax.psum(part, SUB))]
    pallas_call x1 -> x5, Pallas kernels: 244 us -> 265 us  [conv_call(): pl.pallas_call(kern, grid=(columns // BLOCK,), in_specs=in_specs, out_spe...]
  transfers between devices with their start and end apart: 4 -> 8, of which waited for: 4 -> 8; matrix products, arithmetic and copies ran while one was open for 0% -> 1% of each run, Pallas kernels for 0% -> 21%
where the time goes in v3:
time: 868 us
  waiting for transfers between devices  503 us (58%)
  Pallas kernels  265 us (31%)
  blocking collectives  58.3 us (7%)
  between operations  15 us (2%)
  local copies, waits for them, and re-layouts  13.9 us (2%)
    psum x5, waiting for transfers between devices, per_device(): pieces.append(lax.psum(part, SUB))  486 us
    pallas_call x5, Pallas kernels, conv_call(): pl.pallas_call(kern, grid=(columns // BLOCK,), in_specs=in_specs, out_spe...  265 us
    psum x6, blocking collectives, region_sum(): x = lax.psum(x, axis)  58.3 us
  transfers between devices with their start and end apart: 8, of which 8 were waited for; matrix products, arithmetic and copies ran while one was open for 1% of the time, Pallas kernels for 21%

profile of v3, /device:TPU:0, one launch (start us, length us, event | category | flops | bytes accessed | tf_op | source)
XLA Modules:
  0.0 867.8 jit_solution(6178718213410325633)
XLA Ops:
  7.2 0.0 copy-start.1
  7.2 0.0 copy-start.8
  7.2 0.0 copy-start.7
  7.2 0.0 all-gather.2.cloned.1.call-start
  8.0 0.6 fusion.15
  8.6 1.6 fusion.8
  10.2 11.2 %all-reduce = (f32[192]{0:T(256)S(1)}, f32[]{:T(128)}) all-reduce(f32[192]{0:T(256)S(1)} %fusion.8, f32[]{:T(128)} %fusion.15), channel_id=1, replica_groups=mesh['z'=4,'y'=4,'x'=4,'chan'=2] {'x'}, use_global_device_ids=true, to_apply=%region_1.0 | all-reduce | flops 193 | bytes 1544 | tf_op jit(solution)/shard_map/psum | solution.py:19
  21.4 11.3 %all-reduce.1 = (f32[192]{0:T(256)S(1)}, f32[]{:T(128)}) all-reduce(f32[192]{0:T(256)S(1)} %get-tuple-element.30, f32[]{:T(128)} %get-tuple-element.31), channel_id=1, replica_groups=mesh['z'=4,'y'=4,'x'=4,'chan'=2] {'y'}, use_global_device_ids=true, to_apply=%region_2.0 | all-reduce | flops 193 | bytes 1544 | tf_op jit(solution)/shard_map/psum | solution.py:19
  32.8 12.4 %all-reduce.2 = (f32[192]{0:T(256)S(1)}, f32[]{:T(128)}) all-reduce(f32[192]{0:T(256)S(1)} %get-tuple-element.32, f32[]{:T(128)} %get-tuple-element.33), channel_id=1, replica_groups=mesh['z'=4,'y'=4,'x'=4,'chan'=2] {'z'}, use_global_device_ids=true, to_apply=%region_3.0 | all-reduce | flops 193 | bytes 1544 | tf_op jit(solution)/shard_map/psum | solution.py:19
  45.1 0.6 broadcast_divide_fusion
  45.8 1.8 fusion.3
  47.6 0.0 copy-start.6
  47.6 7.9 psum.104
  55.5 7.7 psum.105
  63.2 7.7 psum.106
  70.9 0.0 copy-done.8
  70.9 0.7 rsqrt_multiply_fusion
  71.6 0.0 copy-done.1
  71.6 0.0 copy-done.7
  71.6 1.7 fusion.7
  73.3 0.0 all-gather.2.cloned.1.call-update
  73.4 0.0 all-reduce.9.cloned.1.call-start
  73.4 11.9 %all-gather.2.cloned.1.call-done = bf16[384,3072]{1,0:T(8,128)(2,1)} async-done(((bf16[192,3072]{1,0:T(8,128)(2,1)}), bf16[384,3072]{1,0:T(8,128)(2,1)}) %all-gather.2.cloned.1.call-update) | async-done | bytes 2359312 | tf_op jit(solution)/shard_map/all_gather | solution.py:123
  85.3 1.1 fusion.16
  86.4 3.5 collective-permute-start
  89.9 0.0 copy-done.6
  89.9 0.8 subtract_select_fusion.refs_0_
  90.7 1.3 collective-permute-start.1
  92.0 2.5 collective-permute-done
  94.5 1.8 constant_dynamic-update-slice_fusion.1
  96.3 3.1 collective-permute-done.1
  99.4 0.0 copy-start
  99.4 1.5 copy-done
  100.9 84.6 %shard_map.86 = (f32[192,3072]{1,0:T(8,128)}, f32[9,192,384]{2,1,0:T(8,128)}) custom-call(s32[27,3072]{1,0:T(8,128)} %subtract_select_fusion.refs_0_, bf16[384,3584]{1,0:T(8,128)(2,1)} %copy-done, bf16[27,192,384]{2,1,0:T(8,128)(2,1)} %refs_2_.9, bf16[192,3072]{1,0:T(8,128)(2,1)} %refs_3_.9), custom_call_target="tpu_custom_call" | custom-call | tf_op jit(solution)/shard_map/pallas_call | solution.py:88
  185.5 0.0 all-reduce.9.cloned.1.call-update
  185.6 0.0 all-reduce.11.cloned.1.call-start
  185.6 67.2 %shard_map.87 = (f32[192,3072]{1,0:T(8,128)}, f32[7,192,384]{2,1,0:T(8,128)}) custom-call(s32[27,3072]{1,0:T(8,128)} %subtract_select_fusion.refs_0_, bf16[384,3584]{1,0:T(8,128)(2,1)} %copy-done, bf16[27,192,384]{2,1,0:T(8,128)(2,1)} %refs_2_.9, bf16[192,3072]{1,0:T(8,128)(2,1)} %refs_3_.9, ...), custom_call_target="tpu_custom_call", output_to_operand_aliasing={{0}: (4, {})} | custom-call | tf_op jit(solution)/shard_map/pallas_call | solution.py:88
  252.8 72.5 %all-reduce.9.cloned.1.call-done = f32[9,192,384]{2,1,0:T(8,128)} async-done(((f32[9,192,384]{2,1,0:T(8,128)}), f32[9,192,384]{2,1,0:T(8,128)}) %all-reduce.9.cloned.1.call-update) | async-done | bytes 2654224 | tf_op jit(solution)/shard_map/psum | solution.py:137
  325.3 0.0 all-reduce.11.cloned.1.call-update
  325.3 0.0 all-reduce.13.cloned.1.call-start
  325.3 49.5 %shard_map.88 = (f32[192,3072]{1,0:T(8,128)}, f32[5,192,384]{2,1,0:T(8,128)}) custom-call(s32[27,3072]{1,0:T(8,128)} %subtract_select_fusion.refs_0_, bf16[384,3584]{1,0:T(8,128)(2,1)} %copy-done, bf16[27,192,384]{2,1,0:T(8,128)(2,1)} %refs_2_.9, bf16[192,3072]{1,0:T(8,128)(2,1)} %refs_3_.9, ...), custom_call_target="tpu_custom_call", output_to_operand_aliasing={{0}: (4, {})} | custom-call | tf_op jit(solution)/shard_map/pallas_call | solution.py:88
  374.8 85.8 %all-reduce.11.cloned.1.call-done = f32[7,192,384]{2,1,0:T(8,128)} async-done(((f32[7,192,384]{2,1,0:T(8,128)}), f32[7,192,384]{2,1,0:T(8,128)}) %all-reduce.11.cloned.1.call-update) | async-done | bytes 2064400 | tf_op jit(solution)/shard_map/psum | solution.py:137
  460.6 0.0 all-reduce.13.cloned.1.call-update
  460.7 0.0 all-reduce.15.cloned.1.call-start
  460.7 40.6 %shard_map.89 = (f32[192,3072]{1,0:T(8,128)}, f32[4,192,384]{2,1,0:T(8,128)}) custom-call(s32[27,3072]{1,0:T(8,128)} %subtract_select_fusion.refs_0_, bf16[384,3584]{1,0:T(8,128)(2,1)} %copy-done, bf16[27,192,384]{2,1,0:T(8,128)(2,1)} %refs_2_.9, bf16[192,3072]{1,0:T(8,128)(2,1)} %refs_3_.9, ...), custom_call_target="tpu_custom_call", output_to_operand_aliasing={{0}: (4, {})} | custom-call | tf_op jit(solution)/shard_map/pallas_call | solution.py:88
  501.3 93.4 %all-reduce.13.cloned.1.call-done = f32[5,192,384]{2,1,0:T(8,128)} async-done(((f32[5,192,384]{2,1,0:T(8,128)}), f32[5,192,384]{2,1,0:T(8,128)}) %all-reduce.13.cloned.1.call-update) | async-done | bytes 1474576 | tf_op jit(solution)/shard_map/psum | solution.py:137
  594.7 0.0 all-reduce.15.cloned.1.call-update
  594.7 0.0 all-reduce.17.cloned.1.call-start
  594.8 0.0 copy-start.2
  594.8 22.9 %shard_map.90 = (bf16[192,3072]{1,0:T(8,128)(2,1)}, f32[2,192,384]{2,1,0:T(8,128)}) custom-call(s32[27,3072]{1,0:T(8,128)} %subtract_select_fusion.refs_0_, bf16[384,3584]{1,0:T(8,128)(2,1)} %copy-done, bf16[27,192,384]{2,1,0:T(8,128)(2,1)} %refs_2_.9, bf16[192,3072]{1,0:T(8,128)(2,1)} %refs_3_.9, f32[192,3072]{1,0:T(8,128)} %get-tuple-element.19.refs_4_), custom_call_target="tpu_custom_call" | custom-call | tf_op jit(solution)/shard_map/pallas_call | solution.py:88
  617.6 110.6 %all-reduce.15.cloned.1.call-done = f32[4,192,384]{2,1,0:T(8,128)} async-done(((f32[4,192,384]{2,1,0:T(8,128)}), f32[4,192,384]{2,1,0:T(8,128)}) %all-reduce.15.cloned.1.call-update) | async-done | bytes 1179664 | tf_op jit(solution)/shard_map/psum | solution.py:137
  728.3 0.0 all-reduce.17.cloned.1.call-update
  728.3 0.0 copy-done.2
  728.3 0.0 copy-start.3
  728.3 1.7 constant_dynamic-update-slice_fusion.7
  730.0 0.8 copy-done.3
  730.9 0.0 copy-start.4
  730.9 1.4 constant_dynamic-update-slice_fusion.6
  732.3 0.6 copy-done.4
  732.9 1.2 constant_dynamic-update-slice_fusion.5
  734.1 0.6 copy-done.5
  734.7 1.1 constant_dynamic-update-slice_fusion.4
  735.8 123.2 %all-reduce.17.cloned.1.call-done = f32[2,192,384]{2,1,0:T(8,128)} async-done(((f32[2,192,384]{2,1,0:T(8,128)}), f32[2,192,384]{2,1,0:T(8,128)}) %all-reduce.17.cloned.1.call-update) | async-done | bytes 589840 | tf_op jit(solution)/shard_map/psum | solution.py:137
  859.0 1.9 constant_dynamic-update-slice_fusion.3
  (5 shorter events, 0.0 us)
Async XLA Ops:
  7.2 64.4 %copy-start.1 = (bf16[192,3072]{1,0:T(8,128)(2,1)S(1)}, bf16[192,3072]{1,0:T(8,128)(2,1)}, u32[]{:S(2)}) copy-start(bf16[192,3072]{1,0:T(8,128)(2,1)} %param.7) | copy-start | bytes 3538948
  7.2 63.7 %copy-start.8 = (f32[192]{0:T(256)S(1)}, f32[192]{0:T(256)}, u32[]{:S(2)}) copy-start(f32[192]{0:T(256)} %param.8) | copy-start | bytes 2308
  7.2 64.4 %copy-start.7 = (f32[192]{0:T(256)S(1)}, f32[192]{0:T(256)}, u32[]{:S(2)}) copy-start(f32[192]{0:T(256)} %param.9) | copy-start | bytes 2308
  7.2 78.1 %all-gather.2.cloned.1.call-start = ((), (), s32[]{:S(2)}) async-start(), calls=%async_computation | async-start | bytes 3538944 | tf_op jit(solution)/shard_map/all_gather | solution.py:123
  47.6 42.3 %copy-start.6 = (s32[27,3072]{1,0:T(8,128)S(1)}, s32[27,3072]{1,0:T(8,128)}, u32[]{:S(2)}) copy-start(s32[27,3072]{1,0:T(8,128)} %param.11) | copy-start | bytes 995332
  73.4 251.9 %all-reduce.9.cloned.1.call-start = ((), (), s32[]{:S(2)}) async-start(), calls=%async_computation.1 | async-start | bytes 5308416 | tf_op jit(solution)/shard_map/psum | solution.py:137
  86.4 8.1 collective-permute-start
  90.7 8.7 %collective-permute-start.1 = (bf16[384,256]{1,0:T(8,128)(2,1)S(1)}, bf16[384,256]{1,0:T(8,128)(2,1)S(1)}, u32[]{:S(2)}, u32[]{:S(2)}) collective-permute-start(bf16[384,256]{1,0:T(8,128)(2,1)S(1)} %get-tuple-element.36), channel_id=1, source_target_pairs={{2,0},{4,2},{6,4},{8,6},{10,8},{12,10},{14,12},{16,14},{18,16},{20... | collective-permute-start | bytes 589832 | tf_op jit(solution)/shard_map/ppermute | solution.py:31
  99.4 1.5 copy-start
  185.6 275.1 %all-reduce.11.cloned.1.call-start = ((), (), s32[]{:S(2)}) async-start(), calls=%async_computation.2 | async-start | bytes 4128768 | tf_op jit(solution)/shard_map/psum | solution.py:137
  325.3 269.4 %all-reduce.13.cloned.1.call-start = ((), (), s32[]{:S(2)}) async-start(), calls=%async_computation.3 | async-start | bytes 2949120 | tf_op jit(solution)/shard_map/psum | solution.py:137
  460.7 267.6 %all-reduce.15.cloned.1.call-start = ((), (), s32[]{:S(2)}) async-start(), calls=%async_computation.4 | async-start | bytes 2359296 | tf_op jit(solution)/shard_map/psum | solution.py:137
  594.7 264.3 %all-reduce.17.cloned.1.call-start = ((), (), s32[]{:S(2)}) async-start(), calls=%async_computation.5 | async-start | bytes 1179648 | tf_op jit(solution)/shard_map/psum | solution.py:137
  594.8 133.6 %copy-start.2 = (f32[9,192,384]{2,1,0:T(8,128)S(1)}, f32[9,192,384]{2,1,0:T(8,128)}, u32[]{:S(2)}) copy-start(f32[9,192,384]{2,1,0:T(8,128)} %all-reduce.9.cloned.1.call-done) | copy-start | bytes 7962628
  728.3 2.5 copy-start.3
  730.9 2.1 copy-start.4
  732.9 1.8 copy-start.5
Sparse Core Ops, SparseCore 0:
  73.5 11.7 all-gather.1
  185.7 139.5 all-reduce.8
  330.1 130.4 all-reduce.10
  465.3 129.3 all-reduce.12
  599.2 128.9 all-reduce.14
  732.8 126.1 all-reduce.16

commit v4 on v2

--- a/solution.py
+++ b/solution.py
@@ -41,7 +41,7 @@
 
     start = pl.multiple_of(b * BLOCK, BLOCK)
     win = act_ref[:, pl.ds(start, window)]
-    g_blk = g_ref[...]
+    g_t = jnp.transpose(g_ref[...])
     rows = lax.broadcasted_iota(jnp.int32, (window, BLOCK), 0)
 
     def step(k, acc):
@@ -49,12 +49,10 @@
         onehot = jnp.where(rows == idx, 1.0, 0.0).astype(jnp.bfloat16)
         picked = jnp.dot(win, onehot, preferred_element_type=jnp.float32).astype(jnp.bfloat16)
         acc = acc + jnp.dot(w_ref[k], picked, preferred_element_type=jnp.float32)
-        kg_ref[k] += lax.dot_general(
-            g_blk, picked, (((1,), (1,)), ((), ())), preferred_element_type=jnp.float32
-        )
+        kg_ref[k] += jnp.dot(picked, g_t, preferred_element_type=jnp.float32)
         return acc
 
-    acc = lax.fori_loop(0, offsets, step, jnp.zeros(out_ref.shape, jnp.float32))
+    acc = lax.fori_loop(0, offsets, step, jnp.zeros(out_ref.shape, jnp.float32), unroll=True)
     out_ref[...] = acc.astype(out_ref.dtype)
 
 
@@ -74,11 +72,11 @@
         ],
         out_specs=[
             pl.BlockSpec((o_ch, BLOCK), lambda b: (0, b)),
-            pl.BlockSpec((offsets, o_ch, c_all), lambda b: (0, 0, 0)),
+            pl.BlockSpec((offsets, c_all, o_ch), lambda b: (0, 0, 0)),
         ],
         out_shape=[
             jax.ShapeDtypeStruct((o_ch, columns), jnp.bfloat16),
-            jax.ShapeDtypeStruct((offsets, o_ch, c_all), jnp.float32),
+            jax.ShapeDtypeStruct((offsets, c_all, o_ch), jnp.float32),
         ],
         compiler_params=pltpu.CompilerParams(
             dimension_semantics=("arbitrary",), vmem_limit_bytes=56 * 1024 * 1024
@@ -111,7 +109,7 @@
     block_base = (column // BLOCK) * BLOCK
     rel = jnp.where(neighbors < 0, -1, neighbors - anchor - block_base[None, :])
     conv_out, grad_parts = conv_call(rel, gathered, weights, grad_out, border)
-    kernel_grad = lax.psum(grad_parts, SUB)
+    kernel_grad = jnp.swapaxes(lax.psum(grad_parts, SUB), 1, 2)
     return (conv_out, kernel_grad)
 
 

time: 535 us -> 462 us (0.86)
  Pallas kernels: 244 us -> 159 us
  waiting for transfers between devices: 192 us -> 201 us
    pallas_call x1, Pallas kernels: 244 us -> 159 us  [conv_call(): pl.pallas_call(kern, grid=(columns // BLOCK,), in_specs=[pl.BlockSpec((of...]
    psum x1, waiting for transfers between devices: 173 us -> 183 us  [per_device(): kernel_grad = jnp.swapaxes(lax.psum(grad_parts, SUB), 1, 2)]
where the time goes in v4:
time: 462 us
  waiting for transfers between devices  201 us (44%)
  Pallas kernels  159 us (34%)
  blocking collectives  58.3 us (13%)
  between operations  14.9 us (3%)
  local copies, waits for them, and re-layouts  11.9 us (3%)
  other arithmetic  11.3 us (2%)
  starting transfers between devices  5.04 us (1%)
    psum x1, waiting for transfers between devices, per_device(): kernel_grad = jnp.swapaxes(lax.psum(grad_parts, SUB), 1, 2)  183 us
    pallas_call x1, Pallas kernels, conv_call(): pl.pallas_call(kern, grid=(columns // BLOCK,), in_specs=[pl.BlockSpec((of...  159 us
    psum x6, blocking collectives, region_sum(): x = lax.psum(x, axis)  58.3 us
    all_gather x1, waiting for transfers between devices, per_device(): own_chans = lax.all_gather(normed, 'chan', axis=0, tiled=True)  11.9 us
    unnamed x9, local copies, waits for them, and re-layouts  10.8 us
  transfers between devices with their start and end apart: 4, of which 4 were waited for; matrix products, arithmetic and copies ran while one was open for 0% of the time, Pallas kernels for 0%

profile of v4, /device:TPU:0, one launch (start us, length us, event | category | flops | bytes accessed | tf_op | source)
XLA Modules:
  0.0 461.7 jit_solution(542804341031539386)
XLA Ops:
  7.2 0.0 copy-start
  7.2 0.0 copy-start.3
  7.2 0.0 copy-start.2
  7.2 0.0 all-gather.2.cloned.1.call-start
  8.0 0.6 fusion.15
  8.6 1.6 fusion.8
  10.2 11.2 %all-reduce = (f32[192]{0:T(256)S(1)}, f32[]{:T(128)}) all-reduce(f32[192]{0:T(256)S(1)} %fusion.8, f32[]{:T(128)} %fusion.15), channel_id=1, replica_groups=mesh['z'=4,'y'=4,'x'=4,'chan'=2] {'x'}, use_global_device_ids=true, to_apply=%region_1.0 | all-reduce | flops 193 | bytes 1544 | tf_op jit(solution)/shard_map/psum | solution.py:18
  21.4 11.3 %all-reduce.1 = (f32[192]{0:T(256)S(1)}, f32[]{:T(128)}) all-reduce(f32[192]{0:T(256)S(1)} %get-tuple-element.8, f32[]{:T(128)} %get-tuple-element.9), channel_id=1, replica_groups=mesh['z'=4,'y'=4,'x'=4,'chan'=2] {'y'}, use_global_device_ids=true, to_apply=%region_2.0 | all-reduce | flops 193 | bytes 1544 | tf_op jit(solution)/shard_map/psum | solution.py:18
  32.8 12.4 %all-reduce.2 = (f32[192]{0:T(256)S(1)}, f32[]{:T(128)}) all-reduce(f32[192]{0:T(256)S(1)} %get-tuple-element.10, f32[]{:T(128)} %get-tuple-element.11), channel_id=1, replica_groups=mesh['z'=4,'y'=4,'x'=4,'chan'=2] {'z'}, use_global_device_ids=true, to_apply=%region_3.0 | all-reduce | flops 193 | bytes 1544 | tf_op jit(solution)/shard_map/psum | solution.py:18
  45.1 0.6 broadcast_divide_fusion
  45.8 1.8 fusion.3
  47.6 0.0 copy-start.1
  47.6 7.9 %psum.76 = f32[192]{0:T(256)S(1)} all-reduce(f32[192]{0:T(256)S(1)} %fusion.3), channel_id=1, replica_groups=mesh['z'=4,'y'=4,'x'=4,'chan'=2] {'x'}, use_global_device_ids=true, to_apply=%region_9.0 | all-reduce | flops 192 | bytes 1536 | tf_op jit(solution)/shard_map/psum | solution.py:18
  55.5 7.7 %psum.77 = f32[192]{0:T(256)S(1)} all-reduce(f32[192]{0:T(256)S(1)} %psum.76), channel_id=1, replica_groups=mesh['z'=4,'y'=4,'x'=4,'chan'=2] {'y'}, use_global_device_ids=true, to_apply=%region_10.0 | all-reduce | flops 192 | bytes 1536 | tf_op jit(solution)/shard_map/psum | solution.py:18
  63.2 7.7 %psum.78 = f32[192]{0:T(256)S(1)} all-reduce(f32[192]{0:T(256)S(1)} %psum.77), channel_id=1, replica_groups=mesh['z'=4,'y'=4,'x'=4,'chan'=2] {'z'}, use_global_device_ids=true, to_apply=%region_11.0 | all-reduce | flops 192 | bytes 1536 | tf_op jit(solution)/shard_map/psum | solution.py:18
  70.9 0.0 copy-done.3
  70.9 0.7 rsqrt_multiply_fusion
  71.6 0.0 copy-done
  71.6 0.0 copy-done.2
  71.6 1.7 fusion.7
  73.3 0.0 all-gather.2.cloned.1.call-update
  73.4 0.0 all-reduce.5.cloned.1.call-start
  73.4 11.9 %all-gather.2.cloned.1.call-done = bf16[384,3072]{1,0:T(8,128)(2,1)} async-done(((bf16[192,3072]{1,0:T(8,128)(2,1)}), bf16[384,3072]{1,0:T(8,128)(2,1)}) %all-gather.2.cloned.1.call-update) | async-done | bytes 2359312 | tf_op jit(solution)/shard_map/all_gather | solution.py:106
  85.3 1.1 fusion.16
  86.4 3.5 collective-permute-start
  89.9 1.5 collective-permute-start.1
  91.3 0.0 copy-done.1
  91.3 0.8 subtract_select_fusion.rel_ref
  92.2 2.3 collective-permute-done
  94.4 4.1 collective-permute-done.1
  98.6 3.4 pad_maximum_fusion.act_ref
  102.0 159.2 %shard_map.86 = (bf16[192,3072]{1,0:T(8,128)(2,1)}, f32[27,384,192]{2,1,0:T(8,128)}) custom-call(s32[27,3072]{1,0:T(8,128)} %subtract_select_fusion.rel_ref, bf16[384,3584]{1,0:T(8,128)(2,1)} %pad_maximum_fusion.act_ref, bf16[27,192,384]{2,1,0:T(8,128)(2,1)} %w_ref.1, bf16[192,3072]{1,0:T(8,128)(2,1)} %g_ref.1), custom_call_target="tpu_custom_call" | custom-call | tf_op jit(solution)/shard_map/pallas_call | solution.py:64
  261.2 0.0 all-reduce.5.cloned.1.call-update
  261.2 182.8 %all-reduce.5.cloned.1.call-done = f32[27,192,384]{1,2,0:T(8,128)} async-done(((f32[27,192,384]{1,2,0:T(8,128)}), f32[27,192,384]{1,2,0:T(8,128)}) %all-reduce.5.cloned.1.call-update) | async-done | bytes 7962640 | tf_op jit(solution)/shard_map/psum | solution.py:112
  444.0 10.8 %copy.9 = f32[27,192,384]{2,1,0:T(8,128)} copy(f32[27,192,384]{1,2,0:T(8,128)} %all-reduce.5.cloned.1.call-done) | data formatting | bytes 15925248
  (2 shorter events, 0.0 us)
Async XLA Ops:
  7.2 64.4 %copy-start = (bf16[192,3072]{1,0:T(8,128)(2,1)S(1)}, bf16[192,3072]{1,0:T(8,128)(2,1)}, u32[]{:S(2)}) copy-start(bf16[192,3072]{1,0:T(8,128)(2,1)} %param.7) | copy-start | bytes 3538948
  7.2 63.7 %copy-start.3 = (f32[192]{0:T(256)S(1)}, f32[192]{0:T(256)}, u32[]{:S(2)}) copy-start(f32[192]{0:T(256)} %param.8) | copy-start | bytes 2308
  7.2 64.4 %copy-start.2 = (f32[192]{0:T(256)S(1)}, f32[192]{0:T(256)}, u32[]{:S(2)}) copy-start(f32[192]{0:T(256)} %param.9) | copy-start | bytes 2308
  7.2 78.1 %all-gather.2.cloned.1.call-start = ((), (), s32[]{:S(2)}) async-start(), calls=%async_computation | async-start | bytes 3538944 | tf_op jit(solution)/shard_map/all_gather | solution.py:106
  47.6 43.8 %copy-start.1 = (s32[27,3072]{1,0:T(8,128)S(1)}, s32[27,3072]{1,0:T(8,128)}, u32[]{:S(2)}) copy-start(s32[27,3072]{1,0:T(8,128)} %param.11) | copy-start | bytes 995332
  73.4 370.7 %all-reduce.5.cloned.1.call-start = ((), (), s32[]{:S(2)}) async-start(), calls=%async_computation.1 | async-start | bytes 21233664 | tf_op jit(solution)/shard_map/psum | solution.py:112
  86.4 8.1 %collective-permute-start = (bf16[384,256]{1,0:T(8,128)(2,1)S(1)}, bf16[384,256]{1,0:T(8,128)(2,1)S(1)}, u32[]{:S(2)}, u32[]{:S(2)}) collective-permute-start(bf16[384,256]{1,0:T(8,128)(2,1)S(1)} %get-tuple-element.14), channel_id=1, source_target_pairs={{0,2},{2,4},{4,6},{6,8},{8,10},{10,12},{12,14},{14,16},{16,18},{18... | collective-permute-start | bytes 589832 | tf_op jit(solution)/shard_map/ppermute | solution.py:29
  89.9 8.7 %collective-permute-start.1 = (bf16[384,256]{1,0:T(8,128)(2,1)S(1)}, bf16[384,256]{1,0:T(8,128)(2,1)S(1)}, u32[]{:S(2)}, u32[]{:S(2)}) collective-permute-start(bf16[384,256]{1,0:T(8,128)(2,1)S(1)} %get-tuple-element.15), channel_id=1, source_target_pairs={{2,0},{4,2},{6,4},{8,6},{10,8},{12,10},{14,12},{16,14},{18,16},{20... | collective-permute-start | bytes 589832 | tf_op jit(solution)/shard_map/ppermute | solution.py:30
Sparse Core Ops, SparseCore 0:
  73.5 11.7 all-gather.1
  261.3 182.6 all-reduce.4

commit v5 on v4

--- a/solution.py
+++ b/solution.py
@@ -92,12 +92,20 @@
     live_limit = live[0] - border
     live_mask = ((column < live_limit) | (column >= columns - border)).astype(jnp.float32)
     values = features.astype(jnp.float32)
-    masked = values * live_mask[None, :]
     live_rows = jnp.sum(live_mask)
-    totals, live_total = region_sum((jnp.sum(masked, axis=1), live_rows))
-    average = totals / live_total
-    centered = (values - average[:, None]) * live_mask[None, :]
-    variance = region_sum(jnp.sum(centered * centered, axis=1)) / live_total
+    local_sum = jnp.sum(values * live_mask[None, :], axis=1)
+    local_mean = local_sum / live_rows
+    local_dev = (values - local_mean[:, None]) * live_mask[None, :]
+    local_sq = jnp.sum(local_dev * local_dev, axis=1)
+    stats = jnp.stack([local_sum, local_sq, jnp.broadcast_to(live_rows, local_sum.shape)])
+    for axis in reversed(SUB):
+        stats = lax.all_gather(stats, axis, axis=0, tiled=True)
+    stats = stats.reshape(-1, 3, channels)
+    sums, squares, counts = stats[:, 0], stats[:, 1], stats[:, 2]
+    live_total = jnp.sum(counts[:, 0])
+    average = jnp.sum(sums, axis=0) / live_total
+    spread = sums / counts - average[None, :]
+    variance = (jnp.sum(squares, axis=0) + jnp.sum(counts * spread * spread, axis=0)) / live_total
     factor = gain * lax.rsqrt(variance + 1e-05)
     normed = (
         jnp.maximum((values - average[:, None]) * factor[:, None] + bias[:, None], 0.0)

time: 462 us -> 446 us (0.965)
  blocking collectives: 58.3 us -> 38.2 us
    psum x6 -> x0, blocking collectives: 58.3 us -> none  [region_sum(): x = lax.psum(x, axis)]
    all_gather x0 -> x3, blocking collectives: none -> 38.2 us  [per_device(): stats = lax.all_gather(stats, axis, axis=0, tiled=True)]
    unnamed x9 -> x12, local copies, waits for them, and re-layouts: 10.8 us -> 10.9 us
where the time goes in v5:
time: 446 us
  waiting for transfers between devices  203 us (46%)
  Pallas kernels  159 us (36%)
  blocking collectives  38.2 us (9%)
  between operations  14.9 us (3%)
  other arithmetic  12.8 us (3%)
  local copies, waits for them, and re-layouts  12.7 us (3%)
  starting transfers between devices  5.04 us (1%)
    psum x1, waiting for transfers between devices, per_device(): kernel_grad = jnp.swapaxes(lax.psum(grad_parts, SUB), 1, 2)  183 us
    pallas_call x1, Pallas kernels, conv_call(): pl.pallas_call(kern, grid=(columns // BLOCK,), in_specs=[pl.BlockSpec((of...  159 us
    all_gather x3, blocking collectives, per_device(): stats = lax.all_gather(stats, axis, axis=0, tiled=True)  38.2 us
    all_gather x1, waiting for transfers between devices, per_device(): own_chans = lax.all_gather(normed, 'chan', axis=0, tiled=True)  13.6 us
    unnamed x12, local copies, waits for them, and re-layouts  10.9 us
  transfers between devices with their start and end apart: 4, of which 4 were waited for; matrix products, arithmetic and copies ran while one was open for 0% of the time, Pallas kernels for 0%

profile of v5, /device:TPU:0, one launch (start us, length us, event | category | flops | bytes accessed | tf_op | source)
XLA Modules:
  0.0 445.9 jit_solution(8614909230916220352)
XLA Ops:
  7.2 0.0 copy-start
  7.2 0.0 copy-start.3
  7.2 0.0 copy-start.2
  7.2 0.0 all-gather.4.cloned.1.call-start
  8.0 0.6 fusion.18
  8.6 1.6 fusion
  10.2 0.7 broadcast_divide_fusion.1
  10.8 1.8 fusion.3
  12.6 0.7 pad.5.clone
  13.3 0.1 maximum_bitcast_fusion
  13.4 12.5 %all-gather = f32[4,3,192]{2,1,0:T(4,128)S(1)} all-gather(f32[1,3,192]{2,1,0:T(4,128)S(1)} %maximum_bitcast_fusion), channel_id=1, replica_groups=mesh['z'=4,'y'=4,'x'=4,'chan'=2] {'x'}, dimensions={0}, use_global_device_ids=true | all-gather | bytes 11520 | tf_op jit(solution)/shard_map/all_gather | solution.py:102
  25.9 12.4 %all-gather.1 = f32[4,12,192]{2,1,0:T(8,128)S(1)} all-gather(f32[1,12,192]{2,1,0:T(8,128)S(1)} %reshape.45), channel_id=1, replica_groups=mesh['z'=4,'y'=4,'x'=4,'chan'=2] {'y'}, dimensions={0}, use_global_device_ids=true | all-gather | bytes 46080 | tf_op jit(solution)/shard_map/all_gather | solution.py:102
  38.3 13.3 %all_gather.14 = f32[192,192]{1,0:T(8,128)S(1)} all-gather(f32[48,192]{1,0:T(8,128)S(1)} %reshape.46), channel_id=1, replica_groups=mesh['z'=4,'y'=4,'x'=4,'chan'=2] {'z'}, dimensions={0}, use_global_device_ids=true | all-gather | bytes 184320 | tf_op jit(solution)/shard_map/all_gather | solution.py:102
  51.6 0.1 reshape.42
  51.7 0.2 slice_reduce_fusion.2
  51.9 0.0 copy-start.1
  51.9 0.6 slice_reduce_fusion.1
  52.5 0.6 broadcast_divide_fusion
  53.2 0.0 copy-done.3
  53.2 0.7 rsqrt_multiply_fusion
  53.9 0.0 copy-done
  53.9 0.0 copy-done.2
  53.9 1.7 fusion.8
  55.7 0.0 all-gather.4.cloned.1.call-update
  55.7 0.0 all-reduce.2.cloned.1.call-start
  55.7 13.6 %all-gather.4.cloned.1.call-done = bf16[384,3072]{1,0:T(8,128)(2,1)} async-done(((bf16[192,3072]{1,0:T(8,128)(2,1)}), bf16[384,3072]{1,0:T(8,128)(2,1)}) %all-gather.4.cloned.1.call-update) | async-done | bytes 2359312 | tf_op jit(solution)/shard_map/all_gather | solution.py:114
  69.3 1.1 fusion.19
  70.4 3.5 collective-permute-start
  73.9 1.5 collective-permute-start.1
  75.3 0.0 copy-done.1
  75.4 0.8 subtract_select_fusion.rel_ref
  76.2 2.3 collective-permute-done
  78.5 4.1 collective-permute-done.1
  82.6 3.4 pad_maximum_fusion.act_ref
  86.0 159.2 %shard_map.86 = (bf16[192,3072]{1,0:T(8,128)(2,1)}, f32[27,384,192]{2,1,0:T(8,128)}) custom-call(s32[27,3072]{1,0:T(8,128)} %subtract_select_fusion.rel_ref, bf16[384,3584]{1,0:T(8,128)(2,1)} %pad_maximum_fusion.act_ref, bf16[27,192,384]{2,1,0:T(8,128)(2,1)} %w_ref.1, bf16[192,3072]{1,0:T(8,128)(2,1)} %g_ref.1), custom_call_target="tpu_custom_call" | custom-call | tf_op jit(solution)/shard_map/pallas_call | solution.py:64
  245.2 0.0 all-reduce.2.cloned.1.call-update
  245.2 183.0 %all-reduce.2.cloned.1.call-done = f32[27,192,384]{1,2,0:T(8,128)} async-done(((f32[27,192,384]{1,2,0:T(8,128)}), f32[27,192,384]{1,2,0:T(8,128)}) %all-reduce.2.cloned.1.call-update) | async-done | bytes 7962640 | tf_op jit(solution)/shard_map/psum | solution.py:120
  428.3 10.8 %copy.14 = f32[27,192,384]{2,1,0:T(8,128)} copy(f32[27,192,384]{1,2,0:T(8,128)} %all-reduce.2.cloned.1.call-done) | data formatting | bytes 15925248
  (6 shorter events, 0.1 us)
Async XLA Ops:
  7.2 46.7 %copy-start = (bf16[192,3072]{1,0:T(8,128)(2,1)S(1)}, bf16[192,3072]{1,0:T(8,128)(2,1)}, u32[]{:S(2)}) copy-start(bf16[192,3072]{1,0:T(8,128)(2,1)} %param.7) | copy-start | bytes 3538948
  7.2 46.1 %copy-start.3 = (f32[192]{0:T(256)S(1)}, f32[192]{0:T(256)}, u32[]{:S(2)}) copy-start(f32[192]{0:T(256)} %param.8) | copy-start | bytes 2308
  7.2 46.7 %copy-start.2 = (f32[192]{0:T(256)S(1)}, f32[192]{0:T(256)}, u32[]{:S(2)}) copy-start(f32[192]{0:T(256)} %param.9) | copy-start | bytes 2308
  7.2 62.1 %all-gather.4.cloned.1.call-start = ((), (), s32[]{:S(2)}) async-start(), calls=%async_computation | async-start | bytes 3538944 | tf_op jit(solution)/shard_map/all_gather | solution.py:114
  51.9 23.4 %copy-start.1 = (s32[27,3072]{1,0:T(8,128)S(1)}, s32[27,3072]{1,0:T(8,128)}, u32[]{:S(2)}) copy-start(s32[27,3072]{1,0:T(8,128)} %param.11) | copy-start | bytes 995332
  55.7 372.6 %all-reduce.2.cloned.1.call-start = ((), (), s32[]{:S(2)}) async-start(), calls=%async_computation.1 | async-start | bytes 21233664 | tf_op jit(solution)/shard_map/psum | solution.py:120
  70.4 8.1 %collective-permute-start = (bf16[384,256]{1,0:T(8,128)(2,1)S(1)}, bf16[384,256]{1,0:T(8,128)(2,1)S(1)}, u32[]{:S(2)}, u32[]{:S(2)}) collective-permute-start(bf16[384,256]{1,0:T(8,128)(2,1)S(1)} %get-tuple-element.14), channel_id=1, source_target_pairs={{0,2},{2,4},{4,6},{6,8},{8,10},{10,12},{12,14},{14,16},{16,18},{18... | collective-permute-start | bytes 589832 | tf_op jit(solution)/shard_map/ppermute | solution.py:29
  73.9 8.7 %collective-permute-start.1 = (bf16[384,256]{1,0:T(8,128)(2,1)S(1)}, bf16[384,256]{1,0:T(8,128)(2,1)S(1)}, u32[]{:S(2)}, u32[]{:S(2)}) collective-permute-start(bf16[384,256]{1,0:T(8,128)(2,1)S(1)} %get-tuple-element.15), channel_id=1, source_target_pairs={{2,0},{4,2},{6,4},{8,6},{10,8},{12,10},{14,12},{16,14},{18,16},{20... | collective-permute-start | bytes 589832 | tf_op jit(solution)/shard_map/ppermute | solution.py:30
Sparse Core Ops, SparseCore 0:
  55.8 13.4 all-gather.3
  245.4 182.8 all-reduce.1

commit v6 on v5

--- a/solution.py
+++ b/solution.py
@@ -31,52 +31,61 @@
     return jnp.concatenate([before, x, after], axis=1)
 
 
-def conv_kernel(rel_ref, act_ref, w_ref, g_ref, out_ref, kg_ref, *, halo, offsets):
-    b = pl.program_id(0)
+def offset_kernel(rel_ref, act_ref, w_ref, g_ref, out_ref, kg_ref, picked_ref, acc_ref, *, halo, blocks):
+    k = pl.program_id(0)
     window = BLOCK + 2 * halo
+    rows = lax.broadcasted_iota(jnp.int32, (window, BLOCK), 0)
+    for b in range(blocks):
+        idx = rel_ref[pl.ds(k, 1), pl.ds(b * BLOCK, BLOCK)]
+        onehot = jnp.where(rows == idx, 1.0, 0.0).astype(jnp.bfloat16)
+        win = act_ref[:, pl.ds(b * BLOCK, window)]
+        picked_ref[:, pl.ds(b * BLOCK, BLOCK)] = jnp.dot(
+            win, onehot, preferred_element_type=jnp.float32
+        ).astype(jnp.bfloat16)
+    picked = picked_ref[...]
+    kg_ref[0] = lax.dot_general(
+        g_ref[...], picked, (((1,), (1,)), ((), ())), preferred_element_type=jnp.float32
+    )
+    part = jnp.dot(w_ref[0], picked, preferred_element_type=jnp.float32)
 
-    @pl.when(b == 0)
+    @pl.when(k == 0)
     def _():
-        kg_ref[...] = jnp.zeros_like(kg_ref)
+        acc_ref[...] = part
 
-    start = pl.multiple_of(b * BLOCK, BLOCK)
-    win = act_ref[:, pl.ds(start, window)]
-    g_t = jnp.transpose(g_ref[...])
-    rows = lax.broadcasted_iota(jnp.int32, (window, BLOCK), 0)
+    @pl.when(k > 0)
+    def _():
+        acc_ref[...] += part
 
-    def step(k, acc):
-        idx = rel_ref[pl.ds(k, 1), :]
-        onehot = jnp.where(rows == idx, 1.0, 0.0).astype(jnp.bfloat16)
-        picked = jnp.dot(win, onehot, preferred_element_type=jnp.float32).astype(jnp.bfloat16)
-        acc = acc + jnp.dot(w_ref[k], picked, preferred_element_type=jnp.float32)
-        kg_ref[k] += jnp.dot(picked, g_t, preferred_element_type=jnp.float32)
-        return acc
-
-    acc = lax.fori_loop(0, offsets, step, jnp.zeros(out_ref.shape, jnp.float32), unroll=True)
-    out_ref[...] = acc.astype(out_ref.dtype)
+    @pl.when(k == pl.num_programs(0) - 1)
+    def _():
+        out_ref[...] = acc_ref[...].astype(out_ref.dtype)
 
 
 def conv_call(rel, act, weights, grad_out, halo):
     offsets, o_ch, c_all = weights.shape
-    columns = grad_out.shape[1]
+    columns = rel.shape[1]
     extent = act.shape[1]
-    kern = functools.partial(conv_kernel, halo=halo, offsets=offsets)
+    kern = functools.partial(offset_kernel, halo=halo, blocks=columns // BLOCK)
     return pl.pallas_call(
         kern,
-        grid=(columns // BLOCK,),
+        grid=(offsets,),
         in_specs=[
-            pl.BlockSpec((offsets, BLOCK), lambda b: (0, b)),
-            pl.BlockSpec((c_all, extent), lambda b: (0, 0)),
-            pl.BlockSpec((offsets, o_ch, c_all), lambda b: (0, 0, 0)),
-            pl.BlockSpec((o_ch, BLOCK), lambda b: (0, b)),
+            pl.BlockSpec((offsets, columns), lambda k: (0, 0)),
+            pl.BlockSpec((c_all, extent), lambda k: (0, 0)),
+            pl.BlockSpec((1, o_ch, c_all), lambda k: (k, 0, 0)),
+            pl.BlockSpec((o_ch, columns), lambda k: (0, 0)),
         ],
         out_specs=[
-            pl.BlockSpec((o_ch, BLOCK), lambda b: (0, b)),
-            pl.BlockSpec((offsets, c_all, o_ch), lambda b: (0, 0, 0)),
+            pl.BlockSpec((o_ch, columns), lambda k: (0, 0)),
+            pl.BlockSpec((1, o_ch, c_all), lambda k: (k, 0, 0)),
         ],
         out_shape=[
             jax.ShapeDtypeStruct((o_ch, columns), jnp.bfloat16),
-            jax.ShapeDtypeStruct((offsets, c_all, o_ch), jnp.float32),
+            jax.ShapeDtypeStruct((offsets, o_ch, c_all), jnp.float32),
+        ],
+        scratch_shapes=[
+            pltpu.VMEM((c_all, columns), jnp.bfloat16),
+            pltpu.VMEM((o_ch, columns), jnp.float32),
         ],
         compiler_params=pltpu.CompilerParams(
             dimension_semantics=("arbitrary",), vmem_limit_bytes=56 * 1024 * 1024
@@ -117,7 +126,7 @@
     block_base = (column // BLOCK) * BLOCK
     rel = jnp.where(neighbors < 0, -1, neighbors - anchor - block_base[None, :])
     conv_out, grad_parts = conv_call(rel, gathered, weights, grad_out, border)
-    kernel_grad = jnp.swapaxes(lax.psum(grad_parts, SUB), 1, 2)
+    kernel_grad = lax.psum(grad_parts, SUB)
     return (conv_out, kernel_grad)
 
 

time: 446 us -> 377 us (0.85)
  Pallas kernels: 159 us -> 103 us
  waiting for transfers between devices: 203 us -> 194 us
    pallas_call x1, Pallas kernels: 159 us -> 103 us  [conv_call(): pl.pallas_call(kern, grid=(offsets,), in_specs=[pl.BlockSpec((offsets, co...]
    psum x1, waiting for transfers between devices: 183 us -> 173 us  [per_device(): kernel_grad = lax.psum(grad_parts, SUB)]
where the time goes in v6:
time: 377 us
  waiting for transfers between devices  194 us (51%)
  Pallas kernels  103 us (27%)
  blocking collectives  38.2 us (10%)
  between operations  14.9 us (4%)
  other arithmetic  12.8 us (3%)
  local copies, waits for them, and re-layouts  9.27 us (2%)
  starting transfers between devices  4.86 us (1%)
    psum x1, waiting for transfers between devices, per_device(): kernel_grad = lax.psum(grad_parts, SUB)  173 us
    pallas_call x1, Pallas kernels, conv_call(): pl.pallas_call(kern, grid=(offsets,), in_specs=[pl.BlockSpec((offsets, co...  103 us
    all_gather x3, blocking collectives, per_device(): stats = lax.all_gather(stats, axis, axis=0, tiled=True)  38.2 us
    all_gather x1, waiting for transfers between devices, per_device(): own_chans = lax.all_gather(normed, 'chan', axis=0, tiled=True)  13.6 us
  transfers between devices with their start and end apart: 4, of which 4 were waited for; matrix products, arithmetic and copies ran while one was open for 0% of the time, Pallas kernels for 0%

profile of v6, /device:TPU:0, one launch (start us, length us, event | category | flops | bytes accessed | tf_op | source)
XLA Modules:
  0.0 376.9 jit_solution(3198424804926372917)
XLA Ops:
  7.2 0.0 copy-start
  7.2 0.0 copy-start.3
  7.2 0.0 copy-start.2
  7.2 0.0 all-gather.4.cloned.1.call-start
  8.0 0.6 fusion.18
  8.6 1.6 fusion
  10.2 0.7 broadcast_divide_fusion.1
  10.8 1.8 fusion.3
  12.6 0.7 pad.5.clone
  13.3 0.1 maximum_bitcast_fusion
  13.4 12.5 %all-gather = f32[4,3,192]{2,1,0:T(4,128)S(1)} all-gather(f32[1,3,192]{2,1,0:T(4,128)S(1)} %maximum_bitcast_fusion), channel_id=1, replica_groups=mesh['z'=4,'y'=4,'x'=4,'chan'=2] {'x'}, dimensions={0}, use_global_device_ids=true | all-gather | bytes 11520 | tf_op jit(solution)/shard_map/all_gather | solution.py:111
  25.9 12.4 %all-gather.1 = f32[4,12,192]{2,1,0:T(8,128)S(1)} all-gather(f32[1,12,192]{2,1,0:T(8,128)S(1)} %reshape.45), channel_id=1, replica_groups=mesh['z'=4,'y'=4,'x'=4,'chan'=2] {'y'}, dimensions={0}, use_global_device_ids=true | all-gather | bytes 46080 | tf_op jit(solution)/shard_map/all_gather | solution.py:111
  38.3 13.3 %all_gather.14 = f32[192,192]{1,0:T(8,128)S(1)} all-gather(f32[48,192]{1,0:T(8,128)S(1)} %reshape.46), channel_id=1, replica_groups=mesh['z'=4,'y'=4,'x'=4,'chan'=2] {'z'}, dimensions={0}, use_global_device_ids=true | all-gather | bytes 184320 | tf_op jit(solution)/shard_map/all_gather | solution.py:111
  51.6 0.1 reshape.42
  51.7 0.2 slice_reduce_fusion.2
  51.9 0.0 copy-start.1
  51.9 0.6 slice_reduce_fusion.1
  52.5 0.6 broadcast_divide_fusion
  53.2 0.0 copy-done.3
  53.2 0.7 rsqrt_multiply_fusion
  53.9 0.0 copy-done
  53.9 0.0 copy-done.2
  53.9 1.7 fusion.8
  55.7 0.0 all-gather.4.cloned.1.call-update
  55.7 0.0 all-reduce.2.cloned.1.call-start
  55.7 13.6 %all-gather.4.cloned.1.call-done = bf16[384,3072]{1,0:T(8,128)(2,1)} async-done(((bf16[192,3072]{1,0:T(8,128)(2,1)}), bf16[384,3072]{1,0:T(8,128)(2,1)}) %all-gather.4.cloned.1.call-update) | async-done | bytes 2359312 | tf_op jit(solution)/shard_map/all_gather | solution.py:123
  69.3 1.1 fusion.19
  70.4 3.5 collective-permute-start
  73.9 1.3 collective-permute-start.1
  75.2 0.0 copy-done.1
  75.2 0.8 subtract_select_fusion.rel_ref
  76.0 2.5 collective-permute-done
  78.5 4.1 %collective-permute-done.1 = bf16[384,256]{1,0:T(8,128)(2,1)S(1)} collective-permute-done((bf16[384,256]{1,0:T(8,128)(2,1)S(1)}, bf16[384,256]{1,0:T(8,128)(2,1)S(1)}, u32[]{:S(2)}, u32[]{:S(2)}) %collective-permute-start.1) | collective-permute-done | bytes 196640 | tf_op jit(solution)/shard_map/ppermute | solution.py:30
  82.6 3.4 pad_maximum_fusion.act_ref
  86.0 103.3 %shard_map.86 = (bf16[192,3072]{1,0:T(8,128)(2,1)}, f32[27,192,384]{2,1,0:T(8,128)}) custom-call(s32[27,3072]{1,0:T(8,128)} %subtract_select_fusion.rel_ref, bf16[384,3584]{1,0:T(8,128)(2,1)} %pad_maximum_fusion.act_ref, bf16[27,192,384]{2,1,0:T(8,128)(2,1)} %w_ref.1, bf16[192,3072]{1,0:T(8,128)(2,1)} %g_ref.1), custom_call_target="tpu_custom_call" | custom-call | tf_op jit(solution)/shard_map/pallas_call | solution.py:69
  189.3 0.0 all-reduce.2.cloned.1.call-update
  189.3 173.4 %all-reduce.2.cloned.1.call-done = f32[27,192,384]{2,1,0:T(8,128)} async-done(((f32[27,192,384]{2,1,0:T(8,128)}), f32[27,192,384]{2,1,0:T(8,128)}) %all-reduce.2.cloned.1.call-update) | async-done | bytes 7962640 | tf_op jit(solution)/shard_map/psum | solution.py:129
  362.7 7.4 %copy.28 = f32[27,192,384]{2,1,0:T(8,128)} copy(f32[27,192,384]{2,1,0:T(8,128)} %all-reduce.2.cloned.1.call-done) | data formatting | bytes 15925248
  (6 shorter events, 0.1 us)
Async XLA Ops:
  7.2 46.7 %copy-start = (bf16[192,3072]{1,0:T(8,128)(2,1)S(1)}, bf16[192,3072]{1,0:T(8,128)(2,1)}, u32[]{:S(2)}) copy-start(bf16[192,3072]{1,0:T(8,128)(2,1)} %param.7) | copy-start | bytes 3538948
  7.2 46.1 %copy-start.3 = (f32[192]{0:T(256)S(1)}, f32[192]{0:T(256)}, u32[]{:S(2)}) copy-start(f32[192]{0:T(256)} %param.8) | copy-start | bytes 2308
  7.2 46.7 %copy-start.2 = (f32[192]{0:T(256)S(1)}, f32[192]{0:T(256)}, u32[]{:S(2)}) copy-start(f32[192]{0:T(256)} %param.9) | copy-start | bytes 2308
  7.2 62.1 %all-gather.4.cloned.1.call-start = ((), (), s32[]{:S(2)}) async-start(), calls=%async_computation | async-start | bytes 3538944 | tf_op jit(solution)/shard_map/all_gather | solution.py:123
  51.9 23.3 %copy-start.1 = (s32[27,3072]{1,0:T(8,128)S(1)}, s32[27,3072]{1,0:T(8,128)}, u32[]{:S(2)}) copy-start(s32[27,3072]{1,0:T(8,128)} %param.11) | copy-start | bytes 995332
  55.7 307.0 %all-reduce.2.cloned.1.call-start = ((), (), s32[]{:S(2)}) async-start(), calls=%async_computation.1 | async-start | bytes 15925248 | tf_op jit(solution)/shard_map/psum | solution.py:129
  70.4 8.1 %collective-permute-start = (bf16[384,256]{1,0:T(8,128)(2,1)S(1)}, bf16[384,256]{1,0:T(8,128)(2,1)S(1)}, u32[]{:S(2)}, u32[]{:S(2)}) collective-permute-start(bf16[384,256]{1,0:T(8,128)(2,1)S(1)} %get-tuple-element.8), channel_id=1, source_target_pairs={{0,2},{2,4},{4,6},{6,8},{8,10},{10,12},{12,14},{14,16},{16,18},{18... | collective-permute-start | bytes 589832 | tf_op jit(solution)/shard_map/ppermute | solution.py:29
  73.9 8.7 %collective-permute-start.1 = (bf16[384,256]{1,0:T(8,128)(2,1)S(1)}, bf16[384,256]{1,0:T(8,128)(2,1)S(1)}, u32[]{:S(2)}, u32[]{:S(2)}) collective-permute-start(bf16[384,256]{1,0:T(8,128)(2,1)S(1)} %get-tuple-element.9), channel_id=1, source_target_pairs={{2,0},{4,2},{6,4},{8,6},{10,8},{12,10},{14,12},{16,14},{18,16},{20... | collective-permute-start | bytes 589832 | tf_op jit(solution)/shard_map/ppermute | solution.py:30
Sparse Core Ops, SparseCore 0:
  55.8 13.4 all-gather.3
  189.5 173.2 all-reduce.1

commit v7 on v6

--- a/solution.py
+++ b/solution.py
@@ -31,7 +31,7 @@
     return jnp.concatenate([before, x, after], axis=1)
 
 
-def offset_kernel(rel_ref, act_ref, w_ref, g_ref, out_ref, kg_ref, picked_ref, acc_ref, *, halo, blocks):
+def offset_kernel(rel_ref, act_ref, g_ref, picked_ref, kg_ref, *, halo, blocks):
     k = pl.program_id(0)
     window = BLOCK + 2 * halo
     rows = lax.broadcasted_iota(jnp.int32, (window, BLOCK), 0)
@@ -39,32 +39,18 @@
         idx = rel_ref[pl.ds(k, 1), pl.ds(b * BLOCK, BLOCK)]
         onehot = jnp.where(rows == idx, 1.0, 0.0).astype(jnp.bfloat16)
         win = act_ref[:, pl.ds(b * BLOCK, window)]
-        picked_ref[:, pl.ds(b * BLOCK, BLOCK)] = jnp.dot(
+        picked_ref[0, :, pl.ds(b * BLOCK, BLOCK)] = jnp.dot(
             win, onehot, preferred_element_type=jnp.float32
         ).astype(jnp.bfloat16)
-    picked = picked_ref[...]
     kg_ref[0] = lax.dot_general(
-        g_ref[...], picked, (((1,), (1,)), ((), ())), preferred_element_type=jnp.float32
+        g_ref[...], picked_ref[0], (((1,), (1,)), ((), ())), preferred_element_type=jnp.float32
     )
-    part = jnp.dot(w_ref[0], picked, preferred_element_type=jnp.float32)
-
-    @pl.when(k == 0)
-    def _():
-        acc_ref[...] = part
-
-    @pl.when(k > 0)
-    def _():
-        acc_ref[...] += part
-
-    @pl.when(k == pl.num_programs(0) - 1)
-    def _():
-        out_ref[...] = acc_ref[...].astype(out_ref.dtype)
 
 
-def conv_call(rel, act, weights, grad_out, halo):
-    offsets, o_ch, c_all = weights.shape
-    columns = rel.shape[1]
-    extent = act.shape[1]
+def gather_call(rel, act, grad_out, halo):
+    offsets, columns = rel.shape
+    c_all, extent = act.shape
+    o_ch = grad_out.shape[0]
     kern = functools.partial(offset_kernel, halo=halo, blocks=columns // BLOCK)
     return pl.pallas_call(
         kern,
@@ -72,25 +58,20 @@
         in_specs=[
             pl.BlockSpec((offsets, columns), lambda k: (0, 0)),
             pl.BlockSpec((c_all, extent), lambda k: (0, 0)),
-            pl.BlockSpec((1, o_ch, c_all), lambda k: (k, 0, 0)),
             pl.BlockSpec((o_ch, columns), lambda k: (0, 0)),
         ],
         out_specs=[
-            pl.BlockSpec((o_ch, columns), lambda k: (0, 0)),
+            pl.BlockSpec((1, c_all, columns), lambda k: (k, 0, 0)),
             pl.BlockSpec((1, o_ch, c_all), lambda k: (k, 0, 0)),
         ],
         out_shape=[
-            jax.ShapeDtypeStruct((o_ch, columns), jnp.bfloat16),
+            jax.ShapeDtypeStruct((offsets, c_all, columns), jnp.bfloat16),
             jax.ShapeDtypeStruct((offsets, o_ch, c_all), jnp.float32),
-        ],
-        scratch_shapes=[
-            pltpu.VMEM((c_all, columns), jnp.bfloat16),
-            pltpu.VMEM((o_ch, columns), jnp.float32),
         ],
         compiler_params=pltpu.CompilerParams(
             dimension_semantics=("arbitrary",), vmem_limit_bytes=56 * 1024 * 1024
         ),
-    )(rel, act, weights, grad_out)
+    )(rel, act, grad_out)
 
 
 def per_device(features, gain, bias, live, neighbors, weights, grad_out):
@@ -125,8 +106,11 @@
     anchor = region_idx * columns - border
     block_base = (column // BLOCK) * BLOCK
     rel = jnp.where(neighbors < 0, -1, neighbors - anchor - block_base[None, :])
-    conv_out, grad_parts = conv_call(rel, gathered, weights, grad_out, border)
+    picked, grad_parts = gather_call(rel, gathered, grad_out, border)
     kernel_grad = lax.psum(grad_parts, SUB)
+    conv_out = lax.dot_general(
+        weights, picked, (((0, 2), (0, 1)), ((), ())), preferred_element_type=jnp.float32
+    ).astype(jnp.bfloat16)
     return (conv_out, kernel_grad)
 
 

time: 377 us -> 354 us (0.939)
  waiting for transfers between devices: 194 us -> 167 us
  matrix products: 0 us -> 26.8 us
  Pallas kernels: 103 us -> 79.9 us
    dot_general x0 -> x1, matrix products: none -> 26.8 us  [per_device(): lax.dot_general(weights, picked, (((0, 2), (0, 1)), ((), ())), preferred_...]
    psum x1, waiting for transfers between devices: 173 us -> 147 us  [per_device(): kernel_grad = lax.psum(grad_parts, SUB)]
    pallas_call x1, Pallas kernels: 103 us -> 79.9 us  [gather_call(): pl.pallas_call(kern, grid=(offsets,), in_specs=[pl.BlockSpec((offsets, co...]
  transfers between devices with their start and end apart: 4 -> 4, of which waited for: 4 -> 4; matrix products, arithmetic and copies ran while one was open for 0% -> 8% of each run, Pallas kernels for 0% -> 0%
where the time goes in v7:
time: 354 us
  waiting for transfers between devices  167 us (47%)
  Pallas kernels  79.9 us (23%)
  blocking collectives  38.2 us (11%)
  matrix products  26.8 us (8%)
  between operations  14.9 us (4%)
  other arithmetic  12.8 us (4%)
  local copies, waits for them, and re-layouts  9.27 us (3%)
  starting transfers between devices  4.86 us (1%)
    psum x1, waiting for transfers between devices, per_device(): kernel_grad = lax.psum(grad_parts, SUB)  147 us
    pallas_call x1, Pallas kernels, gather_call(): pl.pallas_call(kern, grid=(offsets,), in_specs=[pl.BlockSpec((offsets, co...  79.9 us
    all_gather x3, blocking collectives, per_device(): stats = lax.all_gather(stats, axis, axis=0, tiled=True)  38.2 us
    dot_general x1, matrix products, per_device(): lax.dot_general(weights, picked, (((0, 2), (0, 1)), ((), ())), preferred_...  26.8 us
    all_gather x1, waiting for transfers between devices, per_device(): own_chans = lax.all_gather(normed, 'chan', axis=0, tiled=True)  13.6 us
    unnamed x12, local copies, waits for them, and re-layouts  7.41 us
  transfers between devices with their start and end apart: 4, of which 4 were waited for; matrix products, arithmetic and copies ran while one was open for 8% of the time, Pallas kernels for 0%

profile of v7, /device:TPU:0, one launch (start us, length us, event | category | flops | bytes accessed | tf_op | source)
XLA Modules:
  0.0 353.8 jit_solution(7492583691892918944)
XLA Ops:
  7.2 0.0 copy-start
  7.2 0.0 copy-start.3
  7.2 0.0 copy-start.2
  7.2 0.0 all-gather.4.cloned.1.call-start
  8.0 0.6 fusion.20
  8.6 1.6 fusion.2
  10.2 0.7 broadcast_divide_fusion.1
  10.8 1.8 fusion.5
  12.6 0.7 pad.5.clone
  13.4 0.1 maximum_bitcast_fusion
  13.4 12.5 %all-gather = f32[4,3,192]{2,1,0:T(4,128)S(1)} all-gather(f32[1,3,192]{2,1,0:T(4,128)S(1)} %maximum_bitcast_fusion), channel_id=1, replica_groups=mesh['z'=4,'y'=4,'x'=4,'chan'=2] {'x'}, dimensions={0}, use_global_device_ids=true | all-gather | bytes 11520 | tf_op jit(solution)/shard_map/all_gather | solution.py:92
  25.9 12.4 %all-gather.1 = f32[4,12,192]{2,1,0:T(8,128)S(1)} all-gather(f32[1,12,192]{2,1,0:T(8,128)S(1)} %reshape.45), channel_id=1, replica_groups=mesh['z'=4,'y'=4,'x'=4,'chan'=2] {'y'}, dimensions={0}, use_global_device_ids=true | all-gather | bytes 46080 | tf_op jit(solution)/shard_map/all_gather | solution.py:92
  38.3 13.3 %all_gather.14 = f32[192,192]{1,0:T(8,128)S(1)} all-gather(f32[48,192]{1,0:T(8,128)S(1)} %reshape.46), channel_id=1, replica_groups=mesh['z'=4,'y'=4,'x'=4,'chan'=2] {'z'}, dimensions={0}, use_global_device_ids=true | all-gather | bytes 184320 | tf_op jit(solution)/shard_map/all_gather | solution.py:92
  51.6 0.1 reshape.42
  51.7 0.2 slice_reduce_fusion.2
  51.9 0.0 copy-start.1
  51.9 0.6 slice_reduce_fusion.1
  52.6 0.6 broadcast_divide_fusion
  53.2 0.0 copy-done.3
  53.3 0.7 rsqrt_multiply_fusion
  53.9 0.0 copy-done
  53.9 0.0 copy-done.2
  53.9 1.7 fusion.10
  55.7 0.0 all-gather.4.cloned.1.call-update
  55.7 0.0 all-reduce.2.cloned.1.call-start
  55.8 13.6 %all-gather.4.cloned.1.call-done = bf16[384,3072]{1,0:T(8,128)(2,1)} async-done(((bf16[192,3072]{1,0:T(8,128)(2,1)}), bf16[384,3072]{1,0:T(8,128)(2,1)}) %all-gather.4.cloned.1.call-update) | async-done | bytes 2359312 | tf_op jit(solution)/shard_map/all_gather | solution.py:104
  69.3 1.1 fusion.21
  70.4 3.5 collective-permute-start
  73.9 1.3 collective-permute-start.1
  75.2 0.0 copy-done.1
  75.2 0.8 subtract_select_fusion.rel_ref
  76.0 2.5 collective-permute-done
  78.5 4.1 %collective-permute-done.1 = bf16[384,256]{1,0:T(8,128)(2,1)S(1)} collective-permute-done((bf16[384,256]{1,0:T(8,128)(2,1)S(1)}, bf16[384,256]{1,0:T(8,128)(2,1)S(1)}, u32[]{:S(2)}, u32[]{:S(2)}) %collective-permute-start.1) | collective-permute-done | bytes 196640 | tf_op jit(solution)/shard_map/ppermute | solution.py:30
  82.6 3.4 pad_maximum_fusion.act_ref
  86.0 79.9 %shard_map.86 = (bf16[27,384,3072]{2,1,0:T(8,128)(2,1)}, f32[27,192,384]{2,1,0:T(8,128)}) custom-call(s32[27,3072]{1,0:T(8,128)} %subtract_select_fusion.rel_ref, bf16[384,3584]{1,0:T(8,128)(2,1)} %pad_maximum_fusion.act_ref, bf16[192,3072]{1,0:T(8,128)(2,1)} %g_ref.1), custom_call_target="tpu_custom_call" | custom-call | tf_op jit(solution)/shard_map/pallas_call | solution.py:55
  165.9 0.0 all-reduce.2.cloned.1.call-update
  165.9 26.8 %fusion.1 = bf16[192,3072]{1,0:T(8,128)(2,1)} fusion(bf16[27,192,384]{2,1,0:T(8,128)(2,1)} %param.12, bf16[27,384,3072]{2,1,0:T(8,128)(2,1)} %get-tuple-element.4), kind=kOutput, calls=%fused_computation.2 | convolution fusion | flops 12231180288 | bytes 68861952 | tf_op jit(solution)/shard_map/dot_general | solution.py:111
  192.7 146.9 %all-reduce.2.cloned.1.call-done = f32[27,192,384]{2,1,0:T(8,128)} async-done(((f32[27,192,384]{2,1,0:T(8,128)}), f32[27,192,384]{2,1,0:T(8,128)}) %all-reduce.2.cloned.1.call-update) | async-done | bytes 7962640 | tf_op jit(solution)/shard_map/psum | solution.py:110
  339.6 7.4 %copy.28 = f32[27,192,384]{2,1,0:T(8,128)} copy(f32[27,192,384]{2,1,0:T(8,128)} %all-reduce.2.cloned.1.call-done) | data formatting | bytes 15925248
  (6 shorter events, 0.1 us)
Async XLA Ops:
  7.2 46.8 %copy-start = (bf16[192,3072]{1,0:T(8,128)(2,1)S(1)}, bf16[192,3072]{1,0:T(8,128)(2,1)}, u32[]{:S(2)}) copy-start(bf16[192,3072]{1,0:T(8,128)(2,1)} %param.7) | copy-start | bytes 3538948
  7.2 46.1 %copy-start.3 = (f32[192]{0:T(256)S(1)}, f32[192]{0:T(256)}, u32[]{:S(2)}) copy-start(f32[192]{0:T(256)} %param.8) | copy-start | bytes 2308
  7.2 46.7 %copy-start.2 = (f32[192]{0:T(256)S(1)}, f32[192]{0:T(256)}, u32[]{:S(2)}) copy-start(f32[192]{0:T(256)} %param.9) | copy-start | bytes 2308
  7.2 62.1 %all-gather.4.cloned.1.call-start = ((), (), s32[]{:S(2)}) async-start(), calls=%async_computation | async-start | bytes 3538944 | tf_op jit(solution)/shard_map/all_gather | solution.py:104
  51.9 23.3 %copy-start.1 = (s32[27,3072]{1,0:T(8,128)S(1)}, s32[27,3072]{1,0:T(8,128)}, u32[]{:S(2)}) copy-start(s32[27,3072]{1,0:T(8,128)} %param.11) | copy-start | bytes 995332
  55.7 283.9 %all-reduce.2.cloned.1.call-start = ((), (), s32[]{:S(2)}) async-start(), calls=%async_computation.1 | async-start | bytes 15925248 | tf_op jit(solution)/shard_map/psum | solution.py:110
  70.4 8.1 %collective-permute-start = (bf16[384,256]{1,0:T(8,128)(2,1)S(1)}, bf16[384,256]{1,0:T(8,128)(2,1)S(1)}, u32[]{:S(2)}, u32[]{:S(2)}) collective-permute-start(bf16[384,256]{1,0:T(8,128)(2,1)S(1)} %get-tuple-element.8), channel_id=1, source_target_pairs={{0,2},{2,4},{4,6},{6,8},{8,10},{10,12},{12,14},{14,16},{16,18},{18... | collective-permute-start | bytes 589832 | tf_op jit(solution)/shard_map/ppermute | solution.py:29
  73.9 8.7 %collective-permute-start.1 = (bf16[384,256]{1,0:T(8,128)(2,1)S(1)}, bf16[384,256]{1,0:T(8,128)(2,1)S(1)}, u32[]{:S(2)}, u32[]{:S(2)}) collective-permute-start(bf16[384,256]{1,0:T(8,128)(2,1)S(1)} %get-tuple-element.9), channel_id=1, source_target_pairs={{2,0},{4,2},{6,4},{8,6},{10,8},{12,10},{14,12},{16,14},{18,16},{20... | collective-permute-start | bytes 589832 | tf_op jit(solution)/shard_map/ppermute | solution.py:30
Sparse Core Ops, SparseCore 0:
  55.8 13.4 all-gather.3
  166.0 173.4 all-reduce.1

commit v8 on v7

--- a/solution.py
+++ b/solution.py
@@ -19,16 +19,15 @@
     return x
 
 
-def padded(x, width):
+def halo_pad(x, width, live):
     count = lax.axis_size(SUB)
     length = x.shape[1]
     up = [(i, (i + 1) % count) for i in range(count - 1)]
     down = [(j, i) for i, j in up]
-    last = lax.slice_in_dim(x, length - width, length, axis=1)
-    first = lax.slice_in_dim(x, 0, width, axis=1)
-    before = lax.ppermute(last, SUB, up)
-    after = lax.ppermute(first, SUB, down)
-    return jnp.concatenate([before, x, after], axis=1)
+    before = lax.ppermute(x[:, length - width:], SUB, up)
+    after = lax.ppermute(x[:, :width], SUB, down)
+    next_live = lax.ppermute(live, SUB, down)
+    return jnp.concatenate([before, x, after], axis=1), next_live
 
 
 def offset_kernel(rel_ref, act_ref, g_ref, picked_ref, kg_ref, *, halo, blocks):
@@ -79,6 +78,8 @@
     border = columns // 12
     region_idx = lax.axis_index(SUB)
     column = jnp.arange(columns, dtype=jnp.int32)
+    raw_pad, next_live = halo_pad(features, border, live)
+    table = lax.all_gather(raw_pad, "chan", axis=0, tiled=True).astype(jnp.float32)
     live_limit = live[0] - border
     live_mask = ((column < live_limit) | (column >= columns - border)).astype(jnp.float32)
     values = features.astype(jnp.float32)
@@ -87,22 +88,28 @@
     local_mean = local_sum / live_rows
     local_dev = (values - local_mean[:, None]) * live_mask[None, :]
     local_sq = jnp.sum(local_dev * local_dev, axis=1)
-    stats = jnp.stack([local_sum, local_sq, jnp.broadcast_to(live_rows, local_sum.shape)])
+    stats = jnp.stack(
+        [local_sum, local_sq, jnp.broadcast_to(live_rows, local_sum.shape), gain, bias]
+    )
+    stats = lax.all_gather(stats, "chan", axis=1, tiled=True)
+    gain_all, bias_all = stats[3], stats[4]
+    stats = stats[:3]
     for axis in reversed(SUB):
         stats = lax.all_gather(stats, axis, axis=0, tiled=True)
-    stats = stats.reshape(-1, 3, channels)
+    stats = stats.reshape(-1, 3, stats.shape[-1])
     sums, squares, counts = stats[:, 0], stats[:, 1], stats[:, 2]
     live_total = jnp.sum(counts[:, 0])
     average = jnp.sum(sums, axis=0) / live_total
     spread = sums / counts - average[None, :]
     variance = (jnp.sum(squares, axis=0) + jnp.sum(counts * spread * spread, axis=0)) / live_total
-    factor = gain * lax.rsqrt(variance + 1e-05)
-    normed = (
-        jnp.maximum((values - average[:, None]) * factor[:, None] + bias[:, None], 0.0)
-        * live_mask[None, :]
+    factor = gain_all * lax.rsqrt(variance + 1e-05)
+    halo_row = jnp.arange(border, dtype=jnp.int32)
+    after_mask = (halo_row < next_live[0] - border).astype(jnp.float32)
+    table_mask = jnp.concatenate([jnp.ones((border,), jnp.float32), live_mask, after_mask])
+    gathered = (
+        jnp.maximum((table - average[:, None]) * factor[:, None] + bias_all[:, None], 0.0)
+        * table_mask[None, :]
     ).astype(jnp.bfloat16)
-    own_chans = lax.all_gather(normed, "chan", axis=0, tiled=True)
-    gathered = padded(own_chans, border)
     anchor = region_idx * columns - border
     block_base = (column // BLOCK) * BLOCK
     rel = jnp.where(neighbors < 0, -1, neighbors - anchor - block_base[None, :])

time: 354 us -> 345 us (0.975)
  waiting for transfers between devices: 167 us -> 144 us
  blocking collectives: 38.2 us -> 47.1 us
    all_gather x1, waiting for transfers between devices: 13.6 us -> 0.02 us  [per_device(): lax.all_gather(raw_pad, 'chan', axis=0, tiled=True).astype(jnp.float32)]
    all_gather x3, blocking collectives: 38.2 us -> 45.3 us  [per_device(): stats = lax.all_gather(stats, axis, axis=0, tiled=True)]
    psum x1, waiting for transfers between devices: 147 us -> 142 us  [per_device(): kernel_grad = lax.psum(grad_parts, SUB)]
    ppermute x2 -> x3, waiting for transfers between devices: 6.6 us -> 2.34 us  [the longest x1 2.34 us: halo_pad(): after = lax.ppermute(x[:, :width], SUB, down)]
    ppermute x2 -> x3, starting transfers between devices: 4.78 us -> 7.27 us  [the longest x1 4.69 us: halo_pad(): before = lax.ppermute(x[:, length - width:], SUB, up)]
    unnamed x12 -> x14, local copies, waits for them, and re-layouts: 7.41 us -> 7.5 us
  transfers between devices with their start and end apart: 4 -> 5, of which waited for: 4 -> 2; matrix products, arithmetic and copies ran while one was open for 8% -> 11% of each run, Pallas kernels for 0% -> 0%
where the time goes in v8:
time: 345 us; the launch traced here: 344 us
  waiting for transfers between devices  144 us (42%)
  Pallas kernels  80 us (23%)
  blocking collectives  47.1 us (14%)
  matrix products  27.2 us (8%)
  between operations  15.6 us (5%)
  other arithmetic  13.9 us (4%)
  local copies, waits for them, and re-layouts  9.22 us (3%)
  starting transfers between devices  7.35 us (2%)
    psum x1, waiting for transfers between devices, per_device(): kernel_grad = lax.psum(grad_parts, SUB)  142 us
    pallas_call x1, Pallas kernels, gather_call(): pl.pallas_call(kern, grid=(offsets,), in_specs=[pl.BlockSpec((offsets, co...  80 us
    all_gather x3, blocking collectives, per_device(): stats = lax.all_gather(stats, axis, axis=0, tiled=True)  45.3 us
    dot_general x1, matrix products, per_device(): lax.dot_general(weights, picked, (((0, 2), (0, 1)), ((), ())), preferred_...  27.2 us
    unnamed x14, local copies, waits for them, and re-layouts  7.5 us
  transfers between devices with their start and end apart: 5, of which 2 were waited for; matrix products, arithmetic and copies ran while one was open for 11% of the time, Pallas kernels for 0%

profile of v8, /device:TPU:0, one launch (start us, length us, event | category | flops | bytes accessed | tf_op | source)
XLA Modules:
  0.0 344.1 jit_solution(12343536857209850473)
XLA Ops:
  7.2 0.0 all-gather.5.cloned.1.call-start
  7.2 1.3 collective-permute-start.2
  8.5 1.0 fusion.16
  9.5 0.0 copy-start
  9.5 4.7 %collective-permute-start = (bf16[192,256]{1,0:T(8,128)(2,1)S(1)}, bf16[192,256]{1,0:T(8,128)(2,1)S(1)}, u32[]{:S(2)}, u32[]{:S(2)}) collective-permute-start(bf16[192,256]{1,0:T(8,128)(2,1)S(1)} %get-tuple-element.10), channel_id=1, source_target_pairs={{0,2},{2,4},{4,6},{6,8},{8,10},{10,12},{12,14},{14,16},{16,18},{18... | collective-permute-start | bytes 294920 | tf_op jit(solution)/shard_map/ppermute | solution.py:27
  14.2 1.3 collective-permute-start.1
  16.1 0.6 fusion.15
  16.7 1.6 fusion.2
  18.3 0.0 copy-start.2
  18.3 0.0 copy-start.3
  18.3 0.0 collective-permute-done
  18.4 2.3 collective-permute-done.1
  20.7 2.4 pad_maximum_fusion
  23.1 0.0 copy-start.1
  23.1 0.0 all-gather.5.cloned.1.call-update
  23.2 0.0 all-reduce.2.cloned.1.call-start
  23.2 0.6 broadcast_divide_fusion.1
  23.8 0.0 copy-done
  23.8 0.5 fusion.5
  24.4 0.6 stack_broadcast_in_dim.3
  25.0 0.0 copy-done.2
  25.0 0.0 copy-done.3
  25.0 1.8 all-gather
  26.8 0.1 reshape.59
  26.9 15.8 %all-gather.1 = f32[4,3,384]{2,1,0:T(4,128)S(1)} all-gather(f32[1,3,384]{2,1,0:T(4,128)S(1)} %slice_bitcast_fusion), channel_id=1, replica_groups=mesh['z'=4,'y'=4,'x'=4,'chan'=2] {'x'}, dimensions={0}, use_global_device_ids=true | all-gather | bytes 23040 | tf_op jit(solution)/shard_map/all_gather | solution.py:98
  42.8 15.9 %all-gather.2 = f32[4,12,384]{2,1,0:T(8,128)S(1)} all-gather(f32[1,12,384]{2,1,0:T(8,128)S(1)} %reshape.62), channel_id=1, replica_groups=mesh['z'=4,'y'=4,'x'=4,'chan'=2] {'y'}, dimensions={0}, use_global_device_ids=true | all-gather | bytes 92160 | tf_op jit(solution)/shard_map/all_gather | solution.py:98
  58.7 13.5 %all_gather.19 = f32[192,384]{1,0:T(8,128)S(1)} all-gather(f32[48,384]{1,0:T(8,128)S(1)} %reshape.63), channel_id=1, replica_groups=mesh['z'=4,'y'=4,'x'=4,'chan'=2] {'z'}, dimensions={0}, use_global_device_ids=true | all-gather | bytes 368640 | tf_op jit(solution)/shard_map/all_gather | solution.py:98
  72.2 0.1 reshape.57
  72.4 0.2 slice_reduce_fusion.4
  72.7 0.6 slice_reduce_fusion.1
  73.3 0.6 broadcast_divide_fusion
  73.9 0.1 fusion.6
  74.0 0.7 rsqrt_multiply_fusion
  74.6 0.0 copy-done.1
  74.7 0.8 subtract_select_fusion.rel_ref
  75.5 0.0 collective-permute-done.2
  76.2 0.0 all-gather.5.cloned.1.call-done
  76.2 5.1 %multiply_convert_fusion.act_ref = bf16[384,3584]{1,0:T(8,128)(2,1)} fusion(bf16[384,3584]{1,0:T(8,128)(2,1)} %all-gather.5.cloned.1.call-done, f32[3584]{0:T(1024)S(1)} %pad_maximum_fusion.1, f32[384]{0:T(512)S(1)} %get-tuple-element.9, f32[384]{0:T(512)S(1)} %rsqrt_multiply_fusion, f32[384]{0:T(512)S(1)} %broadcast_divide_fusion), kind=kLoop, calls=%fused_computation | loop fusion | flops 9633792 | bytes 5523968 | tf_op jit(solution)/shard_map/convert_element_type | solution.py:112
  81.3 80.0 %shard_map.86 = (bf16[27,384,3072]{2,1,0:T(8,128)(2,1)}, f32[27,192,384]{2,1,0:T(8,128)}) custom-call(s32[27,3072]{1,0:T(8,128)} %subtract_select_fusion.rel_ref, bf16[384,3584]{1,0:T(8,128)(2,1)} %multiply_convert_fusion.act_ref, bf16[192,3072]{1,0:T(8,128)(2,1)} %g_ref.1), custom_call_target="tpu_custom_call" | custom-call | tf_op jit(solution)/shard_map/pallas_call | solution.py:54
  161.2 0.0 all-reduce.2.cloned.1.call-update
  161.3 27.2 %fusion.1 = bf16[192,3072]{1,0:T(8,128)(2,1)} fusion(bf16[27,192,384]{2,1,0:T(8,128)(2,1)} %param.12, bf16[27,384,3072]{2,1,0:T(8,128)(2,1)} %get-tuple-element.4), kind=kOutput, calls=%fused_computation.3 | convolution fusion | flops 12231180288 | bytes 68861952 | tf_op jit(solution)/shard_map/dot_general | solution.py:118
  188.4 141.5 %all-reduce.2.cloned.1.call-done = f32[27,192,384]{2,1,0:T(8,128)} async-done(((f32[27,192,384]{2,1,0:T(8,128)}), f32[27,192,384]{2,1,0:T(8,128)}) %all-reduce.2.cloned.1.call-update) | async-done | bytes 7962640 | tf_op jit(solution)/shard_map/psum | solution.py:117
  329.9 7.4 %copy.29 = f32[27,192,384]{2,1,0:T(8,128)} copy(f32[27,192,384]{2,1,0:T(8,128)} %all-reduce.2.cloned.1.call-done) | data formatting | bytes 15925248
  (12 shorter events, 0.1 us)
Async XLA Ops:
  7.2 69.0 %all-gather.5.cloned.1.call-start = ((), (), s32[]{:S(2)}) async-start(), calls=%async_computation | async-start | bytes 4128768 | tf_op jit(solution)/shard_map/all_gather | solution.py:82
  7.2 68.3 %collective-permute-start.2 = (s32[1]{0:T(128)}, s32[1]{0:T(128)}, u32[]{:S(2)}, u32[]{:S(2)}) collective-permute-start(s32[1]{0:T(128)} %param.10), channel_id=1, source_target_pairs={{2,0},{4,2},{6,4},{8,6},{10,8},{12,10},{14,12},{16,14},{18,16},{20... | collective-permute-start | bytes 20 | tf_op jit(solution)/shard_map/ppermute | solution.py:29
  9.5 14.4 %copy-start = (bf16[192,3072]{1,0:T(8,128)(2,1)S(1)}, bf16[192,3072]{1,0:T(8,128)(2,1)}, u32[]{:S(2)}) copy-start(bf16[192,3072]{1,0:T(8,128)(2,1)} %param.7) | copy-start | bytes 3538948
  9.5 8.9 %collective-permute-start = (bf16[192,256]{1,0:T(8,128)(2,1)S(1)}, bf16[192,256]{1,0:T(8,128)(2,1)S(1)}, u32[]{:S(2)}, u32[]{:S(2)}) collective-permute-start(bf16[192,256]{1,0:T(8,128)(2,1)S(1)} %get-tuple-element.10), channel_id=1, source_target_pairs={{0,2},{2,4},{4,6},{6,8},{8,10},{10,12},{12,14},{14,16},{16,18},{18... | collective-permute-start | bytes 294920 | tf_op jit(solution)/shard_map/ppermute | solution.py:27
  14.2 6.5 %collective-permute-start.1 = (bf16[192,256]{1,0:T(8,128)(2,1)S(1)}, bf16[192,256]{1,0:T(8,128)(2,1)S(1)}, u32[]{:S(2)}, u32[]{:S(2)}) collective-permute-start(bf16[192,256]{1,0:T(8,128)(2,1)S(1)} %get-tuple-element.11), channel_id=1, source_target_pairs={{2,0},{4,2},{6,4},{8,6},{10,8},{12,10},{14,12},{16,14},{18,16},{20... | collective-permute-start | bytes 294920 | tf_op jit(solution)/shard_map/ppermute | solution.py:28
  18.3 6.6 %copy-start.2 = (f32[192]{0:T(256)S(1)}, f32[192]{0:T(256)}, u32[]{:S(2)}) copy-start(f32[192]{0:T(256)} %param.8) | copy-start | bytes 2308
  18.3 6.6 %copy-start.3 = (f32[192]{0:T(256)S(1)}, f32[192]{0:T(256)}, u32[]{:S(2)}) copy-start(f32[192]{0:T(256)} %param.9) | copy-start | bytes 2308
  23.1 51.5 %copy-start.1 = (s32[27,3072]{1,0:T(8,128)S(1)}, s32[27,3072]{1,0:T(8,128)}, u32[]{:S(2)}) copy-start(s32[27,3072]{1,0:T(8,128)} %param.11) | copy-start | bytes 995332
  23.2 306.8 %all-reduce.2.cloned.1.call-start = ((), (), s32[]{:S(2)}) async-start(), calls=%async_computation.1 | async-start | bytes 15925248 | tf_op jit(solution)/shard_map/psum | solution.py:117
Sparse Core Ops, SparseCore 0:
  23.3 24.5 all-gather.4
  161.4 168.5 all-reduce.1

commit v9 on v8

--- a/solution.py
+++ b/solution.py
@@ -17,6 +17,14 @@
     for axis in reversed(SUB):
         x = lax.psum(x, axis)
     return x
+
+
+def ring_gather(x, axis):
+    count = lax.axis_size(axis)
+    parts = [x]
+    for shift in range(1, count):
+        parts.append(lax.ppermute(x, axis, [(i, (i + shift) % count) for i in range(count)]))
+    return jnp.concatenate(parts, axis=0)
 
 
 def halo_pad(x, width, live):
@@ -95,7 +103,7 @@
     gain_all, bias_all = stats[3], stats[4]
     stats = stats[:3]
     for axis in reversed(SUB):
-        stats = lax.all_gather(stats, axis, axis=0, tiled=True)
+        stats = ring_gather(stats, axis)
     stats = stats.reshape(-1, 3, stats.shape[-1])
     sums, squares, counts = stats[:, 0], stats[:, 1], stats[:, 2]
     live_total = jnp.sum(counts[:, 0])

time: 345 us -> 330 us (0.957)
  blocking collectives: 47.1 us -> 1.82 us
  starting transfers between devices: 7.35 us -> 29 us
  waiting for transfers between devices: 144 us -> 154 us
    all_gather x3 -> x0, blocking collectives: 45.3 us -> none  [per_device(): stats = lax.all_gather(stats, axis, axis=0, tiled=True)]
    ppermute x0 -> x9, starting transfers between devices: none -> 21.7 us  [ring_gather(): lax.ppermute(x, axis, [(i, (i + shift) % count) for i in range(count)])]
    ppermute x0 -> x9, waiting for transfers between devices: none -> 11.3 us  [ring_gather(): lax.ppermute(x, axis, [(i, (i + shift) % count) for i in range(count)])]
    unnamed x14 -> x11, local copies, waits for them, and re-layouts: 7.5 us -> 7.47 us
  transfers between devices with their start and end apart: 5 -> 14, of which waited for: 2 -> 7; matrix products, arithmetic and copies ran while one was open for 11% -> 11% of each run, Pallas kernels for 0% -> 0%
where the time goes in v9:
time: 330 us
  waiting for transfers between devices  154 us (47%)
  Pallas kernels  79.9 us (24%)
  starting transfers between devices  29 us (9%)
  matrix products  27.2 us (8%)
  between operations  15.6 us (5%)
  other arithmetic  12.7 us (4%)
  local copies, waits for them, and re-layouts  9.96 us (3%)
    psum x1, waiting for transfers between devices, per_device(): kernel_grad = lax.psum(grad_parts, SUB)  139 us
    pallas_call x1, Pallas kernels, gather_call(): pl.pallas_call(kern, grid=(offsets,), in_specs=[pl.BlockSpec((offsets, co...  79.9 us
    dot_general x1, matrix products, per_device(): lax.dot_general(weights, picked, (((0, 2), (0, 1)), ((), ())), preferred_...  27.2 us
    ppermute x9, starting transfers between devices, ring_gather(): lax.ppermute(x, axis, [(i, (i + shift) % count) for i in range(count)])  21.7 us
    ppermute x9, waiting for transfers between devices, ring_gather(): lax.ppermute(x, axis, [(i, (i + shift) % count) for i in range(count)])  11.3 us
    unnamed x11, local copies, waits for them, and re-layouts  7.47 us
  transfers between devices with their start and end apart: 14, of which 7 were waited for; matrix products, arithmetic and copies ran while one was open for 11% of the time, Pallas kernels for 0%

profile of v9, /device:TPU:0, one launch (start us, length us, event | category | flops | bytes accessed | tf_op | source)
XLA Modules:
  0.0 330.1 jit_solution(4487982636716121627)
XLA Ops:
  7.2 0.0 copy-start
  7.2 0.0 all-gather.3.cloned.1.call-start
  7.2 1.4 collective-permute-start.11
  8.7 1.0 fusion.15
  9.6 4.6 %collective-permute-start = (bf16[192,256]{1,0:T(8,128)(2,1)S(1)}, bf16[192,256]{1,0:T(8,128)(2,1)S(1)}, u32[]{:S(2)}, u32[]{:S(2)}) collective-permute-start(bf16[192,256]{1,0:T(8,128)(2,1)S(1)} %get-tuple-element.10), channel_id=1, source_target_pairs={{0,2},{2,4},{4,6},{6,8},{8,10},{10,12},{12,14},{14,16},{16,18},{18... | collective-permute-start | bytes 294920 | tf_op jit(solution)/shard_map/ppermute | solution.py:35
  14.2 1.3 collective-permute-start.1
  16.1 0.6 fusion.14
  16.7 0.0 copy-start.2
  16.7 0.0 copy-start.3
  16.7 0.0 copy-start.1
  16.8 0.0 collective-permute-done
  16.8 3.9 %collective-permute-done.1 = bf16[192,256]{1,0:T(8,128)(2,1)S(1)} collective-permute-done((bf16[192,256]{1,0:T(8,128)(2,1)S(1)}, bf16[192,256]{1,0:T(8,128)(2,1)S(1)}, u32[]{:S(2)}, u32[]{:S(2)}) %collective-permute-start.1) | collective-permute-done | bytes 98336 | tf_op jit(solution)/shard_map/ppermute | solution.py:36
  20.7 2.4 pad_maximum_fusion
  23.1 0.0 all-gather.3.cloned.1.call-update
  23.1 0.0 all-reduce.2.cloned.1.call-start
  23.2 0.0 copy-done
  23.2 0.3 fusion.2
  23.5 0.6 broadcast_divide_fusion.1
  24.1 0.5 fusion.5
  24.7 0.6 stack_broadcast_in_dim.3
  25.2 0.0 copy-done.2
  25.3 0.0 copy-done.3
  25.3 1.8 all-gather
  27.1 0.1 reshape.59
  27.2 7.1 %collective-permute-start.4 = (f32[3,384]{1,0:T(4,128)S(1)}, f32[3,384]{1,0:T(4,128)S(1)}, u32[]{:S(2)}, u32[]{:S(2)}) collective-permute-start(f32[3,384]{1,0:T(4,128)S(1)} %slice.36), channel_id=1, source_target_pairs={{0,6},{2,0},{4,2},{6,4},{1,7},{3,1},{5,3},{7,5},{8,14},{10,8},{12,... | collective-permute-start | bytes 13832 | tf_op jit(solution)/shard_map/ppermute | solution.py:26
  34.3 0.0 collective-permute-start.3
  34.3 0.9 collective-permute-start.2
  35.3 0.0 copy-done.1
  35.3 0.8 subtract_select_fusion.rel_ref
  36.1 0.0 collective-permute-done.11
  36.8 0.0 collective-permute-done.4
  36.8 2.7 collective-permute-done.3
  39.4 0.0 collective-permute-done.2
  39.5 7.3 %collective-permute-start.7 = (f32[12,384]{1,0:T(8,128)S(1)}, f32[12,384]{1,0:T(8,128)S(1)}, u32[]{:S(2)}, u32[]{:S(2)}) collective-permute-start(f32[12,384]{1,0:T(8,128)S(1)} %pad_maximum_fusion.1), channel_id=1, source_target_pairs={{0,24},{8,0},{16,8},{24,16},{1,25},{9,1},{17,9},{25,17},{2,26},{10... | collective-permute-start | bytes 55304 | tf_op jit(solution)/shard_map/ppermute | solution.py:26
  46.8 0.0 collective-permute-start.6
  46.8 0.9 collective-permute-start.5
  47.7 0.6 collective-permute-done.7
  48.3 3.8 %collective-permute-done.6 = f32[12,384]{1,0:T(8,128)S(1)} collective-permute-done((f32[12,384]{1,0:T(8,128)S(1)}, f32[12,384]{1,0:T(8,128)S(1)}, u32[]{:S(2)}, u32[]{:S(2)}) %collective-permute-start.6) | collective-permute-done | bytes 18464 | tf_op jit(solution)/shard_map/ppermute | solution.py:26
  52.1 0.0 collective-permute-done.5
  52.1 0.4 concatenate.19
  52.5 0.2 collective-permute-start.10
  52.7 3.8 %collective-permute-start.9 = (f32[48,384]{1,0:T(8,128)S(1)}, f32[48,384]{1,0:T(8,128)S(1)}, u32[]{:S(2)}, u32[]{:S(2)}) collective-permute-start(f32[48,384]{1,0:T(8,128)S(1)} %concatenate.19), channel_id=1, source_target_pairs={{0,64},{32,96},{64,0},{96,32},{1,65},{33,97},{65,1},{97,33},{2,66}... | collective-permute-start | bytes 221192 | tf_op jit(solution)/shard_map/ppermute | solution.py:26
  56.5 1.3 collective-permute-start.8
  57.9 0.0 collective-permute-done.10
  57.9 1.1 collective-permute-done.9
  58.9 3.2 collective-permute-done.8
  62.1 0.4 concatenate.20
  62.5 0.1 reshape.57
  62.6 0.2 slice_reduce_fusion.4
  62.9 0.7 slice_reduce_fusion.1
  63.6 0.7 broadcast_divide_fusion
  64.3 0.1 fusion.6
  64.3 0.7 rsqrt_multiply_fusion
  65.0 0.0 all-gather.3.cloned.1.call-done
  65.0 5.1 %multiply_convert_fusion.act_ref = bf16[384,3584]{1,0:T(8,128)(2,1)} fusion(bf16[384,3584]{1,0:T(8,128)(2,1)} %all-gather.3.cloned.1.call-done, f32[3584]{0:T(1024)S(1)} %pad_maximum_fusion.2, f32[384]{0:T(512)S(1)} %get-tuple-element.9, f32[384]{0:T(512)S(1)} %rsqrt_multiply_fusion, f32[384]{0:T(512)S(1)} %broadcast_divide_fusion), kind=kLoop, calls=%fused_computation | loop fusion | flops 9633792 | bytes 5523968 | tf_op jit(solution)/shard_map/convert_element_type | solution.py:120
  70.1 79.9 %shard_map.86 = (bf16[27,384,3072]{2,1,0:T(8,128)(2,1)}, f32[27,192,384]{2,1,0:T(8,128)}) custom-call(s32[27,3072]{1,0:T(8,128)} %subtract_select_fusion.rel_ref, bf16[384,3584]{1,0:T(8,128)(2,1)} %multiply_convert_fusion.act_ref, bf16[192,3072]{1,0:T(8,128)(2,1)} %g_ref.1), custom_call_target="tpu_custom_call" | custom-call | tf_op jit(solution)/shard_map/pallas_call | solution.py:62
  150.0 0.0 all-reduce.2.cloned.1.call-update
  150.1 27.2 %fusion.1 = bf16[192,3072]{1,0:T(8,128)(2,1)} fusion(bf16[27,192,384]{2,1,0:T(8,128)(2,1)} %param.12, bf16[27,384,3072]{2,1,0:T(8,128)(2,1)} %get-tuple-element.4), kind=kOutput, calls=%fused_computation.3 | convolution fusion | flops 12231180288 | bytes 68861952 | tf_op jit(solution)/shard_map/dot_general | solution.py:126
  177.3 138.6 %all-reduce.2.cloned.1.call-done = f32[27,192,384]{2,1,0:T(8,128)} async-done(((f32[27,192,384]{2,1,0:T(8,128)}), f32[27,192,384]{2,1,0:T(8,128)}) %all-reduce.2.cloned.1.call-update) | async-done | bytes 7962640 | tf_op jit(solution)/shard_map/psum | solution.py:125
  315.9 7.4 %copy.20 = f32[27,192,384]{2,1,0:T(8,128)} copy(f32[27,192,384]{2,1,0:T(8,128)} %all-reduce.2.cloned.1.call-done) | data formatting | bytes 15925248
  (11 shorter events, 0.1 us)
Async XLA Ops:
  7.2 16.0 %copy-start = (bf16[192,3072]{1,0:T(8,128)(2,1)S(1)}, bf16[192,3072]{1,0:T(8,128)(2,1)}, u32[]{:S(2)}) copy-start(bf16[192,3072]{1,0:T(8,128)(2,1)} %param.7) | copy-start | bytes 3538948
  7.2 57.8 %all-gather.3.cloned.1.call-start = ((), (), s32[]{:S(2)}) async-start(), calls=%async_computation | async-start | bytes 4128768 | tf_op jit(solution)/shard_map/all_gather | solution.py:90
  7.2 28.9 %collective-permute-start.11 = (s32[1]{0:T(128)}, s32[1]{0:T(128)}, u32[]{:S(2)}, u32[]{:S(2)}) collective-permute-start(s32[1]{0:T(128)} %param.10), channel_id=1, source_target_pairs={{2,0},{4,2},{6,4},{8,6},{10,8},{12,10},{14,12},{16,14},{18,16},{20... | collective-permute-start | bytes 20 | tf_op jit(solution)/shard_map/ppermute | solution.py:37
  9.6 7.1 %collective-permute-start = (bf16[192,256]{1,0:T(8,128)(2,1)S(1)}, bf16[192,256]{1,0:T(8,128)(2,1)S(1)}, u32[]{:S(2)}, u32[]{:S(2)}) collective-permute-start(bf16[192,256]{1,0:T(8,128)(2,1)S(1)} %get-tuple-element.10), channel_id=1, source_target_pairs={{0,2},{2,4},{4,6},{6,8},{8,10},{10,12},{12,14},{14,16},{16,18},{18... | collective-permute-start | bytes 294920 | tf_op jit(solution)/shard_map/ppermute | solution.py:35
  14.2 6.5 %collective-permute-start.1 = (bf16[192,256]{1,0:T(8,128)(2,1)S(1)}, bf16[192,256]{1,0:T(8,128)(2,1)S(1)}, u32[]{:S(2)}, u32[]{:S(2)}) collective-permute-start(bf16[192,256]{1,0:T(8,128)(2,1)S(1)} %get-tuple-element.11), channel_id=1, source_target_pairs={{2,0},{4,2},{6,4},{8,6},{10,8},{12,10},{14,12},{16,14},{18,16},{20... | collective-permute-start | bytes 294920 | tf_op jit(solution)/shard_map/ppermute | solution.py:36
  16.7 8.5 %copy-start.2 = (f32[192]{0:T(256)S(1)}, f32[192]{0:T(256)}, u32[]{:S(2)}) copy-start(f32[192]{0:T(256)} %param.8) | copy-start | bytes 2308
  16.7 8.5 %copy-start.3 = (f32[192]{0:T(256)S(1)}, f32[192]{0:T(256)}, u32[]{:S(2)}) copy-start(f32[192]{0:T(256)} %param.9) | copy-start | bytes 2308
  16.7 18.5 %copy-start.1 = (s32[27,3072]{1,0:T(8,128)S(1)}, s32[27,3072]{1,0:T(8,128)}, u32[]{:S(2)}) copy-start(s32[27,3072]{1,0:T(8,128)} %param.11) | copy-start | bytes 995332
  23.1 292.7 %all-reduce.2.cloned.1.call-start = ((), (), s32[]{:S(2)}) async-start(), calls=%async_computation.1 | async-start | bytes 15925248 | tf_op jit(solution)/shard_map/psum | solution.py:125
  27.2 9.6 %collective-permute-start.4 = (f32[3,384]{1,0:T(4,128)S(1)}, f32[3,384]{1,0:T(4,128)S(1)}, u32[]{:S(2)}, u32[]{:S(2)}) collective-permute-start(f32[3,384]{1,0:T(4,128)S(1)} %slice.36), channel_id=1, source_target_pairs={{0,6},{2,0},{4,2},{6,4},{1,7},{3,1},{5,3},{7,5},{8,14},{10,8},{12,... | collective-permute-start | bytes 13832 | tf_op jit(solution)/shard_map/ppermute | solution.py:26
  34.3 5.1 %collective-permute-start.3 = (f32[3,384]{1,0:T(4,128)S(1)}, f32[3,384]{1,0:T(4,128)S(1)}, u32[]{:S(2)}, u32[]{:S(2)}) collective-permute-start(f32[3,384]{1,0:T(4,128)S(1)} %slice.36), channel_id=1, source_target_pairs={{0,4},{2,6},{4,0},{6,2},{1,5},{3,7},{5,1},{7,3},{8,12},{10,14},{12... | collective-permute-start | bytes 13832 | tf_op jit(solution)/shard_map/ppermute | solution.py:26
  34.3 5.1 %collective-permute-start.2 = (f32[3,384]{1,0:T(4,128)S(1)}, f32[3,384]{1,0:T(4,128)S(1)}, u32[]{:S(2)}, u32[]{:S(2)}) collective-permute-start(f32[3,384]{1,0:T(4,128)S(1)} %slice.36), channel_id=1, source_target_pairs={{0,2},{2,4},{4,6},{6,0},{1,3},{3,5},{5,7},{7,1},{8,10},{10,12},{12... | collective-permute-start | bytes 13832 | tf_op jit(solution)/shard_map/ppermute | solution.py:26
  39.5 8.8 %collective-permute-start.7 = (f32[12,384]{1,0:T(8,128)S(1)}, f32[12,384]{1,0:T(8,128)S(1)}, u32[]{:S(2)}, u32[]{:S(2)}) collective-permute-start(f32[12,384]{1,0:T(8,128)S(1)} %pad_maximum_fusion.1), channel_id=1, source_target_pairs={{0,24},{8,0},{16,8},{24,16},{1,25},{9,1},{17,9},{25,17},{2,26},{10... | collective-permute-start | bytes 55304 | tf_op jit(solution)/shard_map/ppermute | solution.py:26
  46.8 5.3 %collective-permute-start.6 = (f32[12,384]{1,0:T(8,128)S(1)}, f32[12,384]{1,0:T(8,128)S(1)}, u32[]{:S(2)}, u32[]{:S(2)}) collective-permute-start(f32[12,384]{1,0:T(8,128)S(1)} %pad_maximum_fusion.1), channel_id=1, source_target_pairs={{0,16},{8,24},{16,0},{24,8},{1,17},{9,25},{17,1},{25,9},{2,18},{10... | collective-permute-start | bytes 55304 | tf_op jit(solution)/shard_map/ppermute | solution.py:26
  46.8 5.3 %collective-permute-start.5 = (f32[12,384]{1,0:T(8,128)S(1)}, f32[12,384]{1,0:T(8,128)S(1)}, u32[]{:S(2)}, u32[]{:S(2)}) collective-permute-start(f32[12,384]{1,0:T(8,128)S(1)} %pad_maximum_fusion.1), channel_id=1, source_target_pairs={{0,8},{8,16},{16,24},{24,0},{1,9},{9,17},{17,25},{25,1},{2,10},{10... | collective-permute-start | bytes 55304 | tf_op jit(solution)/shard_map/ppermute | solution.py:26
  52.5 5.4 %collective-permute-start.10 = (f32[48,384]{1,0:T(8,128)S(1)}, f32[48,384]{1,0:T(8,128)S(1)}, u32[]{:S(2)}, u32[]{:S(2)}) collective-permute-start(f32[48,384]{1,0:T(8,128)S(1)} %concatenate.19), channel_id=1, source_target_pairs={{0,96},{32,0},{64,32},{96,64},{1,97},{33,1},{65,33},{97,65},{2,98}... | collective-permute-start | bytes 221192 | tf_op jit(solution)/shard_map/ppermute | solution.py:26
  52.7 6.2 %collective-permute-start.9 = (f32[48,384]{1,0:T(8,128)S(1)}, f32[48,384]{1,0:T(8,128)S(1)}, u32[]{:S(2)}, u32[]{:S(2)}) collective-permute-start(f32[48,384]{1,0:T(8,128)S(1)} %concatenate.19), channel_id=1, source_target_pairs={{0,64},{32,96},{64,0},{96,32},{1,65},{33,97},{65,1},{97,33},{2,66}... | collective-permute-start | bytes 221192 | tf_op jit(solution)/shard_map/ppermute | solution.py:26
  56.5 5.6 %collective-permute-start.8 = (f32[48,384]{1,0:T(8,128)S(1)}, f32[48,384]{1,0:T(8,128)S(1)}, u32[]{:S(2)}, u32[]{:S(2)}) collective-permute-start(f32[48,384]{1,0:T(8,128)S(1)} %concatenate.19), channel_id=1, source_target_pairs={{0,32},{32,64},{64,96},{96,0},{1,33},{33,65},{65,97},{97,1},{2,34}... | collective-permute-start | bytes 221192 | tf_op jit(solution)/shard_map/ppermute | solution.py:26
Sparse Core Ops, SparseCore 0:
  23.3 24.5 all-gather.2
  150.2 165.6 all-reduce.1

commit v10 on v9

--- a/solution.py
+++ b/solution.py
@@ -86,8 +86,9 @@
     border = columns // 12
     region_idx = lax.axis_index(SUB)
     column = jnp.arange(columns, dtype=jnp.int32)
-    raw_pad, next_live = halo_pad(features, border, live)
-    table = lax.all_gather(raw_pad, "chan", axis=0, tiled=True).astype(jnp.float32)
+    own_table = lax.all_gather(features, "chan", axis=0, tiled=True)
+    raw_pad, next_live = halo_pad(own_table, border, live)
+    table = raw_pad.astype(jnp.float32)
     live_limit = live[0] - border
     live_mask = ((column < live_limit) | (column >= columns - border)).astype(jnp.float32)
     values = features.astype(jnp.float32)

time: 330 us -> 331 us (level)
  waiting for transfers between devices: 154 us -> 163 us
  starting transfers between devices: 29 us -> 21.5 us
    psum x1, waiting for transfers between devices: 139 us -> 145 us  [per_device(): kernel_grad = lax.psum(grad_parts, SUB)]
    ppermute x9, starting transfers between devices: 21.7 us -> 15.9 us  [ring_gather(): lax.ppermute(x, axis, [(i, (i + shift) % count) for i in range(count)])]
    unnamed x11 -> x5, local copies, waits for them, and re-layouts: 7.47 us -> 7.46 us
  transfers between devices with their start and end apart: 14 -> 14, of which waited for: 7 -> 11; matrix products, arithmetic and copies ran while one was open for 11% -> 11% of each run, Pallas kernels for 0% -> 0%
where the time goes in v10:
time: 331 us
  waiting for transfers between devices  163 us (49%)
  Pallas kernels  79.9 us (24%)
  matrix products  27 us (8%)
  starting transfers between devices  21.5 us (6%)
  between operations  15.4 us (5%)
  other arithmetic  11.7 us (4%)
  local copies, waits for them, and re-layouts  10.8 us (3%)
    psum x1, waiting for transfers between devices, per_device(): kernel_grad = lax.psum(grad_parts, SUB)  145 us
    pallas_call x1, Pallas kernels, gather_call(): pl.pallas_call(kern, grid=(offsets,), in_specs=[pl.BlockSpec((offsets, co...  79.9 us
    dot_general x1, matrix products, per_device(): lax.dot_general(weights, picked, (((0, 2), (0, 1)), ((), ())), preferred_...  27 us
    ppermute x9, starting transfers between devices, ring_gather(): lax.ppermute(x, axis, [(i, (i + shift) % count) for i in range(count)])  15.9 us
    ppermute x9, waiting for transfers between devices, ring_gather(): lax.ppermute(x, axis, [(i, (i + shift) % count) for i in range(count)])  11.9 us
    unnamed x5, local copies, waits for them, and re-layouts  7.46 us
  transfers between devices with their start and end apart: 14, of which 11 were waited for; matrix products, arithmetic and copies ran while one was open for 11% of the time, Pallas kernels for 0%

profile of v10, /device:TPU:0, one launch (start us, length us, event | category | flops | bytes accessed | tf_op | source)
XLA Modules:
  0.0 331.0 jit_solution(17477273668781298231)
XLA Ops:
  7.2 0.0 copy-start
  7.2 0.0 all-gather.3.cloned.1.call-start
  7.2 0.7 all-gather.3.cloned.1.call-update
  7.9 0.0 all-reduce.2.cloned.1.call-start
  8.0 1.3 collective-permute-start.11
  9.9 0.6 fusion.14
  10.5 1.6 fusion.2
  12.1 0.7 broadcast_divide_fusion.1
  12.8 1.8 fusion.5
  14.6 0.6 stack_broadcast_in_dim.3
  15.2 0.7 stack.19
  15.9 1.8 all-gather
  17.8 0.1 reshape.59
  17.8 4.3 %collective-permute-start.4 = (f32[3,384]{1,0:T(4,128)S(1)}, f32[3,384]{1,0:T(4,128)S(1)}, u32[]{:S(2)}, u32[]{:S(2)}) collective-permute-start(f32[3,384]{1,0:T(4,128)S(1)} %slice.38), channel_id=1, source_target_pairs={{0,6},{2,0},{4,2},{6,4},{1,7},{3,1},{5,3},{7,5},{8,14},{10,8},{12,... | collective-permute-start | bytes 13832 | tf_op jit(solution)/shard_map/ppermute | solution.py:26
  22.2 0.4 collective-permute-start.3
  22.6 1.0 collective-permute-start.2
  23.6 0.0 copy-done
  23.6 0.8 subtract_select_fusion.rel_ref
  24.4 0.0 collective-permute-done.11
  25.0 0.0 collective-permute-done.4
  25.0 2.3 collective-permute-done.3
  27.3 0.1 collective-permute-done.2
  27.4 3.5 %collective-permute-start.7 = (f32[12,384]{1,0:T(8,128)S(1)}, f32[12,384]{1,0:T(8,128)S(1)}, u32[]{:S(2)}, u32[]{:S(2)}) collective-permute-start(f32[12,384]{1,0:T(8,128)S(1)} %pad_maximum_fusion), channel_id=1, source_target_pairs={{0,24},{8,0},{16,8},{24,16},{1,25},{9,1},{17,9},{25,17},{2,26},{10... | collective-permute-start | bytes 55304 | tf_op jit(solution)/shard_map/ppermute | solution.py:26
  30.9 0.3 collective-permute-start.6
  31.3 1.0 collective-permute-start.5
  32.3 0.2 collective-permute-done.7
  32.5 3.8 %collective-permute-done.6 = f32[12,384]{1,0:T(8,128)S(1)} collective-permute-done((f32[12,384]{1,0:T(8,128)S(1)}, f32[12,384]{1,0:T(8,128)S(1)}, u32[]{:S(2)}, u32[]{:S(2)}) %collective-permute-start.6) | collective-permute-done | bytes 18464 | tf_op jit(solution)/shard_map/ppermute | solution.py:26
  36.3 0.2 collective-permute-done.5
  36.5 0.4 concatenate.19
  36.9 4.2 %collective-permute-start.10 = (f32[48,384]{1,0:T(8,128)S(1)}, f32[48,384]{1,0:T(8,128)S(1)}, u32[]{:S(2)}, u32[]{:S(2)}) collective-permute-start(f32[48,384]{1,0:T(8,128)S(1)} %concatenate.19), channel_id=1, source_target_pairs={{0,96},{32,0},{64,32},{96,64},{1,97},{33,1},{65,33},{97,65},{2,98}... | collective-permute-start | bytes 221192 | tf_op jit(solution)/shard_map/ppermute | solution.py:26
  41.1 0.0 collective-permute-start.9
  41.1 1.2 collective-permute-start.8
  42.3 0.8 collective-permute-done.10
  43.1 4.0 %collective-permute-done.9 = f32[48,384]{1,0:T(8,128)S(1)} collective-permute-done((f32[48,384]{1,0:T(8,128)S(1)}, f32[48,384]{1,0:T(8,128)S(1)}, u32[]{:S(2)}, u32[]{:S(2)}) %collective-permute-start.9) | collective-permute-done | bytes 73760 | tf_op jit(solution)/shard_map/ppermute | solution.py:26
  47.1 0.4 collective-permute-done.8
  47.5 0.4 concatenate.20
  47.9 0.1 reshape.57
  48.0 0.2 slice_reduce_fusion.4
  48.3 0.6 slice_reduce_fusion.1
  48.9 0.6 broadcast_divide_fusion
  49.5 0.1 fusion.6
  49.6 0.0 all-gather.3.cloned.1.call-done
  49.6 1.1 fusion.15
  50.7 2.8 collective-permute-start
  53.5 1.5 collective-permute-start.1
  54.9 0.7 rsqrt_multiply_fusion
  55.6 1.0 collective-permute-done
  56.6 4.4 %collective-permute-done.1 = bf16[384,256]{1,0:T(8,128)(2,1)S(1)} collective-permute-done((bf16[384,256]{1,0:T(8,128)(2,1)S(1)}, bf16[384,256]{1,0:T(8,128)(2,1)S(1)}, u32[]{:S(2)}, u32[]{:S(2)}) %collective-permute-start.1) | collective-permute-done | bytes 196640 | tf_op jit(solution)/shard_map/ppermute | solution.py:36
  61.0 4.0 %multiply_convert_fusion.act_ref = bf16[384,3584]{1,0:T(8,128)(2,1)} fusion(bf16[384,256]{1,0:T(8,128)(2,1)S(1)} %collective-permute-done.1, bf16[384,3072]{1,0:T(8,128)(2,1)} %all-gather.3.cloned.1.call-done, bf16[384,256]{1,0:T(8,128)(2,1)S(1)} %collective-permute-done, f32[3584]{0:T(1024)S(1)} %pad_maximum_fusion.1, f32[384]{0:T(512)S(1)} %get-tuple-element.9, ...), kind=kLoop, calls=%fused_computation | loop fusion | flops 16515072 | bytes 5523968 | tf_op jit(solution)/shard_map/convert_element_type | solution.py:121
  65.1 79.9 %shard_map.86 = (bf16[27,384,3072]{2,1,0:T(8,128)(2,1)}, f32[27,192,384]{2,1,0:T(8,128)}) custom-call(s32[27,3072]{1,0:T(8,128)} %subtract_select_fusion.rel_ref, bf16[384,3584]{1,0:T(8,128)(2,1)} %multiply_convert_fusion.act_ref, bf16[192,3072]{1,0:T(8,128)(2,1)} %g_ref.1), custom_call_target="tpu_custom_call" | custom-call | tf_op jit(solution)/shard_map/pallas_call | solution.py:62
  145.0 0.0 all-reduce.2.cloned.1.call-update
  145.0 27.0 %fusion.1 = bf16[192,3072]{1,0:T(8,128)(2,1)} fusion(bf16[27,192,384]{2,1,0:T(8,128)(2,1)} %param.12, bf16[27,384,3072]{2,1,0:T(8,128)(2,1)} %get-tuple-element.4), kind=kOutput, calls=%fused_computation.3 | convolution fusion | flops 12231180288 | bytes 68861952 | tf_op jit(solution)/shard_map/dot_general | solution.py:127
  172.0 144.8 %all-reduce.2.cloned.1.call-done = f32[27,192,384]{2,1,0:T(8,128)} async-done(((f32[27,192,384]{2,1,0:T(8,128)}), f32[27,192,384]{2,1,0:T(8,128)}) %all-reduce.2.cloned.1.call-update) | async-done | bytes 7962640 | tf_op jit(solution)/shard_map/psum | solution.py:126
  316.8 7.4 %copy.20 = f32[27,192,384]{2,1,0:T(8,128)} copy(f32[27,192,384]{2,1,0:T(8,128)} %all-reduce.2.cloned.1.call-done) | data formatting | bytes 15925248
  (10 shorter events, 0.1 us)
Async XLA Ops:
  7.2 16.4 %copy-start = (s32[27,3072]{1,0:T(8,128)S(1)}, s32[27,3072]{1,0:T(8,128)}, u32[]{:S(2)}) copy-start(s32[27,3072]{1,0:T(8,128)} %param.11) | copy-start | bytes 995332
  7.2 42.4 %all-gather.3.cloned.1.call-start = ((), (), s32[]{:S(2)}) async-start(), calls=%async_computation | async-start | bytes 3538944 | tf_op jit(solution)/shard_map/all_gather | solution.py:89
  7.9 308.9 %all-reduce.2.cloned.1.call-start = ((), (), s32[]{:S(2)}) async-start(), calls=%async_computation.1 | async-start | bytes 15925248 | tf_op jit(solution)/shard_map/psum | solution.py:126
  8.0 16.5 %collective-permute-start.11 = (s32[1]{0:T(128)}, s32[1]{0:T(128)}, u32[]{:S(2)}, u32[]{:S(2)}) collective-permute-start(s32[1]{0:T(128)} %param.10), channel_id=1, source_target_pairs={{2,0},{4,2},{6,4},{8,6},{10,8},{12,10},{14,12},{16,14},{18,16},{20... | collective-permute-start | bytes 20 | tf_op jit(solution)/shard_map/ppermute | solution.py:37
  17.8 7.1 %collective-permute-start.4 = (f32[3,384]{1,0:T(4,128)S(1)}, f32[3,384]{1,0:T(4,128)S(1)}, u32[]{:S(2)}, u32[]{:S(2)}) collective-permute-start(f32[3,384]{1,0:T(4,128)S(1)} %slice.38), channel_id=1, source_target_pairs={{0,6},{2,0},{4,2},{6,4},{1,7},{3,1},{5,3},{7,5},{8,14},{10,8},{12,... | collective-permute-start | bytes 13832 | tf_op jit(solution)/shard_map/ppermute | solution.py:26
  22.2 5.1 %collective-permute-start.3 = (f32[3,384]{1,0:T(4,128)S(1)}, f32[3,384]{1,0:T(4,128)S(1)}, u32[]{:S(2)}, u32[]{:S(2)}) collective-permute-start(f32[3,384]{1,0:T(4,128)S(1)} %slice.38), channel_id=1, source_target_pairs={{0,4},{2,6},{4,0},{6,2},{1,5},{3,7},{5,1},{7,3},{8,12},{10,14},{12... | collective-permute-start | bytes 13832 | tf_op jit(solution)/shard_map/ppermute | solution.py:26
  22.6 4.8 %collective-permute-start.2 = (f32[3,384]{1,0:T(4,128)S(1)}, f32[3,384]{1,0:T(4,128)S(1)}, u32[]{:S(2)}, u32[]{:S(2)}) collective-permute-start(f32[3,384]{1,0:T(4,128)S(1)} %slice.38), channel_id=1, source_target_pairs={{0,2},{2,4},{4,6},{6,0},{1,3},{3,5},{5,7},{7,1},{8,10},{10,12},{12... | collective-permute-start | bytes 13832 | tf_op jit(solution)/shard_map/ppermute | solution.py:26
  27.4 5.0 %collective-permute-start.7 = (f32[12,384]{1,0:T(8,128)S(1)}, f32[12,384]{1,0:T(8,128)S(1)}, u32[]{:S(2)}, u32[]{:S(2)}) collective-permute-start(f32[12,384]{1,0:T(8,128)S(1)} %pad_maximum_fusion), channel_id=1, source_target_pairs={{0,24},{8,0},{16,8},{24,16},{1,25},{9,1},{17,9},{25,17},{2,26},{10... | collective-permute-start | bytes 55304 | tf_op jit(solution)/shard_map/ppermute | solution.py:26
  30.9 5.4 %collective-permute-start.6 = (f32[12,384]{1,0:T(8,128)S(1)}, f32[12,384]{1,0:T(8,128)S(1)}, u32[]{:S(2)}, u32[]{:S(2)}) collective-permute-start(f32[12,384]{1,0:T(8,128)S(1)} %pad_maximum_fusion), channel_id=1, source_target_pairs={{0,16},{8,24},{16,0},{24,8},{1,17},{9,25},{17,1},{25,9},{2,18},{10... | collective-permute-start | bytes 55304 | tf_op jit(solution)/shard_map/ppermute | solution.py:26
  31.3 5.3 %collective-permute-start.5 = (f32[12,384]{1,0:T(8,128)S(1)}, f32[12,384]{1,0:T(8,128)S(1)}, u32[]{:S(2)}, u32[]{:S(2)}) collective-permute-start(f32[12,384]{1,0:T(8,128)S(1)} %pad_maximum_fusion), channel_id=1, source_target_pairs={{0,8},{8,16},{16,24},{24,0},{1,9},{9,17},{17,25},{25,1},{2,10},{10... | collective-permute-start | bytes 55304 | tf_op jit(solution)/shard_map/ppermute | solution.py:26
  36.9 6.2 %collective-permute-start.10 = (f32[48,384]{1,0:T(8,128)S(1)}, f32[48,384]{1,0:T(8,128)S(1)}, u32[]{:S(2)}, u32[]{:S(2)}) collective-permute-start(f32[48,384]{1,0:T(8,128)S(1)} %concatenate.19), channel_id=1, source_target_pairs={{0,96},{32,0},{64,32},{96,64},{1,97},{33,1},{65,33},{97,65},{2,98}... | collective-permute-start | bytes 221192 | tf_op jit(solution)/shard_map/ppermute | solution.py:26
  41.1 6.0 %collective-permute-start.9 = (f32[48,384]{1,0:T(8,128)S(1)}, f32[48,384]{1,0:T(8,128)S(1)}, u32[]{:S(2)}, u32[]{:S(2)}) collective-permute-start(f32[48,384]{1,0:T(8,128)S(1)} %concatenate.19), channel_id=1, source_target_pairs={{0,64},{32,96},{64,0},{96,32},{1,65},{33,97},{65,1},{97,33},{2,66}... | collective-permute-start | bytes 221192 | tf_op jit(solution)/shard_map/ppermute | solution.py:26
  41.1 6.4 %collective-permute-start.8 = (f32[48,384]{1,0:T(8,128)S(1)}, f32[48,384]{1,0:T(8,128)S(1)}, u32[]{:S(2)}, u32[]{:S(2)}) collective-permute-start(f32[48,384]{1,0:T(8,128)S(1)} %concatenate.19), channel_id=1, source_target_pairs={{0,32},{32,64},{64,96},{96,0},{1,33},{33,65},{65,97},{97,1},{2,34}... | collective-permute-start | bytes 221192 | tf_op jit(solution)/shard_map/ppermute | solution.py:26
  50.7 5.9 %collective-permute-start = (bf16[384,256]{1,0:T(8,128)(2,1)S(1)}, bf16[384,256]{1,0:T(8,128)(2,1)S(1)}, u32[]{:S(2)}, u32[]{:S(2)}) collective-permute-start(bf16[384,256]{1,0:T(8,128)(2,1)S(1)} %get-tuple-element.10), channel_id=1, source_target_pairs={{0,2},{2,4},{4,6},{6,8},{8,10},{10,12},{12,14},{14,16},{16,18},{18... | collective-permute-start | bytes 589832 | tf_op jit(solution)/shard_map/ppermute | solution.py:35
  53.5 7.6 %collective-permute-start.1 = (bf16[384,256]{1,0:T(8,128)(2,1)S(1)}, bf16[384,256]{1,0:T(8,128)(2,1)S(1)}, u32[]{:S(2)}, u32[]{:S(2)}) collective-permute-start(bf16[384,256]{1,0:T(8,128)(2,1)S(1)} %get-tuple-element.11), channel_id=1, source_target_pairs={{2,0},{4,2},{6,4},{8,6},{10,8},{12,10},{14,12},{16,14},{18,16},{20... | collective-permute-start | bytes 589832 | tf_op jit(solution)/shard_map/ppermute | solution.py:36
Sparse Core Ops, SparseCore 0:
  9.6 16.1 all-gather.2
  145.1 171.6 all-reduce.1

commit v11 on v10

--- a/solution.py
+++ b/solution.py
@@ -38,38 +38,41 @@
     return jnp.concatenate([before, x, after], axis=1), next_live
 
 
-def offset_kernel(rel_ref, act_ref, g_ref, picked_ref, kg_ref, *, halo, blocks):
-    k = pl.program_id(0)
+def offset_kernel(rel_ref, act_ref, g_ref, picked_ref, kg_ref, *, halo, blocks, group):
+    step = pl.program_id(0)
     window = BLOCK + 2 * halo
     rows = lax.broadcasted_iota(jnp.int32, (window, BLOCK), 0)
-    for b in range(blocks):
-        idx = rel_ref[pl.ds(k, 1), pl.ds(b * BLOCK, BLOCK)]
-        onehot = jnp.where(rows == idx, 1.0, 0.0).astype(jnp.bfloat16)
-        win = act_ref[:, pl.ds(b * BLOCK, window)]
-        picked_ref[0, :, pl.ds(b * BLOCK, BLOCK)] = jnp.dot(
-            win, onehot, preferred_element_type=jnp.float32
-        ).astype(jnp.bfloat16)
-    kg_ref[0] = lax.dot_general(
-        g_ref[...], picked_ref[0], (((1,), (1,)), ((), ())), preferred_element_type=jnp.float32
-    )
+    for j in range(group):
+        k = step * group + j
+        for b in range(blocks):
+            idx = rel_ref[pl.ds(k, 1), pl.ds(b * BLOCK, BLOCK)]
+            onehot = jnp.where(rows == idx, 1.0, 0.0).astype(jnp.bfloat16)
+            win = act_ref[:, pl.ds(b * BLOCK, window)]
+            picked_ref[j, :, pl.ds(b * BLOCK, BLOCK)] = jnp.dot(
+                win, onehot, preferred_element_type=jnp.float32
+            ).astype(jnp.bfloat16)
+        kg_ref[j] = lax.dot_general(
+            g_ref[...], picked_ref[j], (((1,), (1,)), ((), ())), preferred_element_type=jnp.float32
+        )
 
 
 def gather_call(rel, act, grad_out, halo):
     offsets, columns = rel.shape
     c_all, extent = act.shape
     o_ch = grad_out.shape[0]
-    kern = functools.partial(offset_kernel, halo=halo, blocks=columns // BLOCK)
+    group = 3 if offsets % 3 == 0 else 1
+    kern = functools.partial(offset_kernel, halo=halo, blocks=columns // BLOCK, group=group)
     return pl.pallas_call(
         kern,
-        grid=(offsets,),
+        grid=(offsets // group,),
         in_specs=[
             pl.BlockSpec((offsets, columns), lambda k: (0, 0)),
             pl.BlockSpec((c_all, extent), lambda k: (0, 0)),
             pl.BlockSpec((o_ch, columns), lambda k: (0, 0)),
         ],
         out_specs=[
-            pl.BlockSpec((1, c_all, columns), lambda k: (k, 0, 0)),
-            pl.BlockSpec((1, o_ch, c_all), lambda k: (k, 0, 0)),
+            pl.BlockSpec((group, c_all, columns), lambda k: (k, 0, 0)),
+            pl.BlockSpec((group, o_ch, c_all), lambda k: (k, 0, 0)),
         ],
         out_shape=[
             jax.ShapeDtypeStruct((offsets, c_all, columns), jnp.bfloat16),

time: 331 us -> 330 us (level)
  no operation moved by 1% of the time
where the time goes in v11:
time: 330 us
  waiting for transfers between devices  163 us (49%)
  Pallas kernels  78.5 us (24%)
  matrix products  27 us (8%)
  starting transfers between devices  21.5 us (7%)
  between operations  15.4 us (5%)
  other arithmetic  11.7 us (4%)
  local copies, waits for them, and re-layouts  10.8 us (3%)
    psum x1, waiting for transfers between devices, per_device(): kernel_grad = lax.psum(grad_parts, SUB)  145 us
    pallas_call x1, Pallas kernels, gather_call(): pl.pallas_call(kern, grid=(offsets // group,), in_specs=[pl.BlockSpec((of...  78.5 us
    dot_general x1, matrix products, per_device(): lax.dot_general(weights, picked, (((0, 2), (0, 1)), ((), ())), preferred_...  27 us
    ppermute x9, starting transfers between devices, ring_gather(): lax.ppermute(x, axis, [(i, (i + shift) % count) for i in range(count)])  15.9 us
    ppermute x9, waiting for transfers between devices, ring_gather(): lax.ppermute(x, axis, [(i, (i + shift) % count) for i in range(count)])  11.9 us
    unnamed x5, local copies, waits for them, and re-layouts  7.46 us
  transfers between devices with their start and end apart: 14, of which 11 were waited for; matrix products, arithmetic and copies ran while one was open for 11% of the time, Pallas kernels for 0%

profile of v11, /device:TPU:0, one launch (start us, length us, event | category | flops | bytes accessed | tf_op | source)
XLA Modules:
  0.0 329.8 jit_solution(6661970563193732966)
XLA Ops:
  7.2 0.0 copy-start
  7.2 0.0 all-gather.3.cloned.1.call-start
  7.2 0.7 all-gather.3.cloned.1.call-update
  7.9 0.0 all-reduce.2.cloned.1.call-start
  8.0 1.3 collective-permute-start.11
  9.9 0.6 fusion.14
  10.5 1.6 fusion.2
  12.1 0.7 broadcast_divide_fusion.1
  12.8 1.8 fusion.5
  14.6 0.6 stack_broadcast_in_dim.3
  15.2 0.7 stack.19
  15.9 1.8 all-gather
  17.8 0.1 reshape.59
  17.8 4.3 %collective-permute-start.4 = (f32[3,384]{1,0:T(4,128)S(1)}, f32[3,384]{1,0:T(4,128)S(1)}, u32[]{:S(2)}, u32[]{:S(2)}) collective-permute-start(f32[3,384]{1,0:T(4,128)S(1)} %slice.38), channel_id=1, source_target_pairs={{0,6},{2,0},{4,2},{6,4},{1,7},{3,1},{5,3},{7,5},{8,14},{10,8},{12,... | collective-permute-start | bytes 13832 | tf_op jit(solution)/shard_map/ppermute | solution.py:26
  22.2 0.4 collective-permute-start.3
  22.6 1.0 collective-permute-start.2
  23.6 0.0 copy-done
  23.6 0.8 subtract_select_fusion.rel_ref
  24.4 0.0 collective-permute-done.11
  25.0 0.0 collective-permute-done.4
  25.0 2.3 collective-permute-done.3
  27.3 0.1 collective-permute-done.2
  27.4 3.5 %collective-permute-start.7 = (f32[12,384]{1,0:T(8,128)S(1)}, f32[12,384]{1,0:T(8,128)S(1)}, u32[]{:S(2)}, u32[]{:S(2)}) collective-permute-start(f32[12,384]{1,0:T(8,128)S(1)} %pad_maximum_fusion), channel_id=1, source_target_pairs={{0,24},{8,0},{16,8},{24,16},{1,25},{9,1},{17,9},{25,17},{2,26},{10... | collective-permute-start | bytes 55304 | tf_op jit(solution)/shard_map/ppermute | solution.py:26
  30.9 0.3 collective-permute-start.6
  31.3 1.0 collective-permute-start.5
  32.3 0.2 collective-permute-done.7
  32.5 3.8 %collective-permute-done.6 = f32[12,384]{1,0:T(8,128)S(1)} collective-permute-done((f32[12,384]{1,0:T(8,128)S(1)}, f32[12,384]{1,0:T(8,128)S(1)}, u32[]{:S(2)}, u32[]{:S(2)}) %collective-permute-start.6) | collective-permute-done | bytes 18464 | tf_op jit(solution)/shard_map/ppermute | solution.py:26
  36.3 0.2 collective-permute-done.5
  36.5 0.4 concatenate.19
  36.9 4.2 %collective-permute-start.10 = (f32[48,384]{1,0:T(8,128)S(1)}, f32[48,384]{1,0:T(8,128)S(1)}, u32[]{:S(2)}, u32[]{:S(2)}) collective-permute-start(f32[48,384]{1,0:T(8,128)S(1)} %concatenate.19), channel_id=1, source_target_pairs={{0,96},{32,0},{64,32},{96,64},{1,97},{33,1},{65,33},{97,65},{2,98}... | collective-permute-start | bytes 221192 | tf_op jit(solution)/shard_map/ppermute | solution.py:26
  41.1 0.0 collective-permute-start.9
  41.1 1.2 collective-permute-start.8
  42.3 0.8 collective-permute-done.10
  43.1 4.0 %collective-permute-done.9 = f32[48,384]{1,0:T(8,128)S(1)} collective-permute-done((f32[48,384]{1,0:T(8,128)S(1)}, f32[48,384]{1,0:T(8,128)S(1)}, u32[]{:S(2)}, u32[]{:S(2)}) %collective-permute-start.9) | collective-permute-done | bytes 73760 | tf_op jit(solution)/shard_map/ppermute | solution.py:26
  47.1 0.4 collective-permute-done.8
  47.5 0.4 concatenate.20
  47.9 0.1 reshape.57
  48.0 0.2 slice_reduce_fusion.4
  48.3 0.6 slice_reduce_fusion.1
  48.9 0.6 broadcast_divide_fusion
  49.5 0.1 fusion.6
  49.6 0.0 all-gather.3.cloned.1.call-done
  49.6 1.1 fusion.15
  50.7 2.8 collective-permute-start
  53.5 1.5 collective-permute-start.1
  54.9 0.7 rsqrt_multiply_fusion
  55.6 1.0 collective-permute-done
  56.6 4.4 %collective-permute-done.1 = bf16[384,256]{1,0:T(8,128)(2,1)S(1)} collective-permute-done((bf16[384,256]{1,0:T(8,128)(2,1)S(1)}, bf16[384,256]{1,0:T(8,128)(2,1)S(1)}, u32[]{:S(2)}, u32[]{:S(2)}) %collective-permute-start.1) | collective-permute-done | bytes 196640 | tf_op jit(solution)/shard_map/ppermute | solution.py:36
  61.0 4.0 %multiply_convert_fusion.act_ref = bf16[384,3584]{1,0:T(8,128)(2,1)} fusion(bf16[384,256]{1,0:T(8,128)(2,1)S(1)} %collective-permute-done.1, bf16[384,3072]{1,0:T(8,128)(2,1)} %all-gather.3.cloned.1.call-done, bf16[384,256]{1,0:T(8,128)(2,1)S(1)} %collective-permute-done, f32[3584]{0:T(1024)S(1)} %pad_maximum_fusion.1, f32[384]{0:T(512)S(1)} %get-tuple-element.9, ...), kind=kLoop, calls=%fused_computation | loop fusion | flops 16515072 | bytes 5523968 | tf_op jit(solution)/shard_map/convert_element_type | solution.py:124
  65.1 78.5 %shard_map.86 = (bf16[27,384,3072]{2,1,0:T(8,128)(2,1)}, f32[27,192,384]{2,1,0:T(8,128)}) custom-call(s32[27,3072]{1,0:T(8,128)} %subtract_select_fusion.rel_ref, bf16[384,3584]{1,0:T(8,128)(2,1)} %multiply_convert_fusion.act_ref, bf16[192,3072]{1,0:T(8,128)(2,1)} %g_ref.1), custom_call_target="tpu_custom_call" | custom-call | tf_op jit(solution)/shard_map/pallas_call | solution.py:65
  143.6 0.0 all-reduce.2.cloned.1.call-update
  143.6 27.0 %fusion.1 = bf16[192,3072]{1,0:T(8,128)(2,1)} fusion(bf16[27,192,384]{2,1,0:T(8,128)(2,1)} %param.12, bf16[27,384,3072]{2,1,0:T(8,128)(2,1)} %get-tuple-element.4), kind=kOutput, calls=%fused_computation.3 | convolution fusion | flops 12231180288 | bytes 68861952 | tf_op jit(solution)/shard_map/dot_general | solution.py:130
  170.6 145.0 %all-reduce.2.cloned.1.call-done = f32[27,192,384]{2,1,0:T(8,128)} async-done(((f32[27,192,384]{2,1,0:T(8,128)}), f32[27,192,384]{2,1,0:T(8,128)}) %all-reduce.2.cloned.1.call-update) | async-done | bytes 7962640 | tf_op jit(solution)/shard_map/psum | solution.py:129
  315.6 7.4 %copy.20 = f32[27,192,384]{2,1,0:T(8,128)} copy(f32[27,192,384]{2,1,0:T(8,128)} %all-reduce.2.cloned.1.call-done) | data formatting | bytes 15925248
  (10 shorter events, 0.1 us)
Async XLA Ops:
  7.2 16.4 %copy-start = (s32[27,3072]{1,0:T(8,128)S(1)}, s32[27,3072]{1,0:T(8,128)}, u32[]{:S(2)}) copy-start(s32[27,3072]{1,0:T(8,128)} %param.11) | copy-start | bytes 995332
  7.2 42.4 %all-gather.3.cloned.1.call-start = ((), (), s32[]{:S(2)}) async-start(), calls=%async_computation | async-start | bytes 3538944 | tf_op jit(solution)/shard_map/all_gather | solution.py:92
  7.9 307.7 %all-reduce.2.cloned.1.call-start = ((), (), s32[]{:S(2)}) async-start(), calls=%async_computation.1 | async-start | bytes 15925248 | tf_op jit(solution)/shard_map/psum | solution.py:129
  8.0 16.5 %collective-permute-start.11 = (s32[1]{0:T(128)}, s32[1]{0:T(128)}, u32[]{:S(2)}, u32[]{:S(2)}) collective-permute-start(s32[1]{0:T(128)} %param.10), channel_id=1, source_target_pairs={{2,0},{4,2},{6,4},{8,6},{10,8},{12,10},{14,12},{16,14},{18,16},{20... | collective-permute-start | bytes 20 | tf_op jit(solution)/shard_map/ppermute | solution.py:37
  17.8 7.1 %collective-permute-start.4 = (f32[3,384]{1,0:T(4,128)S(1)}, f32[3,384]{1,0:T(4,128)S(1)}, u32[]{:S(2)}, u32[]{:S(2)}) collective-permute-start(f32[3,384]{1,0:T(4,128)S(1)} %slice.38), channel_id=1, source_target_pairs={{0,6},{2,0},{4,2},{6,4},{1,7},{3,1},{5,3},{7,5},{8,14},{10,8},{12,... | collective-permute-start | bytes 13832 | tf_op jit(solution)/shard_map/ppermute | solution.py:26
  22.2 5.1 %collective-permute-start.3 = (f32[3,384]{1,0:T(4,128)S(1)}, f32[3,384]{1,0:T(4,128)S(1)}, u32[]{:S(2)}, u32[]{:S(2)}) collective-permute-start(f32[3,384]{1,0:T(4,128)S(1)} %slice.38), channel_id=1, source_target_pairs={{0,4},{2,6},{4,0},{6,2},{1,5},{3,7},{5,1},{7,3},{8,12},{10,14},{12... | collective-permute-start | bytes 13832 | tf_op jit(solution)/shard_map/ppermute | solution.py:26
  22.6 4.8 %collective-permute-start.2 = (f32[3,384]{1,0:T(4,128)S(1)}, f32[3,384]{1,0:T(4,128)S(1)}, u32[]{:S(2)}, u32[]{:S(2)}) collective-permute-start(f32[3,384]{1,0:T(4,128)S(1)} %slice.38), channel_id=1, source_target_pairs={{0,2},{2,4},{4,6},{6,0},{1,3},{3,5},{5,7},{7,1},{8,10},{10,12},{12... | collective-permute-start | bytes 13832 | tf_op jit(solution)/shard_map/ppermute | solution.py:26
  27.4 5.0 %collective-permute-start.7 = (f32[12,384]{1,0:T(8,128)S(1)}, f32[12,384]{1,0:T(8,128)S(1)}, u32[]{:S(2)}, u32[]{:S(2)}) collective-permute-start(f32[12,384]{1,0:T(8,128)S(1)} %pad_maximum_fusion), channel_id=1, source_target_pairs={{0,24},{8,0},{16,8},{24,16},{1,25},{9,1},{17,9},{25,17},{2,26},{10... | collective-permute-start | bytes 55304 | tf_op jit(solution)/shard_map/ppermute | solution.py:26
  30.9 5.4 %collective-permute-start.6 = (f32[12,384]{1,0:T(8,128)S(1)}, f32[12,384]{1,0:T(8,128)S(1)}, u32[]{:S(2)}, u32[]{:S(2)}) collective-permute-start(f32[12,384]{1,0:T(8,128)S(1)} %pad_maximum_fusion), channel_id=1, source_target_pairs={{0,16},{8,24},{16,0},{24,8},{1,17},{9,25},{17,1},{25,9},{2,18},{10... | collective-permute-start | bytes 55304 | tf_op jit(solution)/shard_map/ppermute | solution.py:26
  31.3 5.3 %collective-permute-start.5 = (f32[12,384]{1,0:T(8,128)S(1)}, f32[12,384]{1,0:T(8,128)S(1)}, u32[]{:S(2)}, u32[]{:S(2)}) collective-permute-start(f32[12,384]{1,0:T(8,128)S(1)} %pad_maximum_fusion), channel_id=1, source_target_pairs={{0,8},{8,16},{16,24},{24,0},{1,9},{9,17},{17,25},{25,1},{2,10},{10... | collective-permute-start | bytes 55304 | tf_op jit(solution)/shard_map/ppermute | solution.py:26
  36.9 6.2 %collective-permute-start.10 = (f32[48,384]{1,0:T(8,128)S(1)}, f32[48,384]{1,0:T(8,128)S(1)}, u32[]{:S(2)}, u32[]{:S(2)}) collective-permute-start(f32[48,384]{1,0:T(8,128)S(1)} %concatenate.19), channel_id=1, source_target_pairs={{0,96},{32,0},{64,32},{96,64},{1,97},{33,1},{65,33},{97,65},{2,98}... | collective-permute-start | bytes 221192 | tf_op jit(solution)/shard_map/ppermute | solution.py:26
  41.1 6.0 %collective-permute-start.9 = (f32[48,384]{1,0:T(8,128)S(1)}, f32[48,384]{1,0:T(8,128)S(1)}, u32[]{:S(2)}, u32[]{:S(2)}) collective-permute-start(f32[48,384]{1,0:T(8,128)S(1)} %concatenate.19), channel_id=1, source_target_pairs={{0,64},{32,96},{64,0},{96,32},{1,65},{33,97},{65,1},{97,33},{2,66}... | collective-permute-start | bytes 221192 | tf_op jit(solution)/shard_map/ppermute | solution.py:26
  41.1 6.4 %collective-permute-start.8 = (f32[48,384]{1,0:T(8,128)S(1)}, f32[48,384]{1,0:T(8,128)S(1)}, u32[]{:S(2)}, u32[]{:S(2)}) collective-permute-start(f32[48,384]{1,0:T(8,128)S(1)} %concatenate.19), channel_id=1, source_target_pairs={{0,32},{32,64},{64,96},{96,0},{1,33},{33,65},{65,97},{97,1},{2,34}... | collective-permute-start | bytes 221192 | tf_op jit(solution)/shard_map/ppermute | solution.py:26
  50.7 5.9 %collective-permute-start = (bf16[384,256]{1,0:T(8,128)(2,1)S(1)}, bf16[384,256]{1,0:T(8,128)(2,1)S(1)}, u32[]{:S(2)}, u32[]{:S(2)}) collective-permute-start(bf16[384,256]{1,0:T(8,128)(2,1)S(1)} %get-tuple-element.10), channel_id=1, source_target_pairs={{0,2},{2,4},{4,6},{6,8},{8,10},{10,12},{12,14},{14,16},{16,18},{18... | collective-permute-start | bytes 589832 | tf_op jit(solution)/shard_map/ppermute | solution.py:35
  53.5 7.6 %collective-permute-start.1 = (bf16[384,256]{1,0:T(8,128)(2,1)S(1)}, bf16[384,256]{1,0:T(8,128)(2,1)S(1)}, u32[]{:S(2)}, u32[]{:S(2)}) collective-permute-start(bf16[384,256]{1,0:T(8,128)(2,1)S(1)} %get-tuple-element.11), channel_id=1, source_target_pairs={{2,0},{4,2},{6,4},{8,6},{10,8},{12,10},{14,12},{16,14},{18,16},{20... | collective-permute-start | bytes 589832 | tf_op jit(solution)/shard_map/ppermute | solution.py:36
Sparse Core Ops, SparseCore 0:
  9.6 16.1 all-gather.2
  143.7 171.8 all-reduce.1

commit v12 on v11

--- a/solution.py
+++ b/solution.py
@@ -60,7 +60,7 @@
     offsets, columns = rel.shape
     c_all, extent = act.shape
     o_ch = grad_out.shape[0]
-    group = 3 if offsets % 3 == 0 else 1
+    group = 9 if offsets % 9 == 0 else 1
     kern = functools.partial(offset_kernel, halo=halo, blocks=columns // BLOCK, group=group)
     return pl.pallas_call(
         kern,

time: 330 us -> 334 us (1.012)
  Pallas kernels: 78.5 us -> 81.9 us
    pallas_call x1, Pallas kernels: 78.5 us -> 81.9 us  [gather_call(): pl.pallas_call(kern, grid=(offsets // group,), in_specs=[pl.BlockSpec((of...]
where the time goes in v12:
time: 334 us; the launch traced here: 333 us
  waiting for transfers between devices  163 us (49%)
  Pallas kernels  81.9 us (25%)
  matrix products  27 us (8%)
  starting transfers between devices  21.4 us (6%)
  between operations  15.4 us (5%)
  other arithmetic  11.7 us (4%)
  local copies, waits for them, and re-layouts  10.8 us (3%)
    psum x1, waiting for transfers between devices, per_device(): kernel_grad = lax.psum(grad_parts, SUB)  145 us
    pallas_call x1, Pallas kernels, gather_call(): pl.pallas_call(kern, grid=(offsets // group,), in_specs=[pl.BlockSpec((of...  81.9 us
    dot_general x1, matrix products, per_device(): lax.dot_general(weights, picked, (((0, 2), (0, 1)), ((), ())), preferred_...  27 us
    ppermute x9, starting transfers between devices, ring_gather(): lax.ppermute(x, axis, [(i, (i + shift) % count) for i in range(count)])  15.9 us
    ppermute x9, waiting for transfers between devices, ring_gather(): lax.ppermute(x, axis, [(i, (i + shift) % count) for i in range(count)])  11.9 us
    unnamed x5, local copies, waits for them, and re-layouts  7.46 us
  transfers between devices with their start and end apart: 14, of which 11 were waited for; matrix products, arithmetic and copies ran while one was open for 11% of the time, Pallas kernels for 0%

profile of v12, /device:TPU:0, one launch (start us, length us, event | category | flops | bytes accessed | tf_op | source)
XLA Modules:
  0.0 333.2 jit_solution(10119280749511887349)
XLA Ops:
  7.2 0.0 copy-start
  7.2 0.0 all-gather.3.cloned.1.call-start
  7.2 0.7 all-gather.3.cloned.1.call-update
  7.9 0.0 all-reduce.2.cloned.1.call-start
  8.0 1.3 collective-permute-start.11
  9.9 0.6 fusion.14
  10.5 1.6 fusion.2
  12.1 0.7 broadcast_divide_fusion.1
  12.8 1.8 fusion.5
  14.6 0.6 stack_broadcast_in_dim.3
  15.2 0.7 stack.19
  15.9 1.8 all-gather
  17.8 0.1 reshape.59
  17.8 4.3 %collective-permute-start.4 = (f32[3,384]{1,0:T(4,128)S(1)}, f32[3,384]{1,0:T(4,128)S(1)}, u32[]{:S(2)}, u32[]{:S(2)}) collective-permute-start(f32[3,384]{1,0:T(4,128)S(1)} %slice.38), channel_id=1, source_target_pairs={{0,6},{2,0},{4,2},{6,4},{1,7},{3,1},{5,3},{7,5},{8,14},{10,8},{12,... | collective-permute-start | bytes 13832 | tf_op jit(solution)/shard_map/ppermute | solution.py:26
  22.2 0.4 collective-permute-start.3
  22.6 1.0 collective-permute-start.2
  23.6 0.0 copy-done
  23.6 0.8 subtract_select_fusion.rel_ref
  24.4 0.0 collective-permute-done.11
  25.0 0.0 collective-permute-done.4
  25.0 2.3 collective-permute-done.3
  27.3 0.1 collective-permute-done.2
  27.4 3.5 %collective-permute-start.7 = (f32[12,384]{1,0:T(8,128)S(1)}, f32[12,384]{1,0:T(8,128)S(1)}, u32[]{:S(2)}, u32[]{:S(2)}) collective-permute-start(f32[12,384]{1,0:T(8,128)S(1)} %pad_maximum_fusion), channel_id=1, source_target_pairs={{0,24},{8,0},{16,8},{24,16},{1,25},{9,1},{17,9},{25,17},{2,26},{10... | collective-permute-start | bytes 55304 | tf_op jit(solution)/shard_map/ppermute | solution.py:26
  30.9 0.3 collective-permute-start.6
  31.3 1.0 collective-permute-start.5
  32.3 0.2 collective-permute-done.7
  32.5 3.8 %collective-permute-done.6 = f32[12,384]{1,0:T(8,128)S(1)} collective-permute-done((f32[12,384]{1,0:T(8,128)S(1)}, f32[12,384]{1,0:T(8,128)S(1)}, u32[]{:S(2)}, u32[]{:S(2)}) %collective-permute-start.6) | collective-permute-done | bytes 18464 | tf_op jit(solution)/shard_map/ppermute | solution.py:26
  36.3 0.2 collective-permute-done.5
  36.5 0.4 concatenate.19
  36.9 4.2 %collective-permute-start.10 = (f32[48,384]{1,0:T(8,128)S(1)}, f32[48,384]{1,0:T(8,128)S(1)}, u32[]{:S(2)}, u32[]{:S(2)}) collective-permute-start(f32[48,384]{1,0:T(8,128)S(1)} %concatenate.19), channel_id=1, source_target_pairs={{0,96},{32,0},{64,32},{96,64},{1,97},{33,1},{65,33},{97,65},{2,98}... | collective-permute-start | bytes 221192 | tf_op jit(solution)/shard_map/ppermute | solution.py:26
  41.1 0.0 collective-permute-start.9
  41.1 1.2 collective-permute-start.8
  42.3 0.8 collective-permute-done.10
  43.1 4.0 %collective-permute-done.9 = f32[48,384]{1,0:T(8,128)S(1)} collective-permute-done((f32[48,384]{1,0:T(8,128)S(1)}, f32[48,384]{1,0:T(8,128)S(1)}, u32[]{:S(2)}, u32[]{:S(2)}) %collective-permute-start.9) | collective-permute-done | bytes 73760 | tf_op jit(solution)/shard_map/ppermute | solution.py:26
  47.1 0.4 collective-permute-done.8
  47.5 0.4 concatenate.20
  47.9 0.1 reshape.57
  48.0 0.2 slice_reduce_fusion.4
  48.3 0.6 slice_reduce_fusion.1
  48.9 0.6 broadcast_divide_fusion
  49.5 0.1 fusion.6
  49.6 0.0 all-gather.3.cloned.1.call-done
  49.6 1.1 fusion.15
  50.7 2.8 collective-permute-start
  53.5 1.3 collective-permute-start.1
  54.8 0.7 rsqrt_multiply_fusion
  55.4 1.2 collective-permute-done
  56.6 4.4 %collective-permute-done.1 = bf16[384,256]{1,0:T(8,128)(2,1)S(1)} collective-permute-done((bf16[384,256]{1,0:T(8,128)(2,1)S(1)}, bf16[384,256]{1,0:T(8,128)(2,1)S(1)}, u32[]{:S(2)}, u32[]{:S(2)}) %collective-permute-start.1) | collective-permute-done | bytes 196640 | tf_op jit(solution)/shard_map/ppermute | solution.py:36
  61.0 4.0 %multiply_convert_fusion.act_ref = bf16[384,3584]{1,0:T(8,128)(2,1)} fusion(bf16[384,256]{1,0:T(8,128)(2,1)S(1)} %collective-permute-done.1, bf16[384,3072]{1,0:T(8,128)(2,1)} %all-gather.3.cloned.1.call-done, bf16[384,256]{1,0:T(8,128)(2,1)S(1)} %collective-permute-done, f32[3584]{0:T(1024)S(1)} %pad_maximum_fusion.1, f32[384]{0:T(512)S(1)} %get-tuple-element.9, ...), kind=kLoop, calls=%fused_computation | loop fusion | flops 16515072 | bytes 5523968 | tf_op jit(solution)/shard_map/convert_element_type | solution.py:124
  65.1 81.9 %shard_map.86 = (bf16[27,384,3072]{2,1,0:T(8,128)(2,1)}, f32[27,192,384]{2,1,0:T(8,128)}) custom-call(s32[27,3072]{1,0:T(8,128)} %subtract_select_fusion.rel_ref, bf16[384,3584]{1,0:T(8,128)(2,1)} %multiply_convert_fusion.act_ref, bf16[192,3072]{1,0:T(8,128)(2,1)} %g_ref.1), custom_call_target="tpu_custom_call" | custom-call | tf_op jit(solution)/shard_map/pallas_call | solution.py:65
  146.9 0.0 all-reduce.2.cloned.1.call-update
  147.0 27.0 %fusion.1 = bf16[192,3072]{1,0:T(8,128)(2,1)} fusion(bf16[27,192,384]{2,1,0:T(8,128)(2,1)} %param.12, bf16[27,384,3072]{2,1,0:T(8,128)(2,1)} %get-tuple-element.4), kind=kOutput, calls=%fused_computation.3 | convolution fusion | flops 12231180288 | bytes 68861952 | tf_op jit(solution)/shard_map/dot_general | solution.py:130
  173.9 145.0 %all-reduce.2.cloned.1.call-done = f32[27,192,384]{2,1,0:T(8,128)} async-done(((f32[27,192,384]{2,1,0:T(8,128)}), f32[27,192,384]{2,1,0:T(8,128)}) %all-reduce.2.cloned.1.call-update) | async-done | bytes 7962640 | tf_op jit(solution)/shard_map/psum | solution.py:129
  319.0 7.4 %copy.20 = f32[27,192,384]{2,1,0:T(8,128)} copy(f32[27,192,384]{2,1,0:T(8,128)} %all-reduce.2.cloned.1.call-done) | data formatting | bytes 15925248
  (10 shorter events, 0.1 us)
Async XLA Ops:
  7.2 16.4 %copy-start = (s32[27,3072]{1,0:T(8,128)S(1)}, s32[27,3072]{1,0:T(8,128)}, u32[]{:S(2)}) copy-start(s32[27,3072]{1,0:T(8,128)} %param.11) | copy-start | bytes 995332
  7.2 42.4 %all-gather.3.cloned.1.call-start = ((), (), s32[]{:S(2)}) async-start(), calls=%async_computation | async-start | bytes 3538944 | tf_op jit(solution)/shard_map/all_gather | solution.py:92
  7.9 311.0 %all-reduce.2.cloned.1.call-start = ((), (), s32[]{:S(2)}) async-start(), calls=%async_computation.1 | async-start | bytes 15925248 | tf_op jit(solution)/shard_map/psum | solution.py:129
  8.0 16.5 %collective-permute-start.11 = (s32[1]{0:T(128)}, s32[1]{0:T(128)}, u32[]{:S(2)}, u32[]{:S(2)}) collective-permute-start(s32[1]{0:T(128)} %param.10), channel_id=1, source_target_pairs={{2,0},{4,2},{6,4},{8,6},{10,8},{12,10},{14,12},{16,14},{18,16},{20... | collective-permute-start | bytes 20 | tf_op jit(solution)/shard_map/ppermute | solution.py:37
  17.8 7.1 %collective-permute-start.4 = (f32[3,384]{1,0:T(4,128)S(1)}, f32[3,384]{1,0:T(4,128)S(1)}, u32[]{:S(2)}, u32[]{:S(2)}) collective-permute-start(f32[3,384]{1,0:T(4,128)S(1)} %slice.38), channel_id=1, source_target_pairs={{0,6},{2,0},{4,2},{6,4},{1,7},{3,1},{5,3},{7,5},{8,14},{10,8},{12,... | collective-permute-start | bytes 13832 | tf_op jit(solution)/shard_map/ppermute | solution.py:26
  22.2 5.1 %collective-permute-start.3 = (f32[3,384]{1,0:T(4,128)S(1)}, f32[3,384]{1,0:T(4,128)S(1)}, u32[]{:S(2)}, u32[]{:S(2)}) collective-permute-start(f32[3,384]{1,0:T(4,128)S(1)} %slice.38), channel_id=1, source_target_pairs={{0,4},{2,6},{4,0},{6,2},{1,5},{3,7},{5,1},{7,3},{8,12},{10,14},{12... | collective-permute-start | bytes 13832 | tf_op jit(solution)/shard_map/ppermute | solution.py:26
  22.6 4.8 %collective-permute-start.2 = (f32[3,384]{1,0:T(4,128)S(1)}, f32[3,384]{1,0:T(4,128)S(1)}, u32[]{:S(2)}, u32[]{:S(2)}) collective-permute-start(f32[3,384]{1,0:T(4,128)S(1)} %slice.38), channel_id=1, source_target_pairs={{0,2},{2,4},{4,6},{6,0},{1,3},{3,5},{5,7},{7,1},{8,10},{10,12},{12... | collective-permute-start | bytes 13832 | tf_op jit(solution)/shard_map/ppermute | solution.py:26
  27.4 5.0 %collective-permute-start.7 = (f32[12,384]{1,0:T(8,128)S(1)}, f32[12,384]{1,0:T(8,128)S(1)}, u32[]{:S(2)}, u32[]{:S(2)}) collective-permute-start(f32[12,384]{1,0:T(8,128)S(1)} %pad_maximum_fusion), channel_id=1, source_target_pairs={{0,24},{8,0},{16,8},{24,16},{1,25},{9,1},{17,9},{25,17},{2,26},{10... | collective-permute-start | bytes 55304 | tf_op jit(solution)/shard_map/ppermute | solution.py:26
  30.9 5.4 %collective-permute-start.6 = (f32[12,384]{1,0:T(8,128)S(1)}, f32[12,384]{1,0:T(8,128)S(1)}, u32[]{:S(2)}, u32[]{:S(2)}) collective-permute-start(f32[12,384]{1,0:T(8,128)S(1)} %pad_maximum_fusion), channel_id=1, source_target_pairs={{0,16},{8,24},{16,0},{24,8},{1,17},{9,25},{17,1},{25,9},{2,18},{10... | collective-permute-start | bytes 55304 | tf_op jit(solution)/shard_map/ppermute | solution.py:26
  31.3 5.3 %collective-permute-start.5 = (f32[12,384]{1,0:T(8,128)S(1)}, f32[12,384]{1,0:T(8,128)S(1)}, u32[]{:S(2)}, u32[]{:S(2)}) collective-permute-start(f32[12,384]{1,0:T(8,128)S(1)} %pad_maximum_fusion), channel_id=1, source_target_pairs={{0,8},{8,16},{16,24},{24,0},{1,9},{9,17},{17,25},{25,1},{2,10},{10... | collective-permute-start | bytes 55304 | tf_op jit(solution)/shard_map/ppermute | solution.py:26
  36.9 6.2 %collective-permute-start.10 = (f32[48,384]{1,0:T(8,128)S(1)}, f32[48,384]{1,0:T(8,128)S(1)}, u32[]{:S(2)}, u32[]{:S(2)}) collective-permute-start(f32[48,384]{1,0:T(8,128)S(1)} %concatenate.19), channel_id=1, source_target_pairs={{0,96},{32,0},{64,32},{96,64},{1,97},{33,1},{65,33},{97,65},{2,98}... | collective-permute-start | bytes 221192 | tf_op jit(solution)/shard_map/ppermute | solution.py:26
  41.1 6.0 %collective-permute-start.9 = (f32[48,384]{1,0:T(8,128)S(1)}, f32[48,384]{1,0:T(8,128)S(1)}, u32[]{:S(2)}, u32[]{:S(2)}) collective-permute-start(f32[48,384]{1,0:T(8,128)S(1)} %concatenate.19), channel_id=1, source_target_pairs={{0,64},{32,96},{64,0},{96,32},{1,65},{33,97},{65,1},{97,33},{2,66}... | collective-permute-start | bytes 221192 | tf_op jit(solution)/shard_map/ppermute | solution.py:26
  41.1 6.4 %collective-permute-start.8 = (f32[48,384]{1,0:T(8,128)S(1)}, f32[48,384]{1,0:T(8,128)S(1)}, u32[]{:S(2)}, u32[]{:S(2)}) collective-permute-start(f32[48,384]{1,0:T(8,128)S(1)} %concatenate.19), channel_id=1, source_target_pairs={{0,32},{32,64},{64,96},{96,0},{1,33},{33,65},{65,97},{97,1},{2,34}... | collective-permute-start | bytes 221192 | tf_op jit(solution)/shard_map/ppermute | solution.py:26
  50.7 5.9 %collective-permute-start = (bf16[384,256]{1,0:T(8,128)(2,1)S(1)}, bf16[384,256]{1,0:T(8,128)(2,1)S(1)}, u32[]{:S(2)}, u32[]{:S(2)}) collective-permute-start(bf16[384,256]{1,0:T(8,128)(2,1)S(1)} %get-tuple-element.10), channel_id=1, source_target_pairs={{0,2},{2,4},{4,6},{6,8},{8,10},{10,12},{12,14},{14,16},{16,18},{18... | collective-permute-start | bytes 589832 | tf_op jit(solution)/shard_map/ppermute | solution.py:35
  53.5 7.6 %collective-permute-start.1 = (bf16[384,256]{1,0:T(8,128)(2,1)S(1)}, bf16[384,256]{1,0:T(8,128)(2,1)S(1)}, u32[]{:S(2)}, u32[]{:S(2)}) collective-permute-start(bf16[384,256]{1,0:T(8,128)(2,1)S(1)} %get-tuple-element.11), channel_id=1, source_target_pairs={{2,0},{4,2},{6,4},{8,6},{10,8},{12,10},{14,12},{16,14},{18,16},{20... | collective-permute-start | bytes 589832 | tf_op jit(solution)/shard_map/ppermute | solution.py:36
Sparse Core Ops, SparseCore 0:
  9.6 16.1 all-gather.2
  147.1 171.8 all-reduce.1
